TPU v7x, 512 devices: a whole 4x4x16 slice. The times are simulated.
512 devices in a mesh: ctx: 64 (over x, z), ch: 8 (over y, core).
Axes of the slice: x: 4, y: 4, z: 16, core: 2. Of those that a mesh axis runs over, the one named last changes fastest.
Arguments:
- conv_input: bfloat16 [8192, 4096], P('ctx', 'ch'), may hold values from -6 to 6
- residues: float32 [4096, 16], P('ch'), may hold values from -4 to 4
- decay_rates: float32 [4096, 16], P('ch'), as said below
- skip_gain: float32 [4096], P('ch'), may hold values from -1 to 1
- query_rows: bfloat16 [8192, 4096], P('ctx', 'ch'), may hold values from -5 to 5
- key_rows: bfloat16 [8192, 4096], P('ctx', 'ch'), may hold values from -5 to 5
- value_rows: bfloat16 [8192, 4096], P('ctx', 'ch'), may hold values from -16 to 16
- norm_gain: float32 [4096], P('ch'), may hold values from 0.5 to 1.5
Outputs:
- conv_out: bfloat16 [8192, 4096], P('ctx', 'ch')
- attended: bfloat16 [8192, 4096], P('ctx', 'ch')
Inputs may be any that keep to these rules, and one draw needn't show every extreme that they name: `decay_rates`: decay rates lie between 0.5 / 8192 and 1 / 30.
All inputs are finite; a program needn't handle non-finite values.
Results may differ from a plain program's by a relative error of at most 0.019.
Values may be sent and summed in bfloat16 or wider, within the bound.
No kernel may reach another device: no remote copies, remote signals or barrier semaphores. Data moves between devices by JAX's collectives and lax.ppermute only.
A program may use at most 64 MiB of HBM per device.

v0:
```python
import math

import jax
import jax.numpy as jnp
from jax import lax
from jax.sharding import PartitionSpec as P

HD = 128
WIDTH = 4096


HIGHEST = lax.Precision.HIGHEST


def partner_2(value, axis, apart):
    mask = 2**apart
    pairs = [(source, source ^ mask) for source in range(lax.axis_size(axis))]
    return lax.ppermute(value, axis, pairs)


def shifted(block, axis, distance):
    devices = range(lax.axis_size(axis))
    route = [(i - distance, i) for i in devices if i - distance in devices]
    return lax.ppermute(block, axis, route)


def rotate(real_part, imag_part, turn_angle):
    cosine = jnp.cos(turn_angle)
    sine_value = jnp.sin(turn_angle)
    return (
        real_part * cosine - imag_part * sine_value,
        imag_part * cosine + real_part * sine_value,
    )


def rotate_pair(field, turn_angle):
    real_part, imag_part = rotate(field[0], field[1], turn_angle)
    return jnp.stack([real_part, imag_part])


def filter_spectrum(residues, decay_rates, frequency, length_all):
    rates = jnp.transpose(decay_rates)[:, None, None, :]
    gains = jnp.transpose(residues)[:, None, None, :]
    phase_angle = frequency.astype(jnp.float32) * (2.0 * math.pi / length_all)
    half_sine = jnp.sin(0.5 * phase_angle)[None, :, :, None]
    full_sine = jnp.sin(phase_angle)[None, :, :, None]
    parity = (1 - 2 * (frequency % 2)).astype(jnp.float32)[None, :, :, None]
    retain = jnp.exp(-rates)
    shortfall = -jnp.expm1(-rates)
    weight = gains * jnp.sqrt(shortfall * (1.0 + retain))
    tail_factor = 1.0 - parity * jnp.exp(-rates * float(length_all // 2))
    denom_real = shortfall + 2.0 * retain * half_sine * half_sine
    denom_imag = retain * full_sine
    scale_factor = weight * tail_factor / (denom_real * denom_real + denom_imag * denom_imag)
    spec_real = jnp.sum(scale_factor * denom_real, axis=0)
    spec_imag = -jnp.sum(scale_factor * denom_imag, axis=0)
    return (spec_real, spec_imag)


def transform_rows(table, data):
    return jnp.einsum("kj,ejc->ekc", table, data, precision=HIGHEST)


def per_device(
    conv_input, residues, decay_rates, skip_gain, query_rows, key_rows, value_rows, norm_gain
):
    ctx_count = lax.axis_size("ctx")
    ctx_bits = ctx_count.bit_length() - 1
    position = lax.axis_index("ctx")
    row_count, chan_count = conv_input.shape
    length_all = 2 * ctx_count * row_count
    signal = conv_input.astype(jnp.float32)
    wave_index = jnp.arange(row_count, dtype=jnp.int32)
    two_index = jnp.arange(2, dtype=jnp.int32)
    start_angle = position.astype(jnp.float32) * (math.pi / ctx_count)
    zero_part = jnp.zeros_like(signal)
    field = jnp.stack(
        [
            jnp.stack([signal, signal * jnp.cos(start_angle)]),
            jnp.stack([zero_part, -signal * jnp.sin(start_angle)]),
        ]
    )
    for bit_index in range(ctx_bits - 1, -1, -1):
        half_span = 1 << bit_index
        partner = partner_2(field.astype(jnp.bfloat16), "ctx", bit_index).astype(field.dtype)
        upper_half = position >> bit_index & 1
        turn_angle = (position % half_span).astype(jnp.float32) * (-math.pi / half_span)
        field = jnp.where(
            upper_half == 1, rotate_pair(partner - field, turn_angle), field + partner
        )
    reversed_index = jnp.zeros((), jnp.int32)
    for bit_index in range(ctx_bits):
        reversed_index = reversed_index + (position >> bit_index & 1) * (
            1 << ctx_bits - 1 - bit_index
        )
    pair_freq = 2 * reversed_index + two_index
    turn_angle = (pair_freq[:, None] * wave_index[None, :] % length_all).astype(jnp.float32) * (
        -2.0 * math.pi / length_all
    )
    field = rotate_pair(field, turn_angle[:, :, None])
    rows_real = field[0]
    rows_imag = field[1]
    table_angle = (wave_index[:, None] * wave_index[None, :] % row_count).astype(jnp.float32) * (
        2.0 * math.pi / row_count
    )
    table_cos = jnp.cos(table_angle)
    table_sin = jnp.sin(table_angle)
    spec_real = transform_rows(table_cos, rows_real) + transform_rows(table_sin, rows_imag)
    spec_imag = transform_rows(table_cos, rows_imag) - transform_rows(table_sin, rows_real)
    frequency = pair_freq[:, None] + 2 * ctx_count * wave_index[None, :]
    filter_real, filter_imag = filter_spectrum(residues, decay_rates, frequency, length_all)
    product_real = spec_real * filter_real - spec_imag * filter_imag
    product_imag = spec_real * filter_imag + spec_imag * filter_real
    inverse_real = transform_rows(table_cos, product_real) - transform_rows(table_sin, product_imag)
    inverse_imag = transform_rows(table_cos, product_imag) + transform_rows(table_sin, product_real)
    turn_angle = (pair_freq[:, None] * wave_index[None, :] % length_all).astype(jnp.float32) * (
        2.0 * math.pi / length_all
    )
    inverse_real, inverse_imag = rotate(inverse_real, inverse_imag, turn_angle[:, :, None])
    field = jnp.stack([inverse_real, inverse_imag])
    for bit_index in range(ctx_bits):
        half_span = 1 << bit_index
        partner = partner_2(field.astype(jnp.bfloat16), "ctx", bit_index).astype(field.dtype)
        upper_half = position >> bit_index & 1
        turn_angle = (position % half_span).astype(jnp.float32) * (math.pi / half_span)
        field = jnp.where(
            upper_half == 1,
            partner - rotate_pair(field, turn_angle),
            field + rotate_pair(partner, turn_angle),
        )
    convolved = (
        field[0, 0] + jnp.cos(start_angle) * field[0, 1] - jnp.sin(start_angle) * field[1, 1]
    ) / length_all
    conv_out = (convolved + skip_gain[None, :] * signal).astype(jnp.bfloat16)
    gated = (value_rows.astype(jnp.float32) * conv_out.astype(jnp.float32)).astype(jnp.bfloat16)
    heads_here = query_rows.shape[1] // HD
    stacked = jnp.stack([key_rows, gated])
    previous = shifted(stacked, "ctx", 1)
    key_window = jnp.concatenate([previous[0], key_rows], axis=0).reshape(
        2 * row_count, heads_here, HD
    )
    value_window = jnp.concatenate([previous[1], gated], axis=0).reshape(
        2 * row_count, heads_here, HD
    )
    query_heads = query_rows.reshape(row_count, heads_here, HD)
    scores = jnp.einsum(
        "qhd,khd->hqk", query_heads, key_window, preferred_element_type=jnp.float32
    ) * HD ** (-0.5)
    query_place = jnp.arange(row_count, dtype=jnp.int32)[:, None]
    key_place = jnp.arange(2 * row_count, dtype=jnp.int32)[None, :] - row_count
    allowed = (key_place <= query_place) & ((key_place >= 0) | (position > 0))
    scores = jnp.where(allowed[None], scores, -jnp.inf)
    row_max = jnp.max(scores, axis=-1, keepdims=True)
    weights = jnp.exp(scores - row_max)
    row_total = jnp.sum(weights, axis=-1)
    mixed_heads = jnp.einsum(
        "hqk,khd->qhd",
        weights.astype(jnp.bfloat16),
        value_window,
        preferred_element_type=jnp.float32,
    )
    mixed_heads = mixed_heads / jnp.transpose(row_total)[:, :, None]
    attention = mixed_heads.reshape(row_count, heads_here * HD).astype(jnp.bfloat16)
    attention_wide = attention.astype(jnp.float32)
    energy = lax.psum(jnp.sum(attention_wide * attention_wide, axis=1), "ch")
    mean_square = energy / WIDTH
    attended = (
        attention_wide * norm_gain[None, :] / jnp.sqrt(mean_square + 1e-06)[:, None]
    ).astype(jnp.bfloat16)
    return (conv_out, attended)


def solution(mesh):
    return jax.shard_map(
        per_device,
        mesh=mesh,
        in_specs=(
            P("ctx", "ch"),
            P("ch", None),
            P("ch", None),
            P("ch"),
            P("ctx", "ch"),
            P("ctx", "ch"),
            P("ctx", "ch"),
            P("ch"),
        ),
        out_specs=(P("ctx", "ch"), P("ctx", "ch")),
        check_vma=False,
    )
```

profile of v0, /device:TPU:101, one launch (start us, length us, event | category | flops | bytes accessed | tf_op | source)
XLA Modules:
  0.0 390.5 jit_solution(3514862450699222593)
XLA Ops:
  0.8 1.0 copy.28
  2.1 2.1 collective-permute-start
  4.4 13.9 %collective-permute-done = bf16[2,2,128,512]{2,3,1,0:T(8,128)(2,1)S(1)} collective-permute-done((bf16[2,2,128,512]{2,3,1,0:T(8,128)(2,1)S(1)}, bf16[2,2,128,512]{2,3,1,0:T(8,128)(2,1)S(1)}, u32[]{:S(2)}, u32[]{:S(2)}) %collective-permute-start) | collective-permute-done | bytes 524320 | tf_op jit(solution)/shard_map/ppermute | solution.py:18
  18.7 2.8 collective-permute-start.1
  21.7 10.8 %collective-permute-done.1 = bf16[2,2,128,512]{2,3,1,0:T(8,128)(2,1)S(1)} collective-permute-done((bf16[2,2,128,512]{2,3,1,0:T(8,128)(2,1)S(1)}, bf16[2,2,128,512]{2,3,1,0:T(8,128)(2,1)S(1)}, u32[]{:S(2)}, u32[]{:S(2)}) %collective-permute-start.1) | collective-permute-done | bytes 524320 | tf_op jit(solution)/shard_map/ppermute | solution.py:18
  32.9 12.7 %collective-permute-start.2 = (bf16[2,2,128,512]{2,3,1,0:T(8,128)(2,1)S(1)}, bf16[2,2,128,512]{2,3,1,0:T(8,128)(2,1)S(1)}, u32[]{:S(2)}, u32[]{:S(2)}) collective-permute-start(bf16[2,2,128,512]{2,3,1,0:T(8,128)(2,1)S(1)} %get-tuple-element.31), channel_id=1, source_target_pairs={{0,64},{8,72},{16,80},{24,88},{32,96},{40,104},{48,112},{56,120},{... | collective-permute-start | bytes 1572872 | tf_op jit(solution)/shard_map/ppermute | solution.py:18
  45.8 24.3 %collective-permute-done.2 = bf16[2,2,128,512]{2,3,1,0:T(8,128)(2,1)S(1)} collective-permute-done((bf16[2,2,128,512]{2,3,1,0:T(8,128)(2,1)S(1)}, bf16[2,2,128,512]{2,3,1,0:T(8,128)(2,1)S(1)}, u32[]{:S(2)}, u32[]{:S(2)}) %collective-permute-start.2) | collective-permute-done | bytes 524320 | tf_op jit(solution)/shard_map/ppermute | solution.py:18
  70.6 17.1 %collective-permute-start.3 = (bf16[2,2,128,512]{2,3,1,0:T(8,128)(2,1)S(1)}, bf16[2,2,128,512]{2,3,1,0:T(8,128)(2,1)S(1)}, u32[]{:S(2)}, u32[]{:S(2)}) collective-permute-start(bf16[2,2,128,512]{2,3,1,0:T(8,128)(2,1)S(1)} %get-tuple-element.29), channel_id=1, source_target_pairs={{0,32},{8,40},{16,48},{24,56},{32,0},{40,8},{48,16},{56,24},{64,96... | collective-permute-start | bytes 1572872 | tf_op jit(solution)/shard_map/ppermute | solution.py:18
  88.1 47.7 %collective-permute-done.3 = bf16[2,2,128,512]{2,3,1,0:T(8,128)(2,1)S(1)} collective-permute-done((bf16[2,2,128,512]{2,3,1,0:T(8,128)(2,1)S(1)}, bf16[2,2,128,512]{2,3,1,0:T(8,128)(2,1)S(1)}, u32[]{:S(2)}, u32[]{:S(2)}) %collective-permute-start.3) | collective-permute-done | bytes 524320 | tf_op jit(solution)/shard_map/ppermute | solution.py:18
  136.2 1.9 collective-permute-start.4
  138.5 24.8 %collective-permute-done.4 = bf16[2,2,128,512]{2,3,1,0:T(8,128)(2,1)S(1)} collective-permute-done((bf16[2,2,128,512]{2,3,1,0:T(8,128)(2,1)S(1)}, bf16[2,2,128,512]{2,3,1,0:T(8,128)(2,1)S(1)}, u32[]{:S(2)}, u32[]{:S(2)}) %collective-permute-start.4) | collective-permute-done | bytes 524320 | tf_op jit(solution)/shard_map/ppermute | solution.py:18
  163.4 1.0 fusion.132
  164.4 2.1 collective-permute-start.5
  166.5 4.8 %fusion.2 = (f32[2,128,512]{2,1,0:T(8,128)S(1)}, f32[2,128,512]{2,1,0:T(8,128)S(1)}) fusion(f32[2,128]{1,0:T(2,128)S(1)} %get-tuple-element.85, f32[16,512]{1,0:T(8,128)S(1)} %get-tuple-element.78, f32[2,128]{1,0:T(2,128)S(1)} %get-tuple-element.86, f32[16,512]{1,0:T(8,128)S(1)} %get-tuple-element.76, f32[16,512]{1,0:T(8,128)S(1)} %get-tuple-element.79, ...), kind=kLoop, calls=%fused_computation.4 | loop fusion | flops 31195136 | bytes 1215488 | tf_op jit(solution)/shard_map/reduce_sum | solution.py:56
  171.7 6.9 %collective-permute-done.5 = bf16[2,2,128,512]{2,3,1,0:T(8,128)(2,1)S(1)} collective-permute-done((bf16[2,2,128,512]{2,3,1,0:T(8,128)(2,1)}, bf16[2,2,128,512]{2,3,1,0:T(8,128)(2,1)S(1)}, u32[]{:S(2)}, u32[]{:S(2)}) %collective-permute-start.5) | collective-permute-done | bytes 524320 | tf_op jit(solution)/shard_map/ppermute | solution.py:18
  184.9 0.9 fusion.26
  185.9 2.2 collective-permute-start.6
  188.2 10.9 %collective-permute-done.6 = bf16[2,2,128,512]{2,3,1,0:T(8,128)(2,1)S(1)} collective-permute-done((bf16[2,2,128,512]{2,3,1,0:T(8,128)(2,1)S(1)}, bf16[2,2,128,512]{2,3,1,0:T(8,128)(2,1)S(1)}, u32[]{:S(2)}, u32[]{:S(2)}) %collective-permute-start.6) | collective-permute-done | bytes 524320 | tf_op jit(solution)/shard_map/ppermute | solution.py:18
  199.5 4.8 %collective-permute-start.7 = (bf16[2,2,128,512]{2,3,1,0:T(8,128)(2,1)S(1)}, bf16[2,2,128,512]{2,3,1,0:T(8,128)(2,1)S(1)}, u32[]{:S(2)}, u32[]{:S(2)}) collective-permute-start(bf16[2,2,128,512]{2,3,1,0:T(8,128)(2,1)S(1)} %get-tuple-element.20), channel_id=1, source_target_pairs={{0,16},{8,24},{16,0},{24,8},{32,48},{40,56},{48,32},{56,40},{64,80... | collective-permute-start | bytes 1572872 | tf_op jit(solution)/shard_map/ppermute | solution.py:18
  204.5 22.7 %collective-permute-done.7 = bf16[2,2,128,512]{2,3,1,0:T(8,128)(2,1)S(1)} collective-permute-done((bf16[2,2,128,512]{2,3,1,0:T(8,128)(2,1)S(1)}, bf16[2,2,128,512]{2,3,1,0:T(8,128)(2,1)S(1)}, u32[]{:S(2)}, u32[]{:S(2)}) %collective-permute-start.7) | collective-permute-done | bytes 524320 | tf_op jit(solution)/shard_map/ppermute | solution.py:18
  227.7 4.6 %collective-permute-start.8 = (bf16[2,2,128,512]{2,3,1,0:T(8,128)(2,1)S(1)}, bf16[2,2,128,512]{2,3,1,0:T(8,128)(2,1)S(1)}, u32[]{:S(2)}, u32[]{:S(2)}) collective-permute-start(bf16[2,2,128,512]{2,3,1,0:T(8,128)(2,1)S(1)} %get-tuple-element.18), channel_id=1, source_target_pairs={{0,32},{8,40},{16,48},{24,56},{32,0},{40,8},{48,16},{56,24},{64,96... | collective-permute-start | bytes 1572872 | tf_op jit(solution)/shard_map/ppermute | solution.py:18
  232.6 53.8 %collective-permute-done.8 = bf16[2,2,128,512]{2,3,1,0:T(8,128)(2,1)S(1)} collective-permute-done((bf16[2,2,128,512]{2,3,1,0:T(8,128)(2,1)S(1)}, bf16[2,2,128,512]{2,3,1,0:T(8,128)(2,1)S(1)}, u32[]{:S(2)}, u32[]{:S(2)}) %collective-permute-start.8) | collective-permute-done | bytes 524320 | tf_op jit(solution)/shard_map/ppermute | solution.py:18
  286.8 11.5 %collective-permute-start.9 = (bf16[2,2,128,512]{2,3,1,0:T(8,128)(2,1)S(1)}, bf16[2,2,128,512]{2,3,1,0:T(8,128)(2,1)S(1)}, u32[]{:S(2)}, u32[]{:S(2)}) collective-permute-start(bf16[2,2,128,512]{2,3,1,0:T(8,128)(2,1)S(1)} %get-tuple-element.16), channel_id=1, source_target_pairs={{0,64},{8,72},{16,80},{24,88},{32,96},{40,104},{48,112},{56,120},{... | collective-permute-start | bytes 1572872 | tf_op jit(solution)/shard_map/ppermute | solution.py:18
  298.6 34.2 %collective-permute-done.9 = bf16[2,2,128,512]{2,3,1,0:T(8,128)(2,1)S(1)} collective-permute-done((bf16[2,2,128,512]{2,3,1,0:T(8,128)(2,1)S(1)}, bf16[2,2,128,512]{2,3,1,0:T(8,128)(2,1)S(1)}, u32[]{:S(2)}, u32[]{:S(2)}) %collective-permute-start.9) | collective-permute-done | bytes 524320 | tf_op jit(solution)/shard_map/ppermute | solution.py:18
  333.2 2.9 collective-permute-start.10
  336.4 11.7 %collective-permute-done.10 = bf16[2,2,128,512]{2,3,1,0:T(8,128)(2,1)S(1)} collective-permute-done((bf16[2,2,128,512]{2,3,1,0:T(8,128)(2,1)S(1)}, bf16[2,2,128,512]{2,3,1,0:T(8,128)(2,1)S(1)}, u32[]{:S(2)}, u32[]{:S(2)}) %collective-permute-start.10) | collective-permute-done | bytes 524320 | tf_op jit(solution)/shard_map/ppermute | solution.py:18
  348.3 1.0 fusion.122
  349.3 2.2 collective-permute-start.11
  352.1 13.0 %collective-permute-done.11 = bf16[2,2,128,512]{2,3,1,0:T(8,128)(2,1)S(1)} collective-permute-done((bf16[2,2,128,512]{2,3,1,0:T(8,128)(2,1)}, bf16[2,2,128,512]{2,3,1,0:T(8,128)(2,1)S(1)}, u32[]{:S(2)}, u32[]{:S(2)}) %collective-permute-start.11) | collective-permute-done | bytes 524320 | tf_op jit(solution)/shard_map/ppermute | solution.py:18
  366.1 2.3 collective-permute-start.12
  369.5 4.2 %collective-permute-done.12 = bf16[2,128,512]{1,2,0:T(8,128)(2,1)S(1)} collective-permute-done((bf16[2,128,512]{1,2,0:T(8,128)(2,1)S(1)}, bf16[2,128,512]{1,2,0:T(8,128)(2,1)S(1)}, u32[]{:S(2)}, u32[]{:S(2)}) %collective-permute-start.12) | collective-permute-done | bytes 262176 | tf_op jit(solution)/shard_map/ppermute | solution.py:24
  374.6 15.1 %psum.7 = f32[128]{0:T(128)S(1)} all-reduce(f32[128]{0:T(128)S(1)} %get-tuple-element.90), channel_id=1, replica_groups=mesh['ctx'=64,'ch'=8] {'ch'}, use_global_device_ids=true, to_apply=%region_5.6 | all-reduce | flops 128 | bytes 1024 | tf_op jit(solution)/shard_map/psum | solution.py:165
  (91 shorter events, 15.4 us)
Async XLA Ops:
  0.6 373.2 %copy-start = (bf16[128,512]{1,0:T(8,128)(2,1)S(1)}, bf16[128,512]{1,0:T(8,128)(2,1)}, u32[]{:S(2)}) copy-start(bf16[128,512]{1,0:T(8,128)(2,1)} %param.12) | copy-start | bytes 393220
  2.1 16.2 %collective-permute-start = (bf16[2,2,128,512]{2,3,1,0:T(8,128)(2,1)S(1)}, bf16[2,2,128,512]{2,3,1,0:T(8,128)(2,1)S(1)}, u32[]{:S(2)}, u32[]{:S(2)}) collective-permute-start(bf16[2,2,128,512]{2,3,1,0:T(8,128)(2,1)S(1)} %fusion.23), channel_id=1, source_target_pairs={{0,256},{8,264},{16,272},{24,280},{32,288},{40,296},{48,304},{56,3... | collective-permute-start | bytes 1572872 | tf_op jit(solution)/shard_map/ppermute | solution.py:18
  18.7 13.8 %collective-permute-start.1 = (bf16[2,2,128,512]{2,3,1,0:T(8,128)(2,1)S(1)}, bf16[2,2,128,512]{2,3,1,0:T(8,128)(2,1)S(1)}, u32[]{:S(2)}, u32[]{:S(2)}) collective-permute-start(bf16[2,2,128,512]{2,3,1,0:T(8,128)(2,1)S(1)} %get-tuple-element.33), channel_id=1, source_target_pairs={{0,128},{8,136},{16,144},{24,152},{32,160},{40,168},{48,176},{56,1... | collective-permute-start | bytes 1572872 | tf_op jit(solution)/shard_map/ppermute | solution.py:18
  32.9 37.3 %collective-permute-start.2 = (bf16[2,2,128,512]{2,3,1,0:T(8,128)(2,1)S(1)}, bf16[2,2,128,512]{2,3,1,0:T(8,128)(2,1)S(1)}, u32[]{:S(2)}, u32[]{:S(2)}) collective-permute-start(bf16[2,2,128,512]{2,3,1,0:T(8,128)(2,1)S(1)} %get-tuple-element.31), channel_id=1, source_target_pairs={{0,64},{8,72},{16,80},{24,88},{32,96},{40,104},{48,112},{56,120},{... | collective-permute-start | bytes 1572872 | tf_op jit(solution)/shard_map/ppermute | solution.py:18
  70.6 65.2 %collective-permute-start.3 = (bf16[2,2,128,512]{2,3,1,0:T(8,128)(2,1)S(1)}, bf16[2,2,128,512]{2,3,1,0:T(8,128)(2,1)S(1)}, u32[]{:S(2)}, u32[]{:S(2)}) collective-permute-start(bf16[2,2,128,512]{2,3,1,0:T(8,128)(2,1)S(1)} %get-tuple-element.29), channel_id=1, source_target_pairs={{0,32},{8,40},{16,48},{24,56},{32,0},{40,8},{48,16},{56,24},{64,96... | collective-permute-start | bytes 1572872 | tf_op jit(solution)/shard_map/ppermute | solution.py:18
  136.0 2.4 copy-start.3
  136.0 2.4 copy-start.4
  136.2 27.0 %collective-permute-start.4 = (bf16[2,2,128,512]{2,3,1,0:T(8,128)(2,1)S(1)}, bf16[2,2,128,512]{2,3,1,0:T(8,128)(2,1)S(1)}, u32[]{:S(2)}, u32[]{:S(2)}) collective-permute-start(bf16[2,2,128,512]{2,3,1,0:T(8,128)(2,1)S(1)} %get-tuple-element.27), channel_id=1, source_target_pairs={{0,16},{8,24},{16,0},{24,8},{32,48},{40,56},{48,32},{56,40},{64,80... | collective-permute-start | bytes 1572872 | tf_op jit(solution)/shard_map/ppermute | solution.py:18
  164.4 14.2 %collective-permute-start.5 = (bf16[2,2,128,512]{2,3,1,0:T(8,128)(2,1)}, bf16[2,2,128,512]{2,3,1,0:T(8,128)(2,1)S(1)}, u32[]{:S(2)}, u32[]{:S(2)}) collective-permute-start(bf16[2,2,128,512]{2,3,1,0:T(8,128)(2,1)} %get-tuple-element.25), channel_id=1, source_target_pairs={{0,8},{8,0},{16,24},{24,16},{32,40},{40,32},{48,56},{56,48},{64,72... | collective-permute-start | bytes 1572872 | tf_op jit(solution)/shard_map/ppermute | solution.py:18
  185.9 13.2 %collective-permute-start.6 = (bf16[2,2,128,512]{2,3,1,0:T(8,128)(2,1)S(1)}, bf16[2,2,128,512]{2,3,1,0:T(8,128)(2,1)S(1)}, u32[]{:S(2)}, u32[]{:S(2)}) collective-permute-start(bf16[2,2,128,512]{2,3,1,0:T(8,128)(2,1)S(1)} %fusion.22), channel_id=1, source_target_pairs={{0,8},{8,0},{16,24},{24,16},{32,40},{40,32},{48,56},{56,48},{64,72... | collective-permute-start | bytes 1572872 | tf_op jit(solution)/shard_map/ppermute | solution.py:18
  199.5 27.7 %collective-permute-start.7 = (bf16[2,2,128,512]{2,3,1,0:T(8,128)(2,1)S(1)}, bf16[2,2,128,512]{2,3,1,0:T(8,128)(2,1)S(1)}, u32[]{:S(2)}, u32[]{:S(2)}) collective-permute-start(bf16[2,2,128,512]{2,3,1,0:T(8,128)(2,1)S(1)} %get-tuple-element.20), channel_id=1, source_target_pairs={{0,16},{8,24},{16,0},{24,8},{32,48},{40,56},{48,32},{56,40},{64,80... | collective-permute-start | bytes 1572872 | tf_op jit(solution)/shard_map/ppermute | solution.py:18
  227.7 58.7 %collective-permute-start.8 = (bf16[2,2,128,512]{2,3,1,0:T(8,128)(2,1)S(1)}, bf16[2,2,128,512]{2,3,1,0:T(8,128)(2,1)S(1)}, u32[]{:S(2)}, u32[]{:S(2)}) collective-permute-start(bf16[2,2,128,512]{2,3,1,0:T(8,128)(2,1)S(1)} %get-tuple-element.18), channel_id=1, source_target_pairs={{0,32},{8,40},{16,48},{24,56},{32,0},{40,8},{48,16},{56,24},{64,96... | collective-permute-start | bytes 1572872 | tf_op jit(solution)/shard_map/ppermute | solution.py:18
  286.8 45.9 %collective-permute-start.9 = (bf16[2,2,128,512]{2,3,1,0:T(8,128)(2,1)S(1)}, bf16[2,2,128,512]{2,3,1,0:T(8,128)(2,1)S(1)}, u32[]{:S(2)}, u32[]{:S(2)}) collective-permute-start(bf16[2,2,128,512]{2,3,1,0:T(8,128)(2,1)S(1)} %get-tuple-element.16), channel_id=1, source_target_pairs={{0,64},{8,72},{16,80},{24,88},{32,96},{40,104},{48,112},{56,120},{... | collective-permute-start | bytes 1572872 | tf_op jit(solution)/shard_map/ppermute | solution.py:18
  333.2 14.9 %collective-permute-start.10 = (bf16[2,2,128,512]{2,3,1,0:T(8,128)(2,1)S(1)}, bf16[2,2,128,512]{2,3,1,0:T(8,128)(2,1)S(1)}, u32[]{:S(2)}, u32[]{:S(2)}) collective-permute-start(bf16[2,2,128,512]{2,3,1,0:T(8,128)(2,1)S(1)} %get-tuple-element.14), channel_id=1, source_target_pairs={{0,128},{8,136},{16,144},{24,152},{32,160},{40,168},{48,176},{56,1... | collective-permute-start | bytes 1572872 | tf_op jit(solution)/shard_map/ppermute | solution.py:18
  348.3 3.4 copy-start.1
  348.3 3.5 copy-start.2
  349.3 15.7 %collective-permute-start.11 = (bf16[2,2,128,512]{2,3,1,0:T(8,128)(2,1)}, bf16[2,2,128,512]{2,3,1,0:T(8,128)(2,1)S(1)}, u32[]{:S(2)}, u32[]{:S(2)}) collective-permute-start(bf16[2,2,128,512]{2,3,1,0:T(8,128)(2,1)} %get-tuple-element.12), channel_id=1, source_target_pairs={{0,256},{8,264},{16,272},{24,280},{32,288},{40,296},{48,304},{56,3... | collective-permute-start | bytes 1572872 | tf_op jit(solution)/shard_map/ppermute | solution.py:18
  365.3 0.7 copy-start.5
  366.1 7.6 %collective-permute-start.12 = (bf16[2,128,512]{1,2,0:T(8,128)(2,1)S(1)}, bf16[2,128,512]{1,2,0:T(8,128)(2,1)S(1)}, u32[]{:S(2)}, u32[]{:S(2)}) collective-permute-start(bf16[2,128,512]{1,2,0:T(8,128)(2,1)S(1)} %pad_maximum_fusion.2), channel_id=1, source_target_pairs={{0,8},{8,16},{16,24},{24,32},{32,40},{40,48},{48,56},{56,64},{64,7... | collective-permute-start | bytes 786440 | tf_op jit(solution)/shard_map/ppermute | solution.py:24
  374.2 15.5 %copy-start.6 = (f32[512]{0:T(512)S(1)}, f32[512]{0:T(512)}, u32[]{:S(2)}) copy-start(f32[512]{0:T(512)} %param.15) | copy-start | bytes 6148
where the time goes:
time: 391 us; the launch traced here: 390 us
  waiting for transfers between devices  279 us (71%)
  starting transfers between devices  69.2 us (18%)
  blocking collectives  15.1 us (4%)
  other arithmetic  13.6 us (3%)
  matrix products  7.23 us (2%)
    ppermute x12, waiting for transfers between devices, partner_2(): return lax.ppermute(value, axis, pairs)  275 us
    ppermute x12, starting transfers between devices, partner_2(): return lax.ppermute(value, axis, pairs)  66.9 us
    psum x1, blocking collectives, per_device(): energy = lax.psum(jnp.sum(attention_wide * attention_wide, axis=1), 'ch')  15.1 us
  transfers between devices with their start and end apart: 13, of which 13 were waited for; matrix products, arithmetic and copies ran while one was open for 2% of the time, Pallas kernels for 0%

commit v1 on v0

v1 whole, which is shorter than its diff:
```python
import jax
import jax.numpy as jnp
from jax import lax
from jax.sharding import PartitionSpec as P

HD = 128


def partner_2(value, axis, apart):
    mask = 2**apart
    pairs = [(source, source ^ mask) for source in range(lax.axis_size(axis))]
    return lax.ppermute(value, axis, pairs)


def shifted(block, axis, distance):
    devices = range(lax.axis_size(axis))
    route = [(i - distance, i) for i in devices if i - distance in devices]
    return lax.ppermute(block, axis, route)


def per_device(
    conv_input, residues, decay_rates, skip_gain, query_rows, key_rows, value_rows, norm_gain
):
    ctx_count = lax.axis_size("ctx")
    ch_count = lax.axis_size("ch")
    position = lax.axis_index("ctx")
    row_count, chan_count = conv_input.shape
    signal = conv_input.astype(jnp.float32)
    rates = jnp.transpose(decay_rates)
    weight = jnp.transpose(residues) * jnp.sqrt(-jnp.expm1(-rates) * (1.0 + jnp.exp(-rates)))
    steps = jnp.arange(row_count, dtype=jnp.float32)
    last = float(row_count - 1)

    tail = jnp.exp(-rates[:, None, :] * (last - steps)[None, :, None])
    own_state = jnp.sum(tail * signal[None], axis=1)

    before = jnp.zeros_like(own_state)
    span = 1
    while span < ctx_count:
        sent = own_state + before
        got = shifted(sent, "ctx", span)
        before = before + jnp.exp(-rates * float(row_count * span)) * got
        span *= 2

    rise = jnp.exp(rates[:, None, :] * steps[None, :, None])
    lifted = rise * signal[None]
    lifted_hi = lifted.astype(jnp.bfloat16)
    lifted_lo = (lifted - lifted_hi.astype(jnp.float32)).astype(jnp.bfloat16)
    lower = (steps[:, None] >= steps[None, :]).astype(jnp.bfloat16)
    prefix = jnp.einsum(
        "ts,rsc->rtc", lower, lifted_hi, preferred_element_type=jnp.float32
    ) + jnp.einsum("ts,rsc->rtc", lower, lifted_lo, preferred_element_type=jnp.float32)

    fall = weight[:, None, :] * jnp.exp(-rates[:, None, :] * steps[None, :, None])
    carried = jnp.exp(rates * last) * before
    convolved = jnp.sum(fall * (prefix + carried[:, None, :]), axis=0)
    conv_out = (convolved + skip_gain[None, :] * signal).astype(jnp.bfloat16)
    gated = (value_rows.astype(jnp.float32) * conv_out.astype(jnp.float32)).astype(jnp.bfloat16)

    heads_here = query_rows.shape[1] // HD
    previous_keys = shifted(key_rows, "ctx", 1)
    previous_gated = shifted(gated, "ctx", 1)
    key_window = jnp.concatenate([previous_keys, key_rows], axis=0).reshape(
        2 * row_count, heads_here, HD
    )
    value_window = jnp.concatenate([previous_gated, gated], axis=0).reshape(
        2 * row_count, heads_here, HD
    )
    query_heads = query_rows.reshape(row_count, heads_here, HD)
    scores = jnp.einsum(
        "qhd,khd->hqk", query_heads, key_window, preferred_element_type=jnp.float32
    ) * HD ** (-0.5)
    query_place = jnp.arange(row_count, dtype=jnp.int32)[:, None]
    key_place = jnp.arange(2 * row_count, dtype=jnp.int32)[None, :] - row_count
    allowed = (key_place <= query_place) & ((key_place >= 0) | (position > 0))
    scores = jnp.where(allowed[None], scores, -jnp.inf)
    row_max = jnp.max(scores, axis=-1, keepdims=True)
    weights = jnp.exp(scores - row_max)
    row_total = jnp.sum(weights, axis=-1)
    mixed_heads = jnp.einsum(
        "hqk,khd->qhd",
        weights.astype(jnp.bfloat16),
        value_window,
        preferred_element_type=jnp.float32,
    )
    mixed_heads = mixed_heads / jnp.transpose(row_total)[:, :, None]
    attention = mixed_heads.reshape(row_count, heads_here * HD).astype(jnp.bfloat16)
    attention_wide = attention.astype(jnp.float32)
    energy = jnp.sum(attention_wide * attention_wide, axis=1)
    for bit_index in range(ch_count.bit_length() - 1):
        energy = energy + partner_2(energy, "ch", bit_index)
    mean_square = energy / float(query_rows.shape[1] * ch_count)
    attended = (
        attention_wide * norm_gain[None, :] / jnp.sqrt(mean_square + 1e-06)[:, None]
    ).astype(jnp.bfloat16)
    return (conv_out, attended)


def solution(mesh):
    return jax.shard_map(
        per_device,
        mesh=mesh,
        in_specs=(
            P("ctx", "ch"),
            P("ch", None),
            P("ch", None),
            P("ch"),
            P("ctx", "ch"),
            P("ctx", "ch"),
            P("ctx", "ch"),
            P("ch"),
        ),
        out_specs=(P("ctx", "ch"), P("ctx", "ch")),
        check_vma=False,
    )
```

time: 391 us -> 103 us (0.26)
  the two profiles are of different devices: /device:TPU:101 before, /device:TPU:6 now
where the time goes in v1:
time: 103 us
  starting transfers between devices  43 us (42%)
  waiting for transfers between devices  38.6 us (37%)
  matrix products  12.3 us (12%)
  other arithmetic  4.57 us (4%)
  local copies, waits for them, and re-layouts  3.16 us (3%)
    ppermute x8, waiting for transfers between devices, shifted(): return lax.ppermute(block, axis, route)  34.6 us
    ppermute x8, starting transfers between devices, shifted(): return lax.ppermute(block, axis, route)  32.5 us
    ppermute x3, starting transfers between devices, partner_2(): return lax.ppermute(value, axis, pairs)  10.5 us
    dot_general x1, matrix products, per_device(): jnp.einsum('ts,rsc->rtc', lower, lifted_hi, preferred_element_type=jnp.fl...  7.53 us
    dot_general x1, matrix products, per_device(): jnp.einsum('ts,rsc->rtc', lower, lifted_lo, preferred_element_type=jnp.fl...  4.2 us
    ppermute x3, waiting for transfers between devices, partner_2(): return lax.ppermute(value, axis, pairs)  4.05 us
    unnamed x14, local copies, waits for them, and re-layouts  3.03 us
    reduce_sum x1, other arithmetic, per_device(): own_state = jnp.sum(tail * signal[None], axis=1)  2.39 us
  transfers between devices with their start and end apart: 11, of which 10 were waited for; matrix products, arithmetic and copies ran while one was open for 7% of the time, Pallas kernels for 0%

profile of v1, /device:TPU:6, one launch (start us, length us, event | category | flops | bytes accessed | tf_op | source)
XLA Modules:
  0.0 102.5 jit_solution(16474136028110012723)
XLA Ops:
  0.7 1.1 %copy.23 = bf16[128,512]{0,1:T(8,128)(2,1)S(1)} copy(bf16[128,512]{1,0:T(8,128)(2,1)} %param.8) | data formatting | bytes 262144 | tf_op args[0]
  1.8 0.8 bitcast_multiply_fusion.1
  2.6 2.4 %multiply_reduce_fusion = f32[16,512]{1,0:T(8,128)S(1)} fusion(f32[128]{0:T(128)S(1)} %iota_subtract_fusion, f32[128,512]{0,1:T(8,128)S(1)} %convert_element_type.45, f32[16,512]{1,0:T(8,128)S(1)} %get-tuple-element.9), kind=kLoop, calls=%fused_computation.2 | loop fusion | flops 3137536 | bytes 328192 | tf_op jit(solution)/shard_map/reduce_sum | solution.py:35
  5.0 3.8 %collective-permute-start = (f32[16,512]{1,0:T(8,128)S(1)}, f32[16,512]{1,0:T(8,128)S(1)}, u32[]{:S(2)}, u32[]{:S(2)}) collective-permute-start(f32[16,512]{1,0:T(8,128)S(1)} %multiply_reduce_fusion), channel_id=1, source_target_pairs={{0,8},{8,16},{16,24},{24,32},{32,40},{40,48},{48,56},{56,64},{64,7... | collective-permute-start | bytes 98312 | tf_op jit(solution)/shard_map/ppermute | solution.py:18
  8.8 1.0 copy.25
  9.9 3.8 %collective-permute-start.7 = (bf16[128,512]{0,1:T(8,128)(2,1)S(1)}, bf16[128,512]{0,1:T(8,128)(2,1)S(1)}, u32[]{:S(2)}, u32[]{:S(2)}) collective-permute-start(bf16[128,512]{0,1:T(8,128)(2,1)S(1)} %copy.25), channel_id=1, source_target_pairs={{0,8},{8,16},{16,24},{24,32},{32,40},{40,48},{48,56},{56,64},{64,7... | collective-permute-start | bytes 393224 | tf_op jit(solution)/shard_map/ppermute | solution.py:18
  13.7 4.2 %fusion.4 = f32[16,512,128]{2,1,0:T(8,128)} fusion(f32[128,512]{0,1:T(8,128)S(1)} %convert_element_type.45, f32[16,512]{1,0:T(8,128)} %bitcast.53), kind=kOutput, calls=%fused_computation.7 | convolution fusion | flops 274743296 | bytes 4489216 | tf_op jit(solution)/shard_map/ts,rsc->rtc/dot_general | solution.py:52
  17.9 0.7 collective-permute-done
  18.6 5.7 %collective-permute-start.1 = (f32[16,512]{1,0:T(8,128)S(1)}, f32[16,512]{1,0:T(8,128)S(1)}, u32[]{:S(2)}, u32[]{:S(2)}) collective-permute-start(f32[16,512]{1,0:T(8,128)S(1)} %fusion.26), channel_id=1, source_target_pairs={{0,16},{8,24},{16,32},{24,40},{32,48},{40,56},{48,64},{56,72},{64,... | collective-permute-start | bytes 98312 | tf_op jit(solution)/shard_map/ppermute | solution.py:18
  24.3 5.1 %collective-permute-done.1 = f32[16,512]{1,0:T(8,128)S(1)} collective-permute-done((f32[16,512]{1,0:T(8,128)S(1)}, f32[16,512]{1,0:T(8,128)S(1)}, u32[]{:S(2)}, u32[]{:S(2)}) %collective-permute-start.1) | collective-permute-done | bytes 32800 | tf_op jit(solution)/shard_map/ppermute | solution.py:18
  29.5 5.5 %collective-permute-start.2 = (f32[16,512]{1,0:T(8,128)S(1)}, f32[16,512]{1,0:T(8,128)S(1)}, u32[]{:S(2)}, u32[]{:S(2)}) collective-permute-start(f32[16,512]{1,0:T(8,128)S(1)} %fusion.29), channel_id=1, source_target_pairs={{0,32},{8,40},{16,48},{24,56},{32,64},{40,72},{48,80},{56,88},{64,... | collective-permute-start | bytes 98312 | tf_op jit(solution)/shard_map/ppermute | solution.py:18
  35.1 5.4 %collective-permute-done.2 = f32[16,512]{1,0:T(8,128)S(1)} collective-permute-done((f32[16,512]{1,0:T(8,128)S(1)}, f32[16,512]{1,0:T(8,128)S(1)}, u32[]{:S(2)}, u32[]{:S(2)}) %collective-permute-start.2) | collective-permute-done | bytes 32800 | tf_op jit(solution)/shard_map/ppermute | solution.py:18
  40.5 9.0 %collective-permute-start.3 = (f32[16,512]{1,0:T(8,128)S(1)}, f32[16,512]{1,0:T(8,128)S(1)}, u32[]{:S(2)}, u32[]{:S(2)}) collective-permute-start(f32[16,512]{1,0:T(8,128)S(1)} %fusion.27), channel_id=1, source_target_pairs={{0,64},{8,72},{16,80},{24,88},{32,96},{40,104},{48,112},{56,120},{... | collective-permute-start | bytes 98312 | tf_op jit(solution)/shard_map/ppermute | solution.py:18
  49.8 6.3 %collective-permute-done.3 = f32[16,512]{1,0:T(8,128)S(1)} collective-permute-done((f32[16,512]{1,0:T(8,128)S(1)}, f32[16,512]{1,0:T(8,128)S(1)}, u32[]{:S(2)}, u32[]{:S(2)}) %collective-permute-start.3) | collective-permute-done | bytes 32800 | tf_op jit(solution)/shard_map/ppermute | solution.py:18
  56.1 1.3 %collective-permute-start.4 = (f32[16,512]{1,0:T(8,128)S(1)}, f32[16,512]{1,0:T(8,128)S(1)}, u32[]{:S(2)}, u32[]{:S(2)}) collective-permute-start(f32[16,512]{1,0:T(8,128)S(1)} %get-tuple-element.6), channel_id=1, source_target_pairs={{0,128},{8,136},{16,144},{24,152},{32,160},{40,168},{48,176},{56,1... | collective-permute-start | bytes 98312 | tf_op jit(solution)/shard_map/ppermute | solution.py:18
  57.5 4.5 %collective-permute-done.4 = f32[16,512]{1,0:T(8,128)S(1)} collective-permute-done((f32[16,512]{1,0:T(8,128)S(1)}, f32[16,512]{1,0:T(8,128)S(1)}, u32[]{:S(2)}, u32[]{:S(2)}) %collective-permute-start.4) | collective-permute-done | bytes 32800 | tf_op jit(solution)/shard_map/ppermute | solution.py:18
  62.0 1.3 %collective-permute-start.5 = (f32[16,512]{1,0:T(8,128)S(1)}, f32[16,512]{1,0:T(8,128)S(1)}, u32[]{:S(2)}, u32[]{:S(2)}) collective-permute-start(f32[16,512]{1,0:T(8,128)S(1)} %fusion.28), channel_id=1, source_target_pairs={{0,256},{8,264},{16,272},{24,280},{32,288},{40,296},{48,304},{56,3... | collective-permute-start | bytes 98312 | tf_op jit(solution)/shard_map/ppermute | solution.py:18
  63.3 0.3 fusion.31
  63.6 5.7 %collective-permute-done.5 = f32[16,512]{1,0:T(8,128)S(1)} collective-permute-done((f32[16,512]{1,0:T(8,128)S(1)}, f32[16,512]{1,0:T(8,128)S(1)}, u32[]{:S(2)}, u32[]{:S(2)}) %collective-permute-start.5) | collective-permute-done | bytes 32800 | tf_op jit(solution)/shard_map/ppermute | solution.py:18
  69.3 7.5 %fusion = f32[128,512]{0,1:T(8,128)S(1)} fusion(f32[16,512,128]{2,1,0:T(8,128)} %fusion.4, f32[16,512]{1,0:T(8,128)S(1)} %add_multiply_fusion, f32[16,512]{1,0:T(8,128)S(1)} %get-tuple-element.9, f32[16,512]{1,0:T(8,128)S(1)} %get-tuple-element.8, f32[128,512]{0,1:T(8,128)S(1)} %convert_element_type.45, f32[16,512]{1,0:T(8,128)S(1)} %bitcast.54), kind=kOutput, calls=%fused_computation.1 | convolution fusion | flops 277823488 | bytes 4849664 | tf_op jit(solution)/shard_map/ts,rsc->rtc/dot_general | solution.py:50
  76.9 0.1 multiply_convert_fusion
  77.0 1.9 %collective-permute-start.6 = (bf16[128,512]{0,1:T(8,128)(2,1)S(1)}, bf16[128,512]{0,1:T(8,128)(2,1)S(1)}, u32[]{:S(2)}, u32[]{:S(2)}) collective-permute-start(bf16[128,512]{0,1:T(8,128)(2,1)S(1)} %get-tuple-element.4), channel_id=1, source_target_pairs={{0,8},{8,16},{16,24},{24,32},{32,40},{40,48},{48,56},{56,64},{64,7... | collective-permute-start | bytes 393224 | tf_op jit(solution)/shard_map/ppermute | solution.py:18
  79.1 6.9 %collective-permute-done.6 = bf16[128,512]{0,1:T(8,128)(2,1)S(1)} collective-permute-done((bf16[128,512]{0,1:T(8,128)(2,1)S(1)}, bf16[128,512]{0,1:T(8,128)(2,1)S(1)}, u32[]{:S(2)}, u32[]{:S(2)}) %collective-permute-start.6) | collective-permute-done | bytes 131104 | tf_op jit(solution)/shard_map/ppermute | solution.py:18
  86.0 0.3 multiply_reduce_fusion.1
  86.3 1.9 %collective-permute-start.8 = (f32[128]{0:T(128)S(1)}, f32[128]{0:T(128)S(1)}, u32[]{:S(2)}, u32[]{:S(2)}) collective-permute-start(f32[128]{0:T(128)S(1)} %get-tuple-element.12), channel_id=1, source_target_pairs={{0,1},{1,0},{2,3},{3,2},{4,5},{5,4},{6,7},{7,6},{8,9},{9,8},{10,11... | collective-permute-start | bytes 1544 | tf_op jit(solution)/shard_map/ppermute | solution.py:12
  88.2 1.1 %collective-permute-done.8 = f32[128]{0:T(128)S(1)} collective-permute-done((f32[128]{0:T(128)S(1)}, f32[128]{0:T(128)S(1)}, u32[]{:S(2)}, u32[]{:S(2)}) %collective-permute-start.8) | collective-permute-done | bytes 544 | tf_op jit(solution)/shard_map/ppermute | solution.py:12
  89.4 3.5 %collective-permute-start.9 = (f32[128]{0:T(128)S(1)}, f32[128]{0:T(128)S(1)}, u32[]{:S(2)}, u32[]{:S(2)}) collective-permute-start(f32[128]{0:T(128)S(1)} %add.95), channel_id=1, source_target_pairs={{0,2},{1,3},{2,0},{3,1},{4,6},{5,7},{6,4},{7,5},{8,10},{9,11},{10,... | collective-permute-start | bytes 1544 | tf_op jit(solution)/shard_map/ppermute | solution.py:12
  92.8 2.0 %collective-permute-done.9 = f32[128]{0:T(128)S(1)} collective-permute-done((f32[128]{0:T(128)S(1)}, f32[128]{0:T(128)S(1)}, u32[]{:S(2)}, u32[]{:S(2)}) %collective-permute-start.9) | collective-permute-done | bytes 544 | tf_op jit(solution)/shard_map/ppermute | solution.py:12
  94.8 5.1 %collective-permute-start.10 = (f32[128]{0:T(128)S(1)}, f32[128]{0:T(128)S(1)}, u32[]{:S(2)}, u32[]{:S(2)}) collective-permute-start(f32[128]{0:T(128)S(1)} %add.96), channel_id=1, source_target_pairs={{0,4},{1,5},{2,6},{3,7},{4,0},{5,1},{6,2},{7,3},{8,12},{9,13},{10,... | collective-permute-start | bytes 1544 | tf_op jit(solution)/shard_map/ppermute | solution.py:12
  99.9 0.8 copy.31
  100.8 0.9 collective-permute-done.10
  101.8 0.8 divide_convert_fusion
  (30 shorter events, 0.8 us)
Async XLA Ops:
  0.6 62.7 %copy-start = (bf16[128,512]{1,0:T(8,128)(2,1)S(1)}, bf16[128,512]{1,0:T(8,128)(2,1)}, u32[]{:S(2)}) copy-start(bf16[128,512]{1,0:T(8,128)(2,1)} %param.12) | copy-start | bytes 393220
  0.6 17.9 %copy-start.1 = (f32[512,16]{0,1:T(8,128)S(1)}, f32[512,16]{0,1:T(8,128)}, u32[]{:S(2)}) copy-start(f32[512,16]{0,1:T(8,128)} %param.10) | copy-start | bytes 98308
  0.7 49.0 %copy-start.2 = (bf16[128,512]{1,0:T(8,128)(2,1)S(1)}, bf16[128,512]{1,0:T(8,128)(2,1)}, u32[]{:S(2)}) copy-start(bf16[128,512]{1,0:T(8,128)(2,1)} %param.14) | copy-start | bytes 393220
  5.0 13.6 %collective-permute-start = (f32[16,512]{1,0:T(8,128)S(1)}, f32[16,512]{1,0:T(8,128)S(1)}, u32[]{:S(2)}, u32[]{:S(2)}) collective-permute-start(f32[16,512]{1,0:T(8,128)S(1)} %multiply_reduce_fusion), channel_id=1, source_target_pairs={{0,8},{8,16},{16,24},{24,32},{32,40},{40,48},{48,56},{56,64},{64,7... | collective-permute-start | bytes 98312 | tf_op jit(solution)/shard_map/ppermute | solution.py:18
  9.9 47.6 %collective-permute-start.7 = (bf16[128,512]{0,1:T(8,128)(2,1)S(1)}, bf16[128,512]{0,1:T(8,128)(2,1)S(1)}, u32[]{:S(2)}, u32[]{:S(2)}) collective-permute-start(bf16[128,512]{0,1:T(8,128)(2,1)S(1)} %copy.25), channel_id=1, source_target_pairs={{0,8},{8,16},{16,24},{24,32},{32,40},{40,48},{48,56},{56,64},{64,7... | collective-permute-start | bytes 393224 | tf_op jit(solution)/shard_map/ppermute | solution.py:18
  18.6 10.9 %collective-permute-start.1 = (f32[16,512]{1,0:T(8,128)S(1)}, f32[16,512]{1,0:T(8,128)S(1)}, u32[]{:S(2)}, u32[]{:S(2)}) collective-permute-start(f32[16,512]{1,0:T(8,128)S(1)} %fusion.26), channel_id=1, source_target_pairs={{0,16},{8,24},{16,32},{24,40},{32,48},{40,56},{48,64},{56,72},{64,... | collective-permute-start | bytes 98312 | tf_op jit(solution)/shard_map/ppermute | solution.py:18
  29.5 11.0 %collective-permute-start.2 = (f32[16,512]{1,0:T(8,128)S(1)}, f32[16,512]{1,0:T(8,128)S(1)}, u32[]{:S(2)}, u32[]{:S(2)}) collective-permute-start(f32[16,512]{1,0:T(8,128)S(1)} %fusion.29), channel_id=1, source_target_pairs={{0,32},{8,40},{16,48},{24,56},{32,64},{40,72},{48,80},{56,88},{64,... | collective-permute-start | bytes 98312 | tf_op jit(solution)/shard_map/ppermute | solution.py:18
  40.5 15.6 %collective-permute-start.3 = (f32[16,512]{1,0:T(8,128)S(1)}, f32[16,512]{1,0:T(8,128)S(1)}, u32[]{:S(2)}, u32[]{:S(2)}) collective-permute-start(f32[16,512]{1,0:T(8,128)S(1)} %fusion.27), channel_id=1, source_target_pairs={{0,64},{8,72},{16,80},{24,88},{32,96},{40,104},{48,112},{56,120},{... | collective-permute-start | bytes 98312 | tf_op jit(solution)/shard_map/ppermute | solution.py:18
  56.1 5.8 %collective-permute-start.4 = (f32[16,512]{1,0:T(8,128)S(1)}, f32[16,512]{1,0:T(8,128)S(1)}, u32[]{:S(2)}, u32[]{:S(2)}) collective-permute-start(f32[16,512]{1,0:T(8,128)S(1)} %get-tuple-element.6), channel_id=1, source_target_pairs={{0,128},{8,136},{16,144},{24,152},{32,160},{40,168},{48,176},{56,1... | collective-permute-start | bytes 98312 | tf_op jit(solution)/shard_map/ppermute | solution.py:18
  62.0 7.3 %collective-permute-start.5 = (f32[16,512]{1,0:T(8,128)S(1)}, f32[16,512]{1,0:T(8,128)S(1)}, u32[]{:S(2)}, u32[]{:S(2)}) collective-permute-start(f32[16,512]{1,0:T(8,128)S(1)} %fusion.28), channel_id=1, source_target_pairs={{0,256},{8,264},{16,272},{24,280},{32,288},{40,296},{48,304},{56,3... | collective-permute-start | bytes 98312 | tf_op jit(solution)/shard_map/ppermute | solution.py:18
  69.3 7.6 %copy-start.3 = (f32[512]{0:T(512)S(1)}, f32[512]{0:T(512)}, u32[]{:S(2)}) copy-start(f32[512]{0:T(512)} %param.11) | copy-start | bytes 6148
  76.9 24.9 %copy-start.4 = (f32[512]{0:T(512)S(1)}, f32[512]{0:T(512)}, u32[]{:S(2)}) copy-start(f32[512]{0:T(512)} %param.15) | copy-start | bytes 6148
  77.0 9.0 %collective-permute-start.6 = (bf16[128,512]{0,1:T(8,128)(2,1)S(1)}, bf16[128,512]{0,1:T(8,128)(2,1)S(1)}, u32[]{:S(2)}, u32[]{:S(2)}) collective-permute-start(bf16[128,512]{0,1:T(8,128)(2,1)S(1)} %get-tuple-element.4), channel_id=1, source_target_pairs={{0,8},{8,16},{16,24},{24,32},{32,40},{40,48},{48,56},{56,64},{64,7... | collective-permute-start | bytes 393224 | tf_op jit(solution)/shard_map/ppermute | solution.py:18
  86.3 3.1 %collective-permute-start.8 = (f32[128]{0:T(128)S(1)}, f32[128]{0:T(128)S(1)}, u32[]{:S(2)}, u32[]{:S(2)}) collective-permute-start(f32[128]{0:T(128)S(1)} %get-tuple-element.12), channel_id=1, source_target_pairs={{0,1},{1,0},{2,3},{3,2},{4,5},{5,4},{6,7},{7,6},{8,9},{9,8},{10,11... | collective-permute-start | bytes 1544 | tf_op jit(solution)/shard_map/ppermute | solution.py:12
  89.4 5.5 %collective-permute-start.9 = (f32[128]{0:T(128)S(1)}, f32[128]{0:T(128)S(1)}, u32[]{:S(2)}, u32[]{:S(2)}) collective-permute-start(f32[128]{0:T(128)S(1)} %add.95), channel_id=1, source_target_pairs={{0,2},{1,3},{2,0},{3,1},{4,6},{5,7},{6,4},{7,5},{8,10},{9,11},{10,... | collective-permute-start | bytes 1544 | tf_op jit(solution)/shard_map/ppermute | solution.py:12
  94.8 7.0 %collective-permute-start.10 = (f32[128]{0:T(128)S(1)}, f32[128]{0:T(128)S(1)}, u32[]{:S(2)}, u32[]{:S(2)}) collective-permute-start(f32[128]{0:T(128)S(1)} %add.96), channel_id=1, source_target_pairs={{0,4},{1,5},{2,6},{3,7},{4,0},{5,1},{6,2},{7,3},{8,12},{9,13},{10,... | collective-permute-start | bytes 1544 | tf_op jit(solution)/shard_map/ppermute | solution.py:12

commit v2 on v1

--- a/solution.py
+++ b/solution.py
@@ -6,16 +6,23 @@
 HD = 128
 
 
-def partner_2(value, axis, apart):
-    mask = 2**apart
-    pairs = [(source, source ^ mask) for source in range(lax.axis_size(axis))]
-    return lax.ppermute(value, axis, pairs)
-
-
 def shifted(block, axis, distance):
     devices = range(lax.axis_size(axis))
     route = [(i - distance, i) for i in devices if i - distance in devices]
     return lax.ppermute(block, axis, route)
+
+
+def ramp(rates, sign, length, gain=None):
+    fine_count = 16
+    coarse_count = length // fine_count
+    fine_t = jnp.arange(fine_count, dtype=jnp.float32)
+    coarse_t = jnp.arange(coarse_count, dtype=jnp.float32) * float(fine_count)
+    fine = jnp.exp(sign * rates[:, None, :] * fine_t[None, :, None])
+    coarse = jnp.exp(sign * rates[:, None, :] * coarse_t[None, :, None])
+    if gain is not None:
+        coarse = coarse * gain[:, None, :]
+    table = coarse[:, :, None, :] * fine[:, None, :, :]
+    return table.reshape(rates.shape[0], length, rates.shape[1])
 
 
 def per_device(
@@ -31,8 +38,9 @@
     steps = jnp.arange(row_count, dtype=jnp.float32)
     last = float(row_count - 1)
 
-    tail = jnp.exp(-rates[:, None, :] * (last - steps)[None, :, None])
-    own_state = jnp.sum(tail * signal[None], axis=1)
+    rise = ramp(rates, 1.0, row_count)
+    lifted = rise * signal[None]
+    own_state = jnp.exp(-rates * last) * jnp.sum(lifted, axis=1)
 
     before = jnp.zeros_like(own_state)
     span = 1
@@ -42,8 +50,6 @@
         before = before + jnp.exp(-rates * float(row_count * span)) * got
         span *= 2
 
-    rise = jnp.exp(rates[:, None, :] * steps[None, :, None])
-    lifted = rise * signal[None]
     lifted_hi = lifted.astype(jnp.bfloat16)
     lifted_lo = (lifted - lifted_hi.astype(jnp.float32)).astype(jnp.bfloat16)
     lower = (steps[:, None] >= steps[None, :]).astype(jnp.bfloat16)
@@ -51,9 +57,10 @@
         "ts,rsc->rtc", lower, lifted_hi, preferred_element_type=jnp.float32
     ) + jnp.einsum("ts,rsc->rtc", lower, lifted_lo, preferred_element_type=jnp.float32)
 
-    fall = weight[:, None, :] * jnp.exp(-rates[:, None, :] * steps[None, :, None])
+    fall = ramp(rates, -1.0, row_count, weight)
+    local_part = jnp.sum(fall * prefix, axis=0)
     carried = jnp.exp(rates * last) * before
-    convolved = jnp.sum(fall * (prefix + carried[:, None, :]), axis=0)
+    convolved = local_part + jnp.sum(fall * carried[:, None, :], axis=0)
     conv_out = (convolved + skip_gain[None, :] * signal).astype(jnp.bfloat16)
     gated = (value_rows.astype(jnp.float32) * conv_out.astype(jnp.float32)).astype(jnp.bfloat16)
 
@@ -87,8 +94,8 @@
     attention = mixed_heads.reshape(row_count, heads_here * HD).astype(jnp.bfloat16)
     attention_wide = attention.astype(jnp.float32)
     energy = jnp.sum(attention_wide * attention_wide, axis=1)
-    for bit_index in range(ch_count.bit_length() - 1):
-        energy = energy + partner_2(energy, "ch", bit_index)
+    spread = jnp.broadcast_to(energy[None, :], (ch_count, row_count))
+    energy = jnp.sum(lax.all_to_all(spread, "ch", 0, 0, tiled=True), axis=0)
     mean_square = energy / float(query_rows.shape[1] * ch_count)
     attended = (
         attention_wide * norm_gain[None, :] / jnp.sqrt(mean_square + 1e-06)[:, None]

time: 103 us -> 105 us (1.019)
  other arithmetic: 4.57 us -> 11.4 us
  local copies, waits for them, and re-layouts: 3.16 us -> 9.1 us
  starting transfers between devices: 43 us -> 37.4 us
  matrix products: 12.3 us -> 7.74 us
    ppermute x3 -> x0, starting transfers between devices: 10.5 us -> none  [partner_2(): return lax.ppermute(value, axis, pairs)]
    mul x0 -> x1, local copies, waits for them, and re-layouts: none -> 5.35 us  [ramp(): table = coarse[:, :, None, :] * fine[:, None, :, :]]
    dot_general x1, matrix products: 7.53 us -> 2.67 us  [per_device(): jnp.einsum('ts,rsc->rtc', lower, lifted_hi, preferred_element_type=jnp.fl...]
    all_to_all x0 -> x1, starting transfers between devices: none -> 4.48 us  [per_device(): energy = jnp.sum(lax.all_to_all(spread, 'ch', 0, 0, tiled=True), axis=0)]
    all_to_all x0 -> x1, waiting for transfers between devices: none -> 4.31 us  [per_device(): energy = jnp.sum(lax.all_to_all(spread, 'ch', 0, 0, tiled=True), axis=0)]
    ppermute x3 -> x0, waiting for transfers between devices: 4.05 us -> none  [partner_2(): return lax.ppermute(value, axis, pairs)]
    reduce_sum x1 -> x3, other arithmetic: 2.39 us -> 5.27 us  [the longest x1 2.63 us: per_device(): convolved = local_part + jnp.sum(fall * carried[:, None, :], axis=0)]
    convert_element_type x1, other arithmetic: 0.02 us -> 2.87 us  [per_device(): lifted_lo = (lifted - lifted_hi.astype(jnp.float32)).astype(jnp.bfloat16)]
  transfers between devices with their start and end apart: 11 -> 9, of which waited for: 10 -> 8; matrix products, arithmetic and copies ran while one was open for 7% -> 8% of each run, Pallas kernels for 0% -> 0%
where the time goes in v2:
time: 105 us; the launch traced here: 104 us
  waiting for transfers between devices  37.8 us (36%)
  starting transfers between devices  37.4 us (36%)
  other arithmetic  11.4 us (11%)
  local copies, waits for them, and re-layouts  9.1 us (9%)
  matrix products  7.74 us (7%)
    ppermute x8, waiting for transfers between devices, shifted(): return lax.ppermute(block, axis, route)  33.5 us
    ppermute x8, starting transfers between devices, shifted(): return lax.ppermute(block, axis, route)  32.9 us
    mul x1, local copies, waits for them, and re-layouts, ramp(): table = coarse[:, :, None, :] * fine[:, None, :, :]  5.35 us
    dot_general x1, matrix products, per_device(): jnp.einsum('ts,rsc->rtc', lower, lifted_lo, preferred_element_type=jnp.fl...  4.51 us
    all_to_all x1, starting transfers between devices, per_device(): energy = jnp.sum(lax.all_to_all(spread, 'ch', 0, 0, tiled=True), axis=0)  4.48 us
    all_to_all x1, waiting for transfers between devices, per_device(): energy = jnp.sum(lax.all_to_all(spread, 'ch', 0, 0, tiled=True), axis=0)  4.31 us
    convert_element_type x1, other arithmetic, per_device(): lifted_lo = (lifted - lifted_hi.astype(jnp.float32)).astype(jnp.bfloat16)  2.87 us
    unnamed x20, local copies, waits for them, and re-layouts  2.79 us
  transfers between devices with their start and end apart: 9, of which 8 were waited for; matrix products, arithmetic and copies ran while one was open for 8% of the time, Pallas kernels for 0%

profile of v2, /device:TPU:6, one launch (start us, length us, event | category | flops | bytes accessed | tf_op | source)
XLA Modules:
  0.0 104.4 jit_solution(3397499513082835343)
XLA Ops:
  0.7 1.1 %copy.70 = bf16[128,512]{0,1:T(8,128)(2,1)S(1)} copy(bf16[128,512]{1,0:T(8,128)(2,1)} %param.8) | data formatting | bytes 262144 | tf_op args[0]
  1.9 0.8 multiply_exponential_fusion
  2.7 0.9 multiply_exponential_fusion.2
  3.6 2.6 %multiply_reduce_fusion.1 = (f32[16,512]{1,0:T(8,128)S(1)}, f32[16,8,16,512]{3,2,1,0:T(8,128)}) fusion(f32[8,16,512]{2,1,0:T(8,128)S(1)} %bitcast.71, f32[16,16,512]{2,1,0:T(8,128)S(1)} %multiply_exponential_fusion, f32[16,8,512]{2,1,0:T(8,128)S(1)} %multiply_exponential_fusion.2), kind=kLoop, calls=%fused_computation.4 | loop fusion | flops 3137536 | bytes 5275648 | tf_op jit(solution)/shard_map/reduce_sum | solution.py:43
  6.3 3.8 %collective-permute-start = (f32[16,512]{1,0:T(8,128)S(1)}, f32[16,512]{1,0:T(8,128)S(1)}, u32[]{:S(2)}, u32[]{:S(2)}) collective-permute-start(f32[16,512]{1,0:T(8,128)S(1)} %exponential_multiply_fusion.1), channel_id=1, source_target_pairs={{0,8},{8,16},{16,24},{24,32},{32,40},{40,48},{48,56},{56,64},{64,7... | collective-permute-start | bytes 98312 | tf_op jit(solution)/shard_map/ppermute | solution.py:12
  10.2 3.8 %collective-permute-start.7 = (bf16[128,512]{0,1:T(8,128)(2,1)S(1)}, bf16[128,512]{0,1:T(8,128)(2,1)S(1)}, u32[]{:S(2)}, u32[]{:S(2)}) collective-permute-start(bf16[128,512]{0,1:T(8,128)(2,1)S(1)} %copy.78), channel_id=1, source_target_pairs={{0,8},{8,16},{16,24},{24,32},{32,40},{40,48},{48,56},{56,64},{64,7... | collective-permute-start | bytes 393224 | tf_op jit(solution)/shard_map/ppermute | solution.py:12
  14.1 2.9 %subtract_convert_fusion = (bf16[16,128,512]{2,1,0:T(8,128)(2,1)S(1)}, bf16[16,128,512]{2,1,0:T(8,128)(2,1)S(1)}) fusion(f32[16,8,16,512]{3,2,1,0:T(8,128)} %get-tuple-element.19, f32[128,512]{1,0:T(8,128)S(1)} %copy.71), kind=kLoop, calls=%fused_computation.5 | loop fusion | flops 5242880 | bytes 8650752 | tf_op jit(solution)/shard_map/convert_element_type | solution.py:54
  17.0 2.7 %fusion.16 = f32[16,512,128]{2,1,0:T(8,128)} fusion(bf16[16,128,512]{2,1,0:T(8,128)(2,1)S(1)} %get-tuple-element.15), kind=kOutput, calls=%fused_computation.36 | convolution fusion | flops 268451840 | bytes 6291456 | tf_op jit(solution)/shard_map/ts,rsc->rtc/dot_general | solution.py:56
  19.6 0.2 collective-permute-done
  19.8 6.2 %collective-permute-start.1 = (f32[16,512]{1,0:T(8,128)S(1)}, f32[16,512]{1,0:T(8,128)S(1)}, u32[]{:S(2)}, u32[]{:S(2)}) collective-permute-start(f32[16,512]{1,0:T(8,128)S(1)} %fusion.18), channel_id=1, source_target_pairs={{0,16},{8,24},{16,32},{24,40},{32,48},{40,56},{48,64},{56,72},{64,... | collective-permute-start | bytes 98312 | tf_op jit(solution)/shard_map/ppermute | solution.py:12
  26.1 5.1 %collective-permute-done.1 = f32[16,512]{1,0:T(8,128)S(1)} collective-permute-done((f32[16,512]{1,0:T(8,128)S(1)}, f32[16,512]{1,0:T(8,128)S(1)}, u32[]{:S(2)}, u32[]{:S(2)}) %collective-permute-start.1) | collective-permute-done | bytes 32800 | tf_op jit(solution)/shard_map/ppermute | solution.py:12
  31.2 5.5 %collective-permute-start.2 = (f32[16,512]{1,0:T(8,128)S(1)}, f32[16,512]{1,0:T(8,128)S(1)}, u32[]{:S(2)}, u32[]{:S(2)}) collective-permute-start(f32[16,512]{1,0:T(8,128)S(1)} %fusion.21), channel_id=1, source_target_pairs={{0,32},{8,40},{16,48},{24,56},{32,64},{40,72},{48,80},{56,88},{64,... | collective-permute-start | bytes 98312 | tf_op jit(solution)/shard_map/ppermute | solution.py:12
  36.8 5.4 %collective-permute-done.2 = f32[16,512]{1,0:T(8,128)S(1)} collective-permute-done((f32[16,512]{1,0:T(8,128)S(1)}, f32[16,512]{1,0:T(8,128)S(1)}, u32[]{:S(2)}, u32[]{:S(2)}) %collective-permute-start.2) | collective-permute-done | bytes 32800 | tf_op jit(solution)/shard_map/ppermute | solution.py:12
  42.2 9.0 %collective-permute-start.3 = (f32[16,512]{1,0:T(8,128)S(1)}, f32[16,512]{1,0:T(8,128)S(1)}, u32[]{:S(2)}, u32[]{:S(2)}) collective-permute-start(f32[16,512]{1,0:T(8,128)S(1)} %fusion.19), channel_id=1, source_target_pairs={{0,64},{8,72},{16,80},{24,88},{32,96},{40,104},{48,112},{56,120},{... | collective-permute-start | bytes 98312 | tf_op jit(solution)/shard_map/ppermute | solution.py:12
  51.4 0.8 copy.77
  52.2 5.7 %collective-permute-done.3 = f32[16,512]{1,0:T(8,128)S(1)} collective-permute-done((f32[16,512]{1,0:T(8,128)S(1)}, f32[16,512]{1,0:T(8,128)S(1)}, u32[]{:S(2)}, u32[]{:S(2)}) %collective-permute-start.3) | collective-permute-done | bytes 32800 | tf_op jit(solution)/shard_map/ppermute | solution.py:12
  57.9 1.3 %collective-permute-start.4 = (f32[16,512]{1,0:T(8,128)S(1)}, f32[16,512]{1,0:T(8,128)S(1)}, u32[]{:S(2)}, u32[]{:S(2)}) collective-permute-start(f32[16,512]{1,0:T(8,128)S(1)} %get-tuple-element.12), channel_id=1, source_target_pairs={{0,128},{8,136},{16,144},{24,152},{32,160},{40,168},{48,176},{56,1... | collective-permute-start | bytes 98312 | tf_op jit(solution)/shard_map/ppermute | solution.py:12
  59.2 4.5 %collective-permute-done.4 = f32[16,512]{1,0:T(8,128)S(1)} collective-permute-done((f32[16,512]{1,0:T(8,128)S(1)}, f32[16,512]{1,0:T(8,128)S(1)}, u32[]{:S(2)}, u32[]{:S(2)}) %collective-permute-start.4) | collective-permute-done | bytes 32800 | tf_op jit(solution)/shard_map/ppermute | solution.py:12
  63.7 1.3 %collective-permute-start.5 = (f32[16,512]{1,0:T(8,128)S(1)}, f32[16,512]{1,0:T(8,128)S(1)}, u32[]{:S(2)}, u32[]{:S(2)}) collective-permute-start(f32[16,512]{1,0:T(8,128)S(1)} %fusion.20), channel_id=1, source_target_pairs={{0,256},{8,264},{16,272},{24,280},{32,288},{40,296},{48,304},{56,3... | collective-permute-start | bytes 98312 | tf_op jit(solution)/shard_map/ppermute | solution.py:12
  65.0 0.3 fusion.23
  65.3 5.7 %collective-permute-done.5 = f32[16,512]{1,0:T(8,128)S(1)} collective-permute-done((f32[16,512]{1,0:T(8,128)S(1)}, f32[16,512]{1,0:T(8,128)S(1)}, u32[]{:S(2)}, u32[]{:S(2)}) %collective-permute-start.5) | collective-permute-done | bytes 32800 | tf_op jit(solution)/shard_map/ppermute | solution.py:12
  71.3 2.6 %multiply_reduce_fusion = (f32[8,16,512]{2,1,0:T(8,128)S(1)}, f32[16,8,16,512]{3,2,1,0:T(8,128)}) fusion(f32[16,512]{1,0:T(8,128)S(1)} %get-tuple-element.20, f32[16,16,512]{2,1,0:T(8,128)S(1)} %multiply_exponential_fusion.1, f32[16,8,512]{2,1,0:T(8,128)S(1)} %exponential_multiply_fusion), kind=kLoop, calls=%fused_computation.3 | loop fusion | flops 3080192 | bytes 5275648 | tf_op jit(solution)/shard_map/reduce_sum | solution.py:63
  73.9 5.3 %copy.74 = f32[16,128,512]{1,2,0:T(8,128)} copy(f32[16,128,512]{2,1,0:T(8,128)} %bitcast.68) | data formatting | bytes 8388608 | tf_op jit(solution)/shard_map/mul | solution.py:24
  79.4 4.5 %fusion = f32[128,512]{0,1:T(8,128)S(1)} fusion(f32[16,128,512]{1,2,0:T(8,128)} %copy.74, f32[16,512,128]{2,1,0:T(8,128)} %fusion.16, bf16[16,128,512]{2,1,0:T(8,128)(2,1)S(1)} %get-tuple-element.14), kind=kOutput, calls=%fused_computation.1 | convolution fusion | flops 271532032 | bytes 10747904 | tf_op jit(solution)/shard_map/ts,rsc->rtc/dot_general | solution.py:58
  84.1 1.9 %collective-permute-start.6 = (bf16[128,512]{0,1:T(8,128)(2,1)S(1)}, bf16[128,512]{0,1:T(8,128)(2,1)S(1)}, u32[]{:S(2)}, u32[]{:S(2)}) collective-permute-start(bf16[128,512]{0,1:T(8,128)(2,1)S(1)} %get-tuple-element.10), channel_id=1, source_target_pairs={{0,8},{8,16},{16,24},{24,32},{32,40},{40,48},{48,56},{56,64},{64,7... | collective-permute-start | bytes 393224 | tf_op jit(solution)/shard_map/ppermute | solution.py:12
  86.1 6.9 %collective-permute-done.6 = bf16[128,512]{0,1:T(8,128)(2,1)S(1)} collective-permute-done((bf16[128,512]{0,1:T(8,128)(2,1)S(1)}, bf16[128,512]{0,1:T(8,128)(2,1)S(1)}, u32[]{:S(2)}, u32[]{:S(2)}) %collective-permute-start.6) | collective-permute-done | bytes 131104 | tf_op jit(solution)/shard_map/ppermute | solution.py:12
  93.1 0.3 multiply_reduce_fusion.2
  93.4 0.6 broadcast_in_dim.12
  94.0 4.5 %all-to-all-start = ((f32[8,1,128]{2,1,0:T(1,128)}), f32[8,1,128]{2,1,0:T(1,128)S(1)}, u32[]{:S(2)}, u32[]{:S(2)}) async-start(f32[8,1,128]{2,1,0:T(1,128)} %broadcast_in_dim.12), calls=%async_computation | async-start | bytes 8192 | tf_op jit(solution)/shard_map/all_to_all | solution.py:98
  98.4 0.8 copy.85
  99.3 4.3 %all-to-all-done = f32[8,1,128]{2,1,0:T(1,128)S(1)} async-done(((f32[8,1,128]{2,1,0:T(1,128)}), f32[8,1,128]{2,1,0:T(1,128)S(1)}, u32[]{:S(2)}, u32[]{:S(2)}) %all-to-all-start) | async-done | bytes 4128 | tf_op jit(solution)/shard_map/all_to_all | solution.py:98
  103.7 0.8 divide_convert_fusion
  (40 shorter events, 1.4 us)
Async XLA Ops:
  0.6 64.4 %copy-start = (bf16[128,512]{1,0:T(8,128)(2,1)S(1)}, bf16[128,512]{1,0:T(8,128)(2,1)}, u32[]{:S(2)}) copy-start(bf16[128,512]{1,0:T(8,128)(2,1)} %param.12) | copy-start | bytes 393220
  0.6 5.6 %copy-start.1 = (f32[512,16]{0,1:T(8,128)S(1)}, f32[512,16]{0,1:T(8,128)}, u32[]{:S(2)}) copy-start(f32[512,16]{0,1:T(8,128)} %param.10) | copy-start | bytes 98308
  0.7 9.4 %copy-start.3 = (bf16[128,512]{1,0:T(8,128)(2,1)S(1)}, bf16[128,512]{1,0:T(8,128)(2,1)}, u32[]{:S(2)}) copy-start(bf16[128,512]{1,0:T(8,128)(2,1)} %param.13) | copy-start | bytes 393220
  6.3 13.6 %collective-permute-start = (f32[16,512]{1,0:T(8,128)S(1)}, f32[16,512]{1,0:T(8,128)S(1)}, u32[]{:S(2)}, u32[]{:S(2)}) collective-permute-start(f32[16,512]{1,0:T(8,128)S(1)} %exponential_multiply_fusion.1), channel_id=1, source_target_pairs={{0,8},{8,16},{16,24},{24,32},{32,40},{40,48},{48,56},{56,64},{64,7... | collective-permute-start | bytes 98312 | tf_op jit(solution)/shard_map/ppermute | solution.py:12
  10.2 49.0 %collective-permute-start.7 = (bf16[128,512]{0,1:T(8,128)(2,1)S(1)}, bf16[128,512]{0,1:T(8,128)(2,1)S(1)}, u32[]{:S(2)}, u32[]{:S(2)}) collective-permute-start(bf16[128,512]{0,1:T(8,128)(2,1)S(1)} %copy.78), channel_id=1, source_target_pairs={{0,8},{8,16},{16,24},{24,32},{32,40},{40,48},{48,56},{56,64},{64,7... | collective-permute-start | bytes 393224 | tf_op jit(solution)/shard_map/ppermute | solution.py:12
  16.9 34.5 %copy-start.4 = (bf16[128,512]{1,0:T(8,128)(2,1)S(1)}, bf16[128,512]{1,0:T(8,128)(2,1)}, u32[]{:S(2)}) copy-start(bf16[128,512]{1,0:T(8,128)(2,1)} %param.14) | copy-start | bytes 393220
  16.9 54.1 %copy-start.5 = (f32[512,16]{0,1:T(8,128)S(1)}, f32[512,16]{0,1:T(8,128)}, u32[]{:S(2)}) copy-start(f32[512,16]{0,1:T(8,128)} %param.9) | copy-start | bytes 98308
  19.8 11.4 %collective-permute-start.1 = (f32[16,512]{1,0:T(8,128)S(1)}, f32[16,512]{1,0:T(8,128)S(1)}, u32[]{:S(2)}, u32[]{:S(2)}) collective-permute-start(f32[16,512]{1,0:T(8,128)S(1)} %fusion.18), channel_id=1, source_target_pairs={{0,16},{8,24},{16,32},{24,40},{32,48},{40,56},{48,64},{56,72},{64,... | collective-permute-start | bytes 98312 | tf_op jit(solution)/shard_map/ppermute | solution.py:12
  31.2 11.0 %collective-permute-start.2 = (f32[16,512]{1,0:T(8,128)S(1)}, f32[16,512]{1,0:T(8,128)S(1)}, u32[]{:S(2)}, u32[]{:S(2)}) collective-permute-start(f32[16,512]{1,0:T(8,128)S(1)} %fusion.21), channel_id=1, source_target_pairs={{0,32},{8,40},{16,48},{24,56},{32,64},{40,72},{48,80},{56,88},{64,... | collective-permute-start | bytes 98312 | tf_op jit(solution)/shard_map/ppermute | solution.py:12
  42.2 15.6 %collective-permute-start.3 = (f32[16,512]{1,0:T(8,128)S(1)}, f32[16,512]{1,0:T(8,128)S(1)}, u32[]{:S(2)}, u32[]{:S(2)}) collective-permute-start(f32[16,512]{1,0:T(8,128)S(1)} %fusion.19), channel_id=1, source_target_pairs={{0,64},{8,72},{16,80},{24,88},{32,96},{40,104},{48,112},{56,120},{... | collective-permute-start | bytes 98312 | tf_op jit(solution)/shard_map/ppermute | solution.py:12
  57.9 5.8 %collective-permute-start.4 = (f32[16,512]{1,0:T(8,128)S(1)}, f32[16,512]{1,0:T(8,128)S(1)}, u32[]{:S(2)}, u32[]{:S(2)}) collective-permute-start(f32[16,512]{1,0:T(8,128)S(1)} %get-tuple-element.12), channel_id=1, source_target_pairs={{0,128},{8,136},{16,144},{24,152},{32,160},{40,168},{48,176},{56,1... | collective-permute-start | bytes 98312 | tf_op jit(solution)/shard_map/ppermute | solution.py:12
  63.7 7.3 %collective-permute-start.5 = (f32[16,512]{1,0:T(8,128)S(1)}, f32[16,512]{1,0:T(8,128)S(1)}, u32[]{:S(2)}, u32[]{:S(2)}) collective-permute-start(f32[16,512]{1,0:T(8,128)S(1)} %fusion.20), channel_id=1, source_target_pairs={{0,256},{8,264},{16,272},{24,280},{32,288},{40,296},{48,304},{56,3... | collective-permute-start | bytes 98312 | tf_op jit(solution)/shard_map/ppermute | solution.py:12
  79.4 4.5 %copy-start.2 = (bf16[128,512]{0,1:T(8,128)(2,1)S(1)}, bf16[128,512]{0,1:T(8,128)(2,1)}, u32[]{:S(2)}) copy-start(bf16[128,512]{0,1:T(8,128)(2,1)} %copy.77) | copy-start | bytes 393220
  79.4 4.5 %copy-start.6 = (f32[512]{0:T(512)S(1)}, f32[512]{0:T(512)}, u32[]{:S(2)}) copy-start(f32[512]{0:T(512)} %param.11) | copy-start | bytes 6148
  83.9 19.7 %copy-start.7 = (f32[512]{0:T(512)S(1)}, f32[512]{0:T(512)}, u32[]{:S(2)}) copy-start(f32[512]{0:T(512)} %param.15) | copy-start | bytes 6148
  84.1 9.0 %collective-permute-start.6 = (bf16[128,512]{0,1:T(8,128)(2,1)S(1)}, bf16[128,512]{0,1:T(8,128)(2,1)S(1)}, u32[]{:S(2)}, u32[]{:S(2)}) collective-permute-start(bf16[128,512]{0,1:T(8,128)(2,1)S(1)} %get-tuple-element.10), channel_id=1, source_target_pairs={{0,8},{8,16},{16,24},{24,32},{32,40},{40,48},{48,56},{56,64},{64,7... | collective-permute-start | bytes 393224 | tf_op jit(solution)/shard_map/ppermute | solution.py:12
  94.0 9.7 %all-to-all-start = ((f32[8,1,128]{2,1,0:T(1,128)}), f32[8,1,128]{2,1,0:T(1,128)S(1)}, u32[]{:S(2)}, u32[]{:S(2)}) async-start(f32[8,1,128]{2,1,0:T(1,128)} %broadcast_in_dim.12), calls=%async_computation | async-start | bytes 8192 | tf_op jit(solution)/shard_map/all_to_all | solution.py:98

commit v3 on v2

--- a/solution.py
+++ b/solution.py
@@ -4,6 +4,7 @@
 from jax.sharding import PartitionSpec as P
 
 HD = 128
+TIE_SPAN = 4
 
 
 def shifted(block, axis, distance):
@@ -17,12 +18,12 @@
     coarse_count = length // fine_count
     fine_t = jnp.arange(fine_count, dtype=jnp.float32)
     coarse_t = jnp.arange(coarse_count, dtype=jnp.float32) * float(fine_count)
-    fine = jnp.exp(sign * rates[:, None, :] * fine_t[None, :, None])
-    coarse = jnp.exp(sign * rates[:, None, :] * coarse_t[None, :, None])
+    fine = jnp.exp(sign * fine_t[:, None, None] * rates[None])
+    coarse = jnp.exp(sign * coarse_t[:, None, None] * rates[None])
     if gain is not None:
-        coarse = coarse * gain[:, None, :]
-    table = coarse[:, :, None, :] * fine[:, None, :, :]
-    return table.reshape(rates.shape[0], length, rates.shape[1])
+        coarse = coarse * gain[None]
+    table = coarse[:, None] * fine[None]
+    return table.reshape((length,) + rates.shape)
 
 
 def per_device(
@@ -39,28 +40,31 @@
     last = float(row_count - 1)
 
     rise = ramp(rates, 1.0, row_count)
-    lifted = rise * signal[None]
-    own_state = jnp.exp(-rates * last) * jnp.sum(lifted, axis=1)
+    lifted = rise * signal[:, None, :]
+    own_state = jnp.exp(-rates * last) * jnp.sum(lifted, axis=0)
+
+    flat = lifted.reshape(row_count, -1)
+    flat_hi = flat.astype(jnp.bfloat16)
+    flat_lo = (flat - flat_hi.astype(jnp.float32)).astype(jnp.bfloat16)
+    lower = (steps[:, None] >= steps[None, :]).astype(jnp.bfloat16)
+    prefix = jnp.dot(lower, flat_hi, preferred_element_type=jnp.float32) + jnp.dot(
+        lower, flat_lo, preferred_element_type=jnp.float32
+    )
+    fall = ramp(rates, -1.0, row_count, weight)
+    local_part = jnp.sum(fall * prefix.reshape(lifted.shape), axis=1)
 
     before = jnp.zeros_like(own_state)
     span = 1
     while span < ctx_count:
         sent = own_state + before
         got = shifted(sent, "ctx", span)
+        if span == TIE_SPAN:
+            got, local_part = lax.optimization_barrier((got, local_part))
         before = before + jnp.exp(-rates * float(row_count * span)) * got
         span *= 2
 
-    lifted_hi = lifted.astype(jnp.bfloat16)
-    lifted_lo = (lifted - lifted_hi.astype(jnp.float32)).astype(jnp.bfloat16)
-    lower = (steps[:, None] >= steps[None, :]).astype(jnp.bfloat16)
-    prefix = jnp.einsum(
-        "ts,rsc->rtc", lower, lifted_hi, preferred_element_type=jnp.float32
-    ) + jnp.einsum("ts,rsc->rtc", lower, lifted_lo, preferred_element_type=jnp.float32)
-
-    fall = ramp(rates, -1.0, row_count, weight)
-    local_part = jnp.sum(fall * prefix, axis=0)
     carried = jnp.exp(rates * last) * before
-    convolved = local_part + jnp.sum(fall * carried[:, None, :], axis=0)
+    convolved = local_part + jnp.sum(fall * carried[None], axis=1)
     conv_out = (convolved + skip_gain[None, :] * signal).astype(jnp.bfloat16)
     gated = (value_rows.astype(jnp.float32) * conv_out.astype(jnp.float32)).astype(jnp.bfloat16)
 

time: 105 us -> 106 us (level)
  matrix products: 7.74 us -> 2.02 us
  local copies, waits for them, and re-layouts: 9.1 us -> 14 us
  waiting for transfers between devices: 37.8 us -> 39.2 us
    unnamed x20 -> x18, local copies, waits for them, and re-layouts: 2.79 us -> 12.7 us
    dot_general x2, matrix products: 7.19 us -> 1.47 us  [the longest x1 0.76 us: per_device(): jnp.dot(lower, flat_lo, preferred_element_type=jnp.float32)]
    mul x1, local copies, waits for them, and re-layouts: 5.35 us -> 0.52 us  [per_device(): lifted = rise * signal[:, None, :]]
    mul x3 -> x7, other arithmetic: 0.13 us -> 4.91 us  [the longest x2 3.17 us: ramp(): table = coarse[:, None] * fine[None]]
    reduce_sum x2, other arithmetic: 5.25 us -> 2.55 us  [the longest x1 1.56 us: per_device(): local_part = jnp.sum(fall * prefix.reshape(lifted.shape), axis=1)]
    convert_element_type x1, other arithmetic: 2.87 us -> 0.99 us  [per_device(): signal = conv_input.astype(jnp.float32)]
  transfers between devices with their start and end apart: 9 -> 9, of which waited for: 8 -> 7; matrix products, arithmetic and copies ran while one was open for 8% -> 17% of each run, Pallas kernels for 0% -> 0%
where the time goes in v3:
time: 106 us; the launch traced here: 105 us
  waiting for transfers between devices  39.2 us (37%)
  starting transfers between devices  37.6 us (35%)
  local copies, waits for them, and re-layouts  14 us (13%)
  other arithmetic  11.4 us (11%)
  matrix products  2.02 us (2%)
    ppermute x8, waiting for transfers between devices, shifted(): return lax.ppermute(block, axis, route)  34.1 us
    ppermute x8, starting transfers between devices, shifted(): return lax.ppermute(block, axis, route)  33.1 us
    unnamed x18, local copies, waits for them, and re-layouts  12.7 us
    all_to_all x1, waiting for transfers between devices, per_device(): energy = jnp.sum(lax.all_to_all(spread, 'ch', 0, 0, tiled=True), axis=0)  5.08 us
    all_to_all x1, starting transfers between devices, per_device(): energy = jnp.sum(lax.all_to_all(spread, 'ch', 0, 0, tiled=True), axis=0)  4.47 us
    mul x2, other arithmetic, ramp(): table = coarse[:, None] * fine[None]  3.17 us
  transfers between devices with their start and end apart: 9, of which 7 were waited for; matrix products, arithmetic and copies ran while one was open for 17% of the time, Pallas kernels for 0%

profile of v3, /device:TPU:6, one launch (start us, length us, event | category | flops | bytes accessed | tf_op | source)
XLA Modules:
  0.0 105.2 jit_solution(6449318882277199075)
XLA Ops:
  0.7 1.0 convert_element_type.45
  1.7 0.8 bitcast_multiply_fusion.1
  2.5 1.0 multiply_exponential_fusion
  3.5 0.9 exponential_multiply_fusion
  4.4 2.6 %broadcast_multiply_fusion.1 = (f32[8,16,16,512]{3,2,1,0:T(8,128)}, f32[16,512]{1,0:T(8,128)S(1)}) fusion(f32[16,16,512]{2,1,0:T(8,128)S(1)} %get-tuple-element.15, f32[8,16,512]{2,1,0:T(8,128)S(1)} %get-tuple-element.13, f32[8,16,512]{2,1,0:T(8,128)S(1)} %bitcast.75), kind=kLoop, calls=%fused_computation.7 | loop fusion | flops 3137536 | bytes 5275648 | tf_op jit(solution)/shard_map/mul | solution.py:25
  7.1 3.8 %collective-permute-start = (f32[16,512]{1,0:T(8,128)S(1)}, f32[16,512]{1,0:T(8,128)S(1)}, u32[]{:S(2)}, u32[]{:S(2)}) collective-permute-start(f32[16,512]{1,0:T(8,128)S(1)} %fusion.18), channel_id=1, source_target_pairs={{0,8},{8,16},{16,24},{24,32},{32,40},{40,48},{48,56},{56,64},{64,7... | collective-permute-start | bytes 98312 | tf_op jit(solution)/shard_map/ppermute | solution.py:13
  11.0 3.8 %collective-permute-start.7 = (bf16[128,512]{0,1:T(8,128)(2,1)S(1)}, bf16[128,512]{0,1:T(8,128)(2,1)S(1)}, u32[]{:S(2)}, u32[]{:S(2)}) collective-permute-start(bf16[128,512]{0,1:T(8,128)(2,1)S(1)} %copy.29), channel_id=1, source_target_pairs={{0,8},{8,16},{16,24},{24,32},{32,40},{40,48},{48,56},{56,64},{64,7... | collective-permute-start | bytes 393224 | tf_op jit(solution)/shard_map/ppermute | solution.py:13
  14.9 5.6 %copy.39 = f32[16,8,16,512]{3,1,2,0:T(8,128)S(1)} copy(f32[16,8,16,512]{3,2,1,0:T(8,128)} %bitcast.70) | data formatting | bytes 8388608
  20.5 0.5 mul.311
  21.1 3.4 %copy.40 = f32[16,8,16,512]{3,1,2,0:T(8,128)S(1)} copy(f32[16,8,16,512]{3,2,1,0:T(8,128)S(1)} %bitcast.71) | data formatting | bytes 8388608
  24.5 0.7 fusion.2
  25.2 0.8 convolution_add_fusion
  26.0 3.4 %copy.41 = f32[16,8,16,512]{3,2,1,0:T(8,128)S(1)} copy(f32[16,8,16,512]{3,1,2,0:T(8,128)S(1)} %bitcast.72) | data formatting | bytes 8388608
  30.0 1.6 %fusion = f32[128,512]{1,0:T(8,128)S(1)} fusion(f32[16,8,16,512]{3,2,1,0:T(8,128)S(1)} %copy.41, f32[8,16,16,512]{3,2,1,0:T(8,128)S(1)} %broadcast_multiply_fusion), kind=kLoop, calls=%fused_computation.2 | loop fusion | flops 2031616 | bytes 8650752 | tf_op jit(solution)/shard_map/reduce_sum | solution.py:54
  31.6 6.4 %collective-permute-start.1 = (f32[16,512]{1,0:T(8,128)S(1)}, f32[16,512]{1,0:T(8,128)S(1)}, u32[]{:S(2)}, u32[]{:S(2)}) collective-permute-start(f32[16,512]{1,0:T(8,128)S(1)} %fusion.24), channel_id=1, source_target_pairs={{0,16},{8,24},{16,32},{24,40},{32,48},{40,56},{48,64},{56,72},{64,... | collective-permute-start | bytes 98312 | tf_op jit(solution)/shard_map/ppermute | solution.py:13
  38.0 5.1 %collective-permute-done.1 = f32[16,512]{1,0:T(8,128)S(1)} collective-permute-done((f32[16,512]{1,0:T(8,128)S(1)}, f32[16,512]{1,0:T(8,128)S(1)}, u32[]{:S(2)}, u32[]{:S(2)}) %collective-permute-start.1) | collective-permute-done | bytes 32800 | tf_op jit(solution)/shard_map/ppermute | solution.py:13
  43.1 5.5 %collective-permute-start.2 = (f32[16,512]{1,0:T(8,128)S(1)}, f32[16,512]{1,0:T(8,128)S(1)}, u32[]{:S(2)}, u32[]{:S(2)}) collective-permute-start(f32[16,512]{1,0:T(8,128)S(1)} %fusion.27), channel_id=1, source_target_pairs={{0,32},{8,40},{16,48},{24,56},{32,64},{40,72},{48,80},{56,88},{64,... | collective-permute-start | bytes 98312 | tf_op jit(solution)/shard_map/ppermute | solution.py:13
  48.7 5.4 %collective-permute-done.2 = f32[16,512]{1,0:T(8,128)S(1)} collective-permute-done((f32[16,512]{1,0:T(8,128)S(1)}, f32[16,512]{1,0:T(8,128)S(1)}, u32[]{:S(2)}, u32[]{:S(2)}) %collective-permute-start.2) | collective-permute-done | bytes 32800 | tf_op jit(solution)/shard_map/ppermute | solution.py:13
  54.1 9.0 %collective-permute-start.3 = (f32[16,512]{1,0:T(8,128)S(1)}, f32[16,512]{1,0:T(8,128)S(1)}, u32[]{:S(2)}, u32[]{:S(2)}) collective-permute-start(f32[16,512]{1,0:T(8,128)S(1)} %fusion.25), channel_id=1, source_target_pairs={{0,64},{8,72},{16,80},{24,88},{32,96},{40,104},{48,112},{56,120},{... | collective-permute-start | bytes 98312 | tf_op jit(solution)/shard_map/ppermute | solution.py:13
  63.3 6.4 %collective-permute-done.3 = f32[16,512]{1,0:T(8,128)S(1)} collective-permute-done((f32[16,512]{1,0:T(8,128)S(1)}, f32[16,512]{1,0:T(8,128)S(1)}, u32[]{:S(2)}, u32[]{:S(2)}) %collective-permute-start.3) | collective-permute-done | bytes 32800 | tf_op jit(solution)/shard_map/ppermute | solution.py:13
  69.8 1.3 %collective-permute-start.4 = (f32[16,512]{1,0:T(8,128)S(1)}, f32[16,512]{1,0:T(8,128)S(1)}, u32[]{:S(2)}, u32[]{:S(2)}) collective-permute-start(f32[16,512]{1,0:T(8,128)S(1)} %get-tuple-element.8), channel_id=1, source_target_pairs={{0,128},{8,136},{16,144},{24,152},{32,160},{40,168},{48,176},{56,1... | collective-permute-start | bytes 98312 | tf_op jit(solution)/shard_map/ppermute | solution.py:13
  71.1 4.5 %collective-permute-done.4 = f32[16,512]{1,0:T(8,128)S(1)} collective-permute-done((f32[16,512]{1,0:T(8,128)S(1)}, f32[16,512]{1,0:T(8,128)S(1)}, u32[]{:S(2)}, u32[]{:S(2)}) %collective-permute-start.4) | collective-permute-done | bytes 32800 | tf_op jit(solution)/shard_map/ppermute | solution.py:13
  75.6 1.3 %collective-permute-start.5 = (f32[16,512]{1,0:T(8,128)S(1)}, f32[16,512]{1,0:T(8,128)S(1)}, u32[]{:S(2)}, u32[]{:S(2)}) collective-permute-start(f32[16,512]{1,0:T(8,128)S(1)} %fusion.26), channel_id=1, source_target_pairs={{0,256},{8,264},{16,272},{24,280},{32,288},{40,296},{48,304},{56,3... | collective-permute-start | bytes 98312 | tf_op jit(solution)/shard_map/ppermute | solution.py:13
  77.2 5.7 %collective-permute-done.5 = f32[16,512]{1,0:T(8,128)S(1)} collective-permute-done((f32[16,512]{1,0:T(8,128)S(1)}, f32[16,512]{1,0:T(8,128)S(1)}, u32[]{:S(2)}, u32[]{:S(2)}) %collective-permute-start.5) | collective-permute-done | bytes 32800 | tf_op jit(solution)/shard_map/ppermute | solution.py:13
  83.0 1.0 multiply_reduce_fusion
  84.0 0.7 multiply_convert_fusion.3
  84.7 1.9 %collective-permute-start.6 = (bf16[128,512]{1,0:T(8,128)(2,1)S(1)}, bf16[128,512]{1,0:T(8,128)(2,1)S(1)}, u32[]{:S(2)}, u32[]{:S(2)}) collective-permute-start(bf16[128,512]{1,0:T(8,128)(2,1)S(1)} %get-tuple-element.6), channel_id=1, source_target_pairs={{0,8},{8,16},{16,24},{24,32},{32,40},{40,48},{48,56},{56,64},{64,7... | collective-permute-start | bytes 393224 | tf_op jit(solution)/shard_map/ppermute | solution.py:13
  86.7 6.9 %collective-permute-done.6 = bf16[128,512]{1,0:T(8,128)(2,1)S(1)} collective-permute-done((bf16[128,512]{1,0:T(8,128)(2,1)S(1)}, bf16[128,512]{1,0:T(8,128)(2,1)S(1)}, u32[]{:S(2)}, u32[]{:S(2)}) %collective-permute-start.6) | collective-permute-done | bytes 131104 | tf_op jit(solution)/shard_map/ppermute | solution.py:13
  94.1 0.6 broadcast_in_dim.12
  94.7 4.5 %all-to-all-start = ((f32[8,1,128]{2,1,0:T(1,128)}), f32[8,1,128]{2,1,0:T(1,128)S(1)}, u32[]{:S(2)}, u32[]{:S(2)}) async-start(f32[8,1,128]{2,1,0:T(1,128)} %broadcast_in_dim.12), calls=%async_computation | async-start | bytes 8192 | tf_op jit(solution)/shard_map/all_to_all | solution.py:102
  99.3 5.1 %all-to-all-done = f32[8,1,128]{2,1,0:T(1,128)S(1)} async-done(((f32[8,1,128]{2,1,0:T(1,128)}), f32[8,1,128]{2,1,0:T(1,128)S(1)}, u32[]{:S(2)}, u32[]{:S(2)}) %all-to-all-start) | async-done | bytes 4128 | tf_op jit(solution)/shard_map/all_to_all | solution.py:102
  104.4 0.8 divide_convert_fusion
  (39 shorter events, 2.0 us)
Async XLA Ops:
  0.6 76.3 %copy-start = (bf16[128,512]{1,0:T(8,128)(2,1)S(1)}, bf16[128,512]{1,0:T(8,128)(2,1)}, u32[]{:S(2)}) copy-start(bf16[128,512]{1,0:T(8,128)(2,1)} %param.12) | copy-start | bytes 393220
  0.6 6.4 %copy-start.1 = (f32[512,16]{0,1:T(8,128)S(1)}, f32[512,16]{0,1:T(8,128)}, u32[]{:S(2)}) copy-start(f32[512,16]{0,1:T(8,128)} %param.10) | copy-start | bytes 98308
  0.7 10.2 %copy-start.3 = (bf16[128,512]{1,0:T(8,128)(2,1)S(1)}, bf16[128,512]{1,0:T(8,128)(2,1)}, u32[]{:S(2)}) copy-start(bf16[128,512]{1,0:T(8,128)(2,1)} %param.13) | copy-start | bytes 393220
  7.1 24.5 %collective-permute-start = (f32[16,512]{1,0:T(8,128)S(1)}, f32[16,512]{1,0:T(8,128)S(1)}, u32[]{:S(2)}, u32[]{:S(2)}) collective-permute-start(f32[16,512]{1,0:T(8,128)S(1)} %fusion.18), channel_id=1, source_target_pairs={{0,8},{8,16},{16,24},{24,32},{32,40},{40,48},{48,56},{56,64},{64,7... | collective-permute-start | bytes 98312 | tf_op jit(solution)/shard_map/ppermute | solution.py:13
  11.0 60.1 %collective-permute-start.7 = (bf16[128,512]{0,1:T(8,128)(2,1)S(1)}, bf16[128,512]{0,1:T(8,128)(2,1)S(1)}, u32[]{:S(2)}, u32[]{:S(2)}) collective-permute-start(bf16[128,512]{0,1:T(8,128)(2,1)S(1)} %copy.29), channel_id=1, source_target_pairs={{0,8},{8,16},{16,24},{24,32},{32,40},{40,48},{48,56},{56,64},{64,7... | collective-permute-start | bytes 393224 | tf_op jit(solution)/shard_map/ppermute | solution.py:13
  14.9 5.7 %copy-start.2 = (bf16[128,512]{1,0:T(8,128)(2,1)S(1)}, bf16[128,512]{1,0:T(8,128)(2,1)}, u32[]{:S(2)}) copy-start(bf16[128,512]{1,0:T(8,128)(2,1)} %param.8) | copy-start | bytes 393220
  29.9 54.0 %copy-start.4 = (bf16[128,512]{1,0:T(8,128)(2,1)S(1)}, bf16[128,512]{1,0:T(8,128)(2,1)}, u32[]{:S(2)}) copy-start(bf16[128,512]{1,0:T(8,128)(2,1)} %param.14) | copy-start | bytes 393220
  29.9 54.0 %copy-start.5 = (f32[512]{0:T(512)S(1)}, f32[512]{0:T(512)}, u32[]{:S(2)}) copy-start(f32[512]{0:T(512)} %param.11) | copy-start | bytes 6148
  31.6 72.9 %copy-start.6 = (f32[512]{0:T(512)S(1)}, f32[512]{0:T(512)}, u32[]{:S(2)}) copy-start(f32[512]{0:T(512)} %param.15) | copy-start | bytes 6148
  31.6 11.5 %collective-permute-start.1 = (f32[16,512]{1,0:T(8,128)S(1)}, f32[16,512]{1,0:T(8,128)S(1)}, u32[]{:S(2)}, u32[]{:S(2)}) collective-permute-start(f32[16,512]{1,0:T(8,128)S(1)} %fusion.24), channel_id=1, source_target_pairs={{0,16},{8,24},{16,32},{24,40},{32,48},{40,56},{48,64},{56,72},{64,... | collective-permute-start | bytes 98312 | tf_op jit(solution)/shard_map/ppermute | solution.py:13
  43.1 11.0 %collective-permute-start.2 = (f32[16,512]{1,0:T(8,128)S(1)}, f32[16,512]{1,0:T(8,128)S(1)}, u32[]{:S(2)}, u32[]{:S(2)}) collective-permute-start(f32[16,512]{1,0:T(8,128)S(1)} %fusion.27), channel_id=1, source_target_pairs={{0,32},{8,40},{16,48},{24,56},{32,64},{40,72},{48,80},{56,88},{64,... | collective-permute-start | bytes 98312 | tf_op jit(solution)/shard_map/ppermute | solution.py:13
  54.1 15.6 %collective-permute-start.3 = (f32[16,512]{1,0:T(8,128)S(1)}, f32[16,512]{1,0:T(8,128)S(1)}, u32[]{:S(2)}, u32[]{:S(2)}) collective-permute-start(f32[16,512]{1,0:T(8,128)S(1)} %fusion.25), channel_id=1, source_target_pairs={{0,64},{8,72},{16,80},{24,88},{32,96},{40,104},{48,112},{56,120},{... | collective-permute-start | bytes 98312 | tf_op jit(solution)/shard_map/ppermute | solution.py:13
  69.8 5.8 %collective-permute-start.4 = (f32[16,512]{1,0:T(8,128)S(1)}, f32[16,512]{1,0:T(8,128)S(1)}, u32[]{:S(2)}, u32[]{:S(2)}) collective-permute-start(f32[16,512]{1,0:T(8,128)S(1)} %get-tuple-element.8), channel_id=1, source_target_pairs={{0,128},{8,136},{16,144},{24,152},{32,160},{40,168},{48,176},{56,1... | collective-permute-start | bytes 98312 | tf_op jit(solution)/shard_map/ppermute | solution.py:13
  75.6 7.3 %collective-permute-start.5 = (f32[16,512]{1,0:T(8,128)S(1)}, f32[16,512]{1,0:T(8,128)S(1)}, u32[]{:S(2)}, u32[]{:S(2)}) collective-permute-start(f32[16,512]{1,0:T(8,128)S(1)} %fusion.26), channel_id=1, source_target_pairs={{0,256},{8,264},{16,272},{24,280},{32,288},{40,296},{48,304},{56,3... | collective-permute-start | bytes 98312 | tf_op jit(solution)/shard_map/ppermute | solution.py:13
  84.7 9.0 %collective-permute-start.6 = (bf16[128,512]{1,0:T(8,128)(2,1)S(1)}, bf16[128,512]{1,0:T(8,128)(2,1)S(1)}, u32[]{:S(2)}, u32[]{:S(2)}) collective-permute-start(bf16[128,512]{1,0:T(8,128)(2,1)S(1)} %get-tuple-element.6), channel_id=1, source_target_pairs={{0,8},{8,16},{16,24},{24,32},{32,40},{40,48},{48,56},{56,64},{64,7... | collective-permute-start | bytes 393224 | tf_op jit(solution)/shard_map/ppermute | solution.py:13
  94.7 9.7 %all-to-all-start = ((f32[8,1,128]{2,1,0:T(1,128)}), f32[8,1,128]{2,1,0:T(1,128)S(1)}, u32[]{:S(2)}, u32[]{:S(2)}) async-start(f32[8,1,128]{2,1,0:T(1,128)} %broadcast_in_dim.12), calls=%async_computation | async-start | bytes 8192 | tf_op jit(solution)/shard_map/all_to_all | solution.py:102

commit v4 on v3

--- a/solution.py
+++ b/solution.py
@@ -13,19 +13,6 @@
     return lax.ppermute(block, axis, route)
 
 
-def ramp(rates, sign, length, gain=None):
-    fine_count = 16
-    coarse_count = length // fine_count
-    fine_t = jnp.arange(fine_count, dtype=jnp.float32)
-    coarse_t = jnp.arange(coarse_count, dtype=jnp.float32) * float(fine_count)
-    fine = jnp.exp(sign * fine_t[:, None, None] * rates[None])
-    coarse = jnp.exp(sign * coarse_t[:, None, None] * rates[None])
-    if gain is not None:
-        coarse = coarse * gain[None]
-    table = coarse[:, None] * fine[None]
-    return table.reshape((length,) + rates.shape)
-
-
 def per_device(
     conv_input, residues, decay_rates, skip_gain, query_rows, key_rows, value_rows, norm_gain
 ):
@@ -39,19 +26,25 @@
     steps = jnp.arange(row_count, dtype=jnp.float32)
     last = float(row_count - 1)
 
-    rise = ramp(rates, 1.0, row_count)
-    lifted = rise * signal[:, None, :]
-    own_state = jnp.exp(-rates * last) * jnp.sum(lifted, axis=0)
+    fine_count = 16
+    fine_t = jnp.arange(fine_count, dtype=jnp.float32)
+    coarse_t = jnp.arange(row_count // fine_count, dtype=jnp.float32) * float(fine_count)
+    fine = jnp.exp(fine_t[:, None, None] * rates[None])
+    coarse = jnp.exp(coarse_t[:, None, None] * rates[None])
+    split_rows = signal.reshape(row_count // fine_count, fine_count, 1, chan_count)
+    inner = jnp.sum(fine[None] * split_rows, axis=1)
+    own_state = jnp.exp(-rates * last) * jnp.sum(coarse * inner, axis=0)
 
-    flat = lifted.reshape(row_count, -1)
-    flat_hi = flat.astype(jnp.bfloat16)
-    flat_lo = (flat - flat_hi.astype(jnp.float32)).astype(jnp.bfloat16)
+    lifted = jnp.exp(steps[:, None, None] * rates[None]) * signal[:, None, :]
+    lifted_top = lax.reduce_precision(lifted, exponent_bits=8, mantissa_bits=7)
+    lifted_hi = lifted_top.astype(jnp.bfloat16)
+    lifted_lo = (lifted - lifted_top).astype(jnp.bfloat16)
     lower = (steps[:, None] >= steps[None, :]).astype(jnp.bfloat16)
-    prefix = jnp.dot(lower, flat_hi, preferred_element_type=jnp.float32) + jnp.dot(
-        lower, flat_lo, preferred_element_type=jnp.float32
-    )
-    fall = ramp(rates, -1.0, row_count, weight)
-    local_part = jnp.sum(fall * prefix.reshape(lifted.shape), axis=1)
+    prefix = jnp.einsum(
+        "ts,src->trc", lower, lifted_hi, preferred_element_type=jnp.float32
+    ) + jnp.einsum("ts,src->trc", lower, lifted_lo, preferred_element_type=jnp.float32)
+    fall = weight[None] * jnp.exp(-steps[:, None, None] * rates[None])
+    local_part = jnp.sum(fall * prefix, axis=1)
 
     before = jnp.zeros_like(own_state)
     span = 1

time: 106 us -> 91.4 us (0.86)
  local copies, waits for them, and re-layouts: 14 us -> 1.93 us
  other arithmetic: 11.4 us -> 6.66 us
  matrix products: 2.02 us -> 4.37 us
    unnamed x18 -> x13, local copies, waits for them, and re-layouts: 12.7 us -> 1.06 us
    mul x6 -> x1, other arithmetic: 4.1 us -> 0.01 us  [per_device(): jnp.arange(row_count // fine_count, dtype=jnp.float32) * float(fine_count)]
    dot_general x2, matrix products: 1.47 us -> 3.82 us  [the longest x1 2.25 us: per_device(): jnp.einsum('ts,src->trc', lower, lifted_lo, preferred_element_type=jnp.fl...]
  transfers between devices with their start and end apart: 9 -> 9, of which waited for: 7 -> 8; matrix products, arithmetic and copies ran while one was open for 17% -> 6% of each run, Pallas kernels for 0% -> 0%
where the time goes in v4:
time: 91.4 us; the launch traced here: 90.8 us
  waiting for transfers between devices  40.1 us (44%)
  starting transfers between devices  36.8 us (40%)
  other arithmetic  6.66 us (7%)
  matrix products  4.37 us (5%)
  local copies, waits for them, and re-layouts  1.93 us (2%)
  between operations  0.93 us (1%)
    ppermute x8, waiting for transfers between devices, shifted(): return lax.ppermute(block, axis, route)  35 us
    ppermute x8, starting transfers between devices, shifted(): return lax.ppermute(block, axis, route)  32.3 us
    all_to_all x1, waiting for transfers between devices, per_device(): energy = jnp.sum(lax.all_to_all(spread, 'ch', 0, 0, tiled=True), axis=0)  5.08 us
    all_to_all x1, starting transfers between devices, per_device(): energy = jnp.sum(lax.all_to_all(spread, 'ch', 0, 0, tiled=True), axis=0)  4.47 us
    dot_general x1, matrix products, per_device(): jnp.einsum('ts,src->trc', lower, lifted_lo, preferred_element_type=jnp.fl...  2.25 us
  transfers between devices with their start and end apart: 9, of which 8 were waited for; matrix products, arithmetic and copies ran while one was open for 6% of the time, Pallas kernels for 0%

profile of v4, /device:TPU:6, one launch (start us, length us, event | category | flops | bytes accessed | tf_op | source)
XLA Modules:
  0.0 90.8 jit_solution(17673976896824242831)
XLA Ops:
  0.7 0.9 multiply_exponential_fusion
  1.6 0.9 %convert_element_type.42 = f32[128,512]{1,0:T(8,128)S(1)} convert(bf16[128,512]{1,0:T(8,128)(2,1)} %param.8) | non-fusion elementwise | flops 65536 | bytes 393216 | tf_op jit(solution)/shard_map/convert_element_type | solution.py:23
  2.5 0.3 multiply_reduce_fusion.2
  2.8 0.9 multiply_reduce_fusion.4
  3.7 0.8 bitcast_multiply_fusion
  4.5 3.8 %collective-permute-start = (f32[16,512]{1,0:T(8,128)S(1)}, f32[16,512]{1,0:T(8,128)S(1)}, u32[]{:S(2)}, u32[]{:S(2)}) collective-permute-start(f32[16,512]{1,0:T(8,128)S(1)} %get-tuple-element.11), channel_id=1, source_target_pairs={{0,8},{8,16},{16,24},{24,32},{32,40},{40,48},{48,56},{56,64},{64,7... | collective-permute-start | bytes 98312 | tf_op jit(solution)/shard_map/ppermute | solution.py:13
  8.3 1.0 %copy.29 = bf16[128,512]{0,1:T(8,128)(2,1)S(1)} copy(bf16[128,512]{1,0:T(8,128)(2,1)} %param.13) | data formatting | bytes 262144 | tf_op args[5]
  9.4 3.8 %collective-permute-start.7 = (bf16[128,512]{0,1:T(8,128)(2,1)S(1)}, bf16[128,512]{0,1:T(8,128)(2,1)S(1)}, u32[]{:S(2)}, u32[]{:S(2)}) collective-permute-start(bf16[128,512]{0,1:T(8,128)(2,1)S(1)} %copy.29), channel_id=1, source_target_pairs={{0,8},{8,16},{16,24},{24,32},{32,40},{40,48},{48,56},{56,64},{64,7... | collective-permute-start | bytes 393224 | tf_op jit(solution)/shard_map/ppermute | solution.py:13
  13.2 1.6 %fusion.2 = f32[128,16,512]{2,0,1:T(8,128)S(1)} fusion(f32[128,512]{1,0:T(8,128)S(1)} %convert_element_type.42, f32[16,512]{1,0:T(8,128)} %bitcast.53), kind=kOutput, calls=%fused_computation.8 | convolution fusion | flops 272646144 | bytes 4489216 | tf_op jit(solution)/shard_map/ts,src->trc/dot_general | solution.py:43
  14.8 2.3 %multiply_reduce_fusion.1 = f32[128,512]{1,0:T(8,128)S(1)} fusion(f32[128,16,512]{2,0,1:T(8,128)S(1)} %fusion.2, f32[128,512]{1,0:T(8,128)S(1)} %convert_element_type.42, f32[16,512]{1,0:T(8,128)S(1)} %bitcast.54, f32[128]{0:T(128)S(1)} %iota_negate_fusion, f32[16,512]{1,0:T(8,128)S(1)} %get-tuple-element.10), kind=kOutput, calls=%fused_computation.4 | convolution fusion | flops 278872064 | bytes 4784640 | tf_op jit(solution)/shard_map/ts,src->trc/dot_general | solution.py:45
  17.1 1.0 %collective-permute-done = f32[16,512]{1,0:T(8,128)S(1)} collective-permute-done((f32[16,512]{1,0:T(8,128)S(1)}, f32[16,512]{1,0:T(8,128)S(1)}, u32[]{:S(2)}, u32[]{:S(2)}) %collective-permute-start) | collective-permute-done | bytes 32800 | tf_op jit(solution)/shard_map/ppermute | solution.py:13
  18.1 5.6 %collective-permute-start.1 = (f32[16,512]{1,0:T(8,128)S(1)}, f32[16,512]{1,0:T(8,128)S(1)}, u32[]{:S(2)}, u32[]{:S(2)}) collective-permute-start(f32[16,512]{1,0:T(8,128)S(1)} %fusion.29), channel_id=1, source_target_pairs={{0,16},{8,24},{16,32},{24,40},{32,48},{40,56},{48,64},{56,72},{64,... | collective-permute-start | bytes 98312 | tf_op jit(solution)/shard_map/ppermute | solution.py:13
  23.7 5.1 %collective-permute-done.1 = f32[16,512]{1,0:T(8,128)S(1)} collective-permute-done((f32[16,512]{1,0:T(8,128)S(1)}, f32[16,512]{1,0:T(8,128)S(1)}, u32[]{:S(2)}, u32[]{:S(2)}) %collective-permute-start.1) | collective-permute-done | bytes 32800 | tf_op jit(solution)/shard_map/ppermute | solution.py:13
  28.8 5.5 %collective-permute-start.2 = (f32[16,512]{1,0:T(8,128)S(1)}, f32[16,512]{1,0:T(8,128)S(1)}, u32[]{:S(2)}, u32[]{:S(2)}) collective-permute-start(f32[16,512]{1,0:T(8,128)S(1)} %fusion.32), channel_id=1, source_target_pairs={{0,32},{8,40},{16,48},{24,56},{32,64},{40,72},{48,80},{56,88},{64,... | collective-permute-start | bytes 98312 | tf_op jit(solution)/shard_map/ppermute | solution.py:13
  34.4 5.4 %collective-permute-done.2 = f32[16,512]{1,0:T(8,128)S(1)} collective-permute-done((f32[16,512]{1,0:T(8,128)S(1)}, f32[16,512]{1,0:T(8,128)S(1)}, u32[]{:S(2)}, u32[]{:S(2)}) %collective-permute-start.2) | collective-permute-done | bytes 32800 | tf_op jit(solution)/shard_map/ppermute | solution.py:13
  39.8 9.0 %collective-permute-start.3 = (f32[16,512]{1,0:T(8,128)S(1)}, f32[16,512]{1,0:T(8,128)S(1)}, u32[]{:S(2)}, u32[]{:S(2)}) collective-permute-start(f32[16,512]{1,0:T(8,128)S(1)} %fusion.30), channel_id=1, source_target_pairs={{0,64},{8,72},{16,80},{24,88},{32,96},{40,104},{48,112},{56,120},{... | collective-permute-start | bytes 98312 | tf_op jit(solution)/shard_map/ppermute | solution.py:13
  48.9 0.1 fusion.18
  49.0 6.4 %collective-permute-done.3 = f32[16,512]{1,0:T(8,128)S(1)} collective-permute-done((f32[16,512]{1,0:T(8,128)S(1)}, f32[16,512]{1,0:T(8,128)S(1)}, u32[]{:S(2)}, u32[]{:S(2)}) %collective-permute-start.3) | collective-permute-done | bytes 32800 | tf_op jit(solution)/shard_map/ppermute | solution.py:13
  55.5 1.3 %collective-permute-start.4 = (f32[16,512]{1,0:T(8,128)S(1)}, f32[16,512]{1,0:T(8,128)S(1)}, u32[]{:S(2)}, u32[]{:S(2)}) collective-permute-start(f32[16,512]{1,0:T(8,128)S(1)} %get-tuple-element.8), channel_id=1, source_target_pairs={{0,128},{8,136},{16,144},{24,152},{32,160},{40,168},{48,176},{56,1... | collective-permute-start | bytes 98312 | tf_op jit(solution)/shard_map/ppermute | solution.py:13
  56.8 4.5 %collective-permute-done.4 = f32[16,512]{1,0:T(8,128)S(1)} collective-permute-done((f32[16,512]{1,0:T(8,128)S(1)}, f32[16,512]{1,0:T(8,128)S(1)}, u32[]{:S(2)}, u32[]{:S(2)}) %collective-permute-start.4) | collective-permute-done | bytes 32800 | tf_op jit(solution)/shard_map/ppermute | solution.py:13
  61.3 1.3 %collective-permute-start.5 = (f32[16,512]{1,0:T(8,128)S(1)}, f32[16,512]{1,0:T(8,128)S(1)}, u32[]{:S(2)}, u32[]{:S(2)}) collective-permute-start(f32[16,512]{1,0:T(8,128)S(1)} %fusion.31), channel_id=1, source_target_pairs={{0,256},{8,264},{16,272},{24,280},{32,288},{40,296},{48,304},{56,3... | collective-permute-start | bytes 98312 | tf_op jit(solution)/shard_map/ppermute | solution.py:13
  62.6 0.3 fusion.34
  62.9 5.7 %collective-permute-done.5 = f32[16,512]{1,0:T(8,128)S(1)} collective-permute-done((f32[16,512]{1,0:T(8,128)S(1)}, f32[16,512]{1,0:T(8,128)S(1)}, u32[]{:S(2)}, u32[]{:S(2)}) %collective-permute-start.5) | collective-permute-done | bytes 32800 | tf_op jit(solution)/shard_map/ppermute | solution.py:13
  68.7 0.9 multiply_reduce_fusion
  69.6 0.7 multiply_convert_fusion
  70.3 1.9 %collective-permute-start.6 = (bf16[128,512]{1,0:T(8,128)(2,1)S(1)}, bf16[128,512]{1,0:T(8,128)(2,1)S(1)}, u32[]{:S(2)}, u32[]{:S(2)}) collective-permute-start(bf16[128,512]{1,0:T(8,128)(2,1)S(1)} %get-tuple-element.6), channel_id=1, source_target_pairs={{0,8},{8,16},{16,24},{24,32},{32,40},{40,48},{48,56},{56,64},{64,7... | collective-permute-start | bytes 393224 | tf_op jit(solution)/shard_map/ppermute | solution.py:13
  72.3 6.9 %collective-permute-done.6 = bf16[128,512]{1,0:T(8,128)(2,1)S(1)} collective-permute-done((bf16[128,512]{1,0:T(8,128)(2,1)S(1)}, bf16[128,512]{1,0:T(8,128)(2,1)S(1)}, u32[]{:S(2)}, u32[]{:S(2)}) %collective-permute-start.6) | collective-permute-done | bytes 131104 | tf_op jit(solution)/shard_map/ppermute | solution.py:13
  79.4 0.3 multiply_reduce_fusion.3
  79.7 0.6 broadcast_in_dim.12
  80.3 4.5 %all-to-all-start = ((f32[8,1,128]{2,1,0:T(1,128)}), f32[8,1,128]{2,1,0:T(1,128)S(1)}, u32[]{:S(2)}, u32[]{:S(2)}) async-start(f32[8,1,128]{2,1,0:T(1,128)} %broadcast_in_dim.12), calls=%async_computation | async-start | bytes 8192 | tf_op jit(solution)/shard_map/all_to_all | solution.py:95
  84.9 5.1 %all-to-all-done = f32[8,1,128]{2,1,0:T(1,128)S(1)} async-done(((f32[8,1,128]{2,1,0:T(1,128)}), f32[8,1,128]{2,1,0:T(1,128)S(1)}, u32[]{:S(2)}, u32[]{:S(2)}) %all-to-all-start) | async-done | bytes 4128 | tf_op jit(solution)/shard_map/all_to_all | solution.py:95
  90.0 0.8 divide_convert_fusion
  (30 shorter events, 0.6 us)
Async XLA Ops:
  0.6 62.0 %copy-start = (bf16[128,512]{1,0:T(8,128)(2,1)S(1)}, bf16[128,512]{1,0:T(8,128)(2,1)}, u32[]{:S(2)}) copy-start(bf16[128,512]{1,0:T(8,128)(2,1)} %param.12) | copy-start | bytes 393220
  0.6 14.2 %copy-start.1 = (f32[512,16]{0,1:T(8,128)S(1)}, f32[512,16]{0,1:T(8,128)}, u32[]{:S(2)}) copy-start(f32[512,16]{0,1:T(8,128)} %param.10) | copy-start | bytes 98308
  4.5 13.6 %collective-permute-start = (f32[16,512]{1,0:T(8,128)S(1)}, f32[16,512]{1,0:T(8,128)S(1)}, u32[]{:S(2)}, u32[]{:S(2)}) collective-permute-start(f32[16,512]{1,0:T(8,128)S(1)} %get-tuple-element.11), channel_id=1, source_target_pairs={{0,8},{8,16},{16,24},{24,32},{32,40},{40,48},{48,56},{56,64},{64,7... | collective-permute-start | bytes 98312 | tf_op jit(solution)/shard_map/ppermute | solution.py:13
  9.4 47.4 %collective-permute-start.7 = (bf16[128,512]{0,1:T(8,128)(2,1)S(1)}, bf16[128,512]{0,1:T(8,128)(2,1)S(1)}, u32[]{:S(2)}, u32[]{:S(2)}) collective-permute-start(bf16[128,512]{0,1:T(8,128)(2,1)S(1)} %copy.29), channel_id=1, source_target_pairs={{0,8},{8,16},{16,24},{24,32},{32,40},{40,48},{48,56},{56,64},{64,7... | collective-permute-start | bytes 393224 | tf_op jit(solution)/shard_map/ppermute | solution.py:13
  17.1 52.5 %copy-start.2 = (bf16[128,512]{1,0:T(8,128)(2,1)S(1)}, bf16[128,512]{1,0:T(8,128)(2,1)}, u32[]{:S(2)}) copy-start(bf16[128,512]{1,0:T(8,128)(2,1)} %param.8) | copy-start | bytes 393220
  17.1 52.5 %copy-start.3 = (bf16[128,512]{1,0:T(8,128)(2,1)S(1)}, bf16[128,512]{1,0:T(8,128)(2,1)}, u32[]{:S(2)}) copy-start(bf16[128,512]{1,0:T(8,128)(2,1)} %param.14) | copy-start | bytes 393220
  17.1 52.5 %copy-start.4 = (f32[512]{0:T(512)S(1)}, f32[512]{0:T(512)}, u32[]{:S(2)}) copy-start(f32[512]{0:T(512)} %param.11) | copy-start | bytes 6148
  18.1 10.7 %collective-permute-start.1 = (f32[16,512]{1,0:T(8,128)S(1)}, f32[16,512]{1,0:T(8,128)S(1)}, u32[]{:S(2)}, u32[]{:S(2)}) collective-permute-start(f32[16,512]{1,0:T(8,128)S(1)} %fusion.29), channel_id=1, source_target_pairs={{0,16},{8,24},{16,32},{24,40},{32,48},{40,56},{48,64},{56,72},{64,... | collective-permute-start | bytes 98312 | tf_op jit(solution)/shard_map/ppermute | solution.py:13
  28.8 11.0 %collective-permute-start.2 = (f32[16,512]{1,0:T(8,128)S(1)}, f32[16,512]{1,0:T(8,128)S(1)}, u32[]{:S(2)}, u32[]{:S(2)}) collective-permute-start(f32[16,512]{1,0:T(8,128)S(1)} %fusion.32), channel_id=1, source_target_pairs={{0,32},{8,40},{16,48},{24,56},{32,64},{40,72},{48,80},{56,88},{64,... | collective-permute-start | bytes 98312 | tf_op jit(solution)/shard_map/ppermute | solution.py:13
  39.8 15.6 %collective-permute-start.3 = (f32[16,512]{1,0:T(8,128)S(1)}, f32[16,512]{1,0:T(8,128)S(1)}, u32[]{:S(2)}, u32[]{:S(2)}) collective-permute-start(f32[16,512]{1,0:T(8,128)S(1)} %fusion.30), channel_id=1, source_target_pairs={{0,64},{8,72},{16,80},{24,88},{32,96},{40,104},{48,112},{56,120},{... | collective-permute-start | bytes 98312 | tf_op jit(solution)/shard_map/ppermute | solution.py:13
  55.5 34.5 %copy-start.5 = (f32[512]{0:T(512)S(1)}, f32[512]{0:T(512)}, u32[]{:S(2)}) copy-start(f32[512]{0:T(512)} %param.15) | copy-start | bytes 6148
  55.5 5.8 %collective-permute-start.4 = (f32[16,512]{1,0:T(8,128)S(1)}, f32[16,512]{1,0:T(8,128)S(1)}, u32[]{:S(2)}, u32[]{:S(2)}) collective-permute-start(f32[16,512]{1,0:T(8,128)S(1)} %get-tuple-element.8), channel_id=1, source_target_pairs={{0,128},{8,136},{16,144},{24,152},{32,160},{40,168},{48,176},{56,1... | collective-permute-start | bytes 98312 | tf_op jit(solution)/shard_map/ppermute | solution.py:13
  61.3 7.3 %collective-permute-start.5 = (f32[16,512]{1,0:T(8,128)S(1)}, f32[16,512]{1,0:T(8,128)S(1)}, u32[]{:S(2)}, u32[]{:S(2)}) collective-permute-start(f32[16,512]{1,0:T(8,128)S(1)} %fusion.31), channel_id=1, source_target_pairs={{0,256},{8,264},{16,272},{24,280},{32,288},{40,296},{48,304},{56,3... | collective-permute-start | bytes 98312 | tf_op jit(solution)/shard_map/ppermute | solution.py:13
  70.3 9.0 %collective-permute-start.6 = (bf16[128,512]{1,0:T(8,128)(2,1)S(1)}, bf16[128,512]{1,0:T(8,128)(2,1)S(1)}, u32[]{:S(2)}, u32[]{:S(2)}) collective-permute-start(bf16[128,512]{1,0:T(8,128)(2,1)S(1)} %get-tuple-element.6), channel_id=1, source_target_pairs={{0,8},{8,16},{16,24},{24,32},{32,40},{40,48},{48,56},{56,64},{64,7... | collective-permute-start | bytes 393224 | tf_op jit(solution)/shard_map/ppermute | solution.py:13
  80.3 9.7 %all-to-all-start = ((f32[8,1,128]{2,1,0:T(1,128)}), f32[8,1,128]{2,1,0:T(1,128)S(1)}, u32[]{:S(2)}, u32[]{:S(2)}) async-start(f32[8,1,128]{2,1,0:T(1,128)} %broadcast_in_dim.12), calls=%async_computation | async-start | bytes 8192 | tf_op jit(solution)/shard_map/all_to_all | solution.py:95

commit v5 on v4

--- a/solution.py
+++ b/solution.py
@@ -13,19 +13,9 @@
     return lax.ppermute(block, axis, route)
 
 
-def per_device(
-    conv_input, residues, decay_rates, skip_gain, query_rows, key_rows, value_rows, norm_gain
-):
-    ctx_count = lax.axis_size("ctx")
-    ch_count = lax.axis_size("ch")
-    position = lax.axis_index("ctx")
-    row_count, chan_count = conv_input.shape
-    signal = conv_input.astype(jnp.float32)
-    rates = jnp.transpose(decay_rates)
-    weight = jnp.transpose(residues) * jnp.sqrt(-jnp.expm1(-rates) * (1.0 + jnp.exp(-rates)))
-    steps = jnp.arange(row_count, dtype=jnp.float32)
+def block_terms(signal, rates, weight, steps):
+    row_count, chan_count = signal.shape
     last = float(row_count - 1)
-
     fine_count = 16
     fine_t = jnp.arange(fine_count, dtype=jnp.float32)
     coarse_t = jnp.arange(row_count // fine_count, dtype=jnp.float32) * float(fine_count)
@@ -46,24 +36,54 @@
     fall = weight[None] * jnp.exp(-steps[:, None, None] * rates[None])
     local_part = jnp.sum(fall * prefix, axis=1)
 
-    before = jnp.zeros_like(own_state)
+    return own_state, fall, local_part
+
+
+def per_device(
+    conv_input, residues, decay_rates, skip_gain, query_rows, key_rows, value_rows, norm_gain
+):
+    ctx_count = lax.axis_size("ctx")
+    ch_count = lax.axis_size("ch")
+    position = lax.axis_index("ctx")
+    row_count, chan_count = conv_input.shape
+    signal = conv_input.astype(jnp.float32)
+    rates = jnp.transpose(decay_rates)
+    weight = jnp.transpose(residues) * jnp.sqrt(-jnp.expm1(-rates) * (1.0 + jnp.exp(-rates)))
+    steps = jnp.arange(row_count, dtype=jnp.float32)
+    last = float(row_count - 1)
+
+    previous_signal = shifted(conv_input, "ctx", 1).astype(jnp.float32)
+    previous_state, _, previous_local = block_terms(previous_signal, rates, weight, steps)
+    own_state, fall, local_part = block_terms(signal, rates, weight, steps)
+    lookback = shifted(jnp.stack([key_rows, value_rows]), "ctx", 1)
+    previous_keys = lookback[0]
+
+    before_previous = jnp.zeros_like(previous_state)
     span = 1
     while span < ctx_count:
-        sent = own_state + before
+        sent = previous_state + before_previous
         got = shifted(sent, "ctx", span)
         if span == TIE_SPAN:
             got, local_part = lax.optimization_barrier((got, local_part))
-        before = before + jnp.exp(-rates * float(row_count * span)) * got
+        if span == 2 * TIE_SPAN:
+            got, previous_local = lax.optimization_barrier((got, previous_local))
+        before_previous = before_previous + jnp.exp(-rates * float(row_count * span)) * got
         span *= 2
+    before = jnp.exp(-rates * float(row_count)) * (previous_state + before_previous)
 
     carried = jnp.exp(rates * last) * before
     convolved = local_part + jnp.sum(fall * carried[None], axis=1)
     conv_out = (convolved + skip_gain[None, :] * signal).astype(jnp.bfloat16)
     gated = (value_rows.astype(jnp.float32) * conv_out.astype(jnp.float32)).astype(jnp.bfloat16)
 
+    carried_previous = jnp.exp(rates * last) * before_previous
+    convolved_previous = previous_local + jnp.sum(fall * carried_previous[None], axis=1)
+    conv_previous = (convolved_previous + skip_gain[None, :] * previous_signal).astype(jnp.bfloat16)
+    previous_gated = (
+        lookback[1].astype(jnp.float32) * conv_previous.astype(jnp.float32)
+    ).astype(jnp.bfloat16)
+
     heads_here = query_rows.shape[1] // HD
-    previous_keys = shifted(key_rows, "ctx", 1)
-    previous_gated = shifted(gated, "ctx", 1)
     key_window = jnp.concatenate([previous_keys, key_rows], axis=0).reshape(
         2 * row_count, heads_here, HD
     )

time: 91.4 us -> 88 us (0.963)
  waiting for transfers between devices: 40.1 us -> 31.3 us
  matrix products: 4.37 us -> 11.6 us
  starting transfers between devices: 36.8 us -> 35.7 us
    ppermute x8, waiting for transfers between devices: 35 us -> 26.2 us  [shifted(): return lax.ppermute(block, axis, route)]
    dot_general x2 -> x4, matrix products: 3.82 us -> 11.1 us  [the longest x2 5.68 us: block_terms(): jnp.einsum('ts,src->trc', lower, lifted_lo, preferred_element_type=jnp.fl...]
    ppermute x8, starting transfers between devices: 32.3 us -> 31.2 us  [shifted(): return lax.ppermute(block, axis, route)]
    another operation x0 -> x1, other arithmetic: none -> 1 us  [per_device(): lookback = shifted(jnp.stack([key_rows, value_rows]), 'ctx', 1)]
  transfers between devices with their start and end apart: 9 -> 9, of which waited for: 8 -> 8; matrix products, arithmetic and copies ran while one was open for 6% -> 18% of each run, Pallas kernels for 0% -> 0%
where the time goes in v5:
time: 88 us; the launch traced here: 87.5 us
  starting transfers between devices  35.7 us (41%)
  waiting for transfers between devices  31.3 us (36%)
  matrix products  11.6 us (13%)
  other arithmetic  6.44 us (7%)
  local copies, waits for them, and re-layouts  1.43 us (2%)
  between operations  0.99 us (1%)
    ppermute x8, starting transfers between devices, shifted(): return lax.ppermute(block, axis, route)  31.2 us
    ppermute x8, waiting for transfers between devices, shifted(): return lax.ppermute(block, axis, route)  26.2 us
    dot_general x2, matrix products, block_terms(): jnp.einsum('ts,src->trc', lower, lifted_lo, preferred_element_type=jnp.fl...  5.68 us
    dot_general x2, matrix products, block_terms(): jnp.einsum('ts,src->trc', lower, lifted_hi, preferred_element_type=jnp.fl...  5.46 us
    all_to_all x1, waiting for transfers between devices, per_device(): energy = jnp.sum(lax.all_to_all(spread, 'ch', 0, 0, tiled=True), axis=0)  5.08 us
    all_to_all x1, starting transfers between devices, per_device(): energy = jnp.sum(lax.all_to_all(spread, 'ch', 0, 0, tiled=True), axis=0)  4.47 us
  transfers between devices with their start and end apart: 9, of which 8 were waited for; matrix products, arithmetic and copies ran while one was open for 18% of the time, Pallas kernels for 0%

profile of v5, /device:TPU:6, one launch (start us, length us, event | category | flops | bytes accessed | tf_op | source)
XLA Modules:
  0.0 87.5 jit_solution(7620466068812226027)
XLA Ops:
  0.7 4.0 %collective-permute-start = (bf16[128,512]{1,0:T(8,128)(2,1)}, bf16[128,512]{1,0:T(8,128)(2,1)S(1)}, u32[]{:S(2)}, u32[]{:S(2)}) collective-permute-start(bf16[128,512]{1,0:T(8,128)(2,1)} %param.8), channel_id=1, source_target_pairs={{0,8},{8,16},{16,24},{24,32},{32,40},{40,48},{48,56},{56,64},{64,7... | collective-permute-start | bytes 393224 | tf_op jit(solution)/shard_map/ppermute | solution.py:13
  4.6 1.0 %pad_maximum_fusion = bf16[2,128,512]{2,1,0:T(8,128)(2,1)S(1)} fusion(bf16[1,128,512]{2,1,0:T(8,128)(2,1)} %bitcast.68, bf16[1,128,512]{2,1,0:T(8,128)(2,1)} %bitcast.71), kind=kLoop, calls=%fused_computation.36 | loop fusion | flops 131072 | bytes 524288 | tf_op jit(solution)/shard_map/stack | solution.py:58
  5.6 3.8 %collective-permute-start.7 = (bf16[2,128,512]{2,1,0:T(8,128)(2,1)S(1)}, bf16[2,128,512]{2,1,0:T(8,128)(2,1)S(1)}, u32[]{:S(2)}, u32[]{:S(2)}) collective-permute-start(bf16[2,128,512]{2,1,0:T(8,128)(2,1)S(1)} %pad_maximum_fusion), channel_id=1, source_target_pairs={{0,8},{8,16},{16,24},{24,32},{32,40},{40,48},{48,56},{56,64},{64,7... | collective-permute-start | bytes 786440 | tf_op jit(solution)/shard_map/ppermute | solution.py:13
  9.5 0.9 %convert_element_type.68 = f32[128,512]{1,0:T(8,128)S(1)} convert(bf16[128,512]{1,0:T(8,128)(2,1)} %param.8) | non-fusion elementwise | flops 65536 | bytes 393216 | tf_op jit(solution)/shard_map/convert_element_type | solution.py:49
  10.4 0.8 multiply_exponential_fusion.1
  11.3 3.5 %fusion.7 = f32[128,16,512]{2,0,1:T(8,128)} fusion(f32[128,512]{1,0:T(8,128)S(1)} %convert_element_type.68, f32[16,512]{1,0:T(8,128)} %bitcast.61), kind=kOutput, calls=%fused_computation.16 | convolution fusion | flops 272646144 | bytes 4489216 | tf_op jit(solution)/shard_map/ts,src->trc/dot_general | solution.py:33
  14.9 1.3 %collective-permute-done = bf16[128,512]{1,0:T(8,128)(2,1)S(1)} collective-permute-done((bf16[128,512]{1,0:T(8,128)(2,1)}, bf16[128,512]{1,0:T(8,128)(2,1)S(1)}, u32[]{:S(2)}, u32[]{:S(2)}) %collective-permute-start) | collective-permute-done | bytes 131104 | tf_op jit(solution)/shard_map/ppermute | solution.py:13
  16.3 0.3 multiply_reduce_fusion.4
  16.8 2.5 %collective-permute-start.1 = (f32[16,512]{1,0:T(8,128)S(1)}, f32[16,512]{1,0:T(8,128)S(1)}, u32[]{:S(2)}, u32[]{:S(2)}) collective-permute-start(f32[16,512]{1,0:T(8,128)S(1)} %get-tuple-element.23), channel_id=1, source_target_pairs={{0,8},{8,16},{16,24},{24,32},{32,40},{40,48},{48,56},{56,64},{64,7... | collective-permute-start | bytes 98312 | tf_op jit(solution)/shard_map/ppermute | solution.py:13
  19.4 0.1 copy.49
  19.6 5.6 %collective-permute-done.1 = f32[16,512]{1,0:T(8,128)S(1)} collective-permute-done((f32[16,512]{1,0:T(8,128)S(1)}, f32[16,512]{1,0:T(8,128)S(1)}, u32[]{:S(2)}, u32[]{:S(2)}) %collective-permute-start.1) | collective-permute-done | bytes 32800 | tf_op jit(solution)/shard_map/ppermute | solution.py:13
  25.2 2.5 %collective-permute-start.2 = (f32[16,512]{1,0:T(8,128)S(1)}, f32[16,512]{1,0:T(8,128)S(1)}, u32[]{:S(2)}, u32[]{:S(2)}) collective-permute-start(f32[16,512]{1,0:T(8,128)S(1)} %fusion.39), channel_id=1, source_target_pairs={{0,16},{8,24},{16,32},{24,40},{32,48},{40,56},{48,64},{56,72},{64,... | collective-permute-start | bytes 98312 | tf_op jit(solution)/shard_map/ppermute | solution.py:13
  27.7 4.3 %multiply_reduce_fusion.3 = f32[128,512]{1,0:T(8,128)S(1)} fusion(f32[128,16,512]{2,0,1:T(8,128)} %fusion.7, f32[128,512]{1,0:T(8,128)S(1)} %convert_element_type.68, f32[16,512]{1,0:T(8,128)S(1)} %bitcast.63, f32[128]{0:T(128)S(1)} %iota_negate_fusion, f32[16,512]{1,0:T(8,128)S(1)} %get-tuple-element.22), kind=kOutput, calls=%fused_computation.9 | convolution fusion | flops 278872064 | bytes 4784640 | tf_op jit(solution)/shard_map/ts,src->trc/dot_general | solution.py:35
  32.0 2.2 %collective-permute-done.2 = f32[16,512]{1,0:T(8,128)S(1)} collective-permute-done((f32[16,512]{1,0:T(8,128)S(1)}, f32[16,512]{1,0:T(8,128)S(1)}, u32[]{:S(2)}, u32[]{:S(2)}) %collective-permute-start.2) | collective-permute-done | bytes 32800 | tf_op jit(solution)/shard_map/ppermute | solution.py:13
  34.3 6.9 %collective-permute-start.3 = (f32[16,512]{1,0:T(8,128)S(1)}, f32[16,512]{1,0:T(8,128)S(1)}, u32[]{:S(2)}, u32[]{:S(2)}) collective-permute-start(f32[16,512]{1,0:T(8,128)S(1)} %get-tuple-element.18), channel_id=1, source_target_pairs={{0,32},{8,40},{16,48},{24,56},{32,64},{40,72},{48,80},{56,88},{64,... | collective-permute-start | bytes 98312 | tf_op jit(solution)/shard_map/ppermute | solution.py:13
  41.2 1.3 %fusion.4 = f32[128,16,512]{2,0,1:T(8,128)S(1)} fusion(f32[128,512]{1,0:T(8,128)S(1)} %convert_element_type.67, f32[16,512]{1,0:T(8,128)S(1)} %bitcast.64), kind=kOutput, calls=%fused_computation.15 | convolution fusion | flops 273694720 | bytes 4489216 | tf_op jit(solution)/shard_map/ts,src->trc/dot_general | solution.py:35
  42.5 2.6 %collective-permute-done.3 = f32[16,512]{1,0:T(8,128)S(1)} collective-permute-done((f32[16,512]{1,0:T(8,128)S(1)}, f32[16,512]{1,0:T(8,128)S(1)}, u32[]{:S(2)}, u32[]{:S(2)}) %collective-permute-start.3) | collective-permute-done | bytes 32800 | tf_op jit(solution)/shard_map/ppermute | solution.py:13
  45.1 9.0 %collective-permute-start.4 = (f32[16,512]{1,0:T(8,128)S(1)}, f32[16,512]{1,0:T(8,128)S(1)}, u32[]{:S(2)}, u32[]{:S(2)}) collective-permute-start(f32[16,512]{1,0:T(8,128)S(1)} %fusion.40), channel_id=1, source_target_pairs={{0,64},{8,72},{16,80},{24,88},{32,96},{40,104},{48,112},{56,120},{... | collective-permute-start | bytes 98312 | tf_op jit(solution)/shard_map/ppermute | solution.py:13
  54.1 2.0 %multiply_reduce_fusion.2 = f32[128,512]{1,0:T(8,128)S(1)} fusion(f32[128,16,512]{2,0,1:T(8,128)S(1)} %fusion.4, f32[128,512]{1,0:T(8,128)S(1)} %convert_element_type.67, f32[16,512]{1,0:T(8,128)S(1)} %bitcast.65, f32[128]{0:T(128)S(1)} %iota_negate_fusion, f32[16,512]{1,0:T(8,128)S(1)} %get-tuple-element.22), kind=kOutput, calls=%fused_computation.8 | convolution fusion | flops 277823488 | bytes 4784640 | tf_op jit(solution)/shard_map/ts,src->trc/dot_general | solution.py:33
  56.1 4.6 %collective-permute-done.4 = f32[16,512]{1,0:T(8,128)S(1)} collective-permute-done((f32[16,512]{1,0:T(8,128)S(1)}, f32[16,512]{1,0:T(8,128)S(1)}, u32[]{:S(2)}, u32[]{:S(2)}) %collective-permute-start.4) | collective-permute-done | bytes 32800 | tf_op jit(solution)/shard_map/ppermute | solution.py:13
  60.7 1.3 %collective-permute-start.5 = (f32[16,512]{1,0:T(8,128)S(1)}, f32[16,512]{1,0:T(8,128)S(1)}, u32[]{:S(2)}, u32[]{:S(2)}) collective-permute-start(f32[16,512]{1,0:T(8,128)S(1)} %fusion.42), channel_id=1, source_target_pairs={{0,128},{8,136},{16,144},{24,152},{32,160},{40,168},{48,176},{56,1... | collective-permute-start | bytes 98312 | tf_op jit(solution)/shard_map/ppermute | solution.py:13
  62.4 0.2 fusion.45
  62.6 3.9 %collective-permute-done.5 = f32[16,512]{1,0:T(8,128)S(1)} collective-permute-done((f32[16,512]{1,0:T(8,128)S(1)}, f32[16,512]{1,0:T(8,128)S(1)}, u32[]{:S(2)}, u32[]{:S(2)}) %collective-permute-start.5) | collective-permute-done | bytes 32800 | tf_op jit(solution)/shard_map/ppermute | solution.py:13
  66.6 1.3 %collective-permute-start.6 = (f32[16,512]{1,0:T(8,128)S(1)}, f32[16,512]{1,0:T(8,128)S(1)}, u32[]{:S(2)}, u32[]{:S(2)}) collective-permute-start(f32[16,512]{1,0:T(8,128)S(1)} %get-tuple-element.16), channel_id=1, source_target_pairs={{0,256},{8,264},{16,272},{24,280},{32,288},{40,296},{48,304},{56,3... | collective-permute-start | bytes 98312 | tf_op jit(solution)/shard_map/ppermute | solution.py:13
  68.0 5.9 %collective-permute-done.6 = f32[16,512]{1,0:T(8,128)S(1)} collective-permute-done((f32[16,512]{1,0:T(8,128)S(1)}, f32[16,512]{1,0:T(8,128)S(1)}, u32[]{:S(2)}, u32[]{:S(2)}) %collective-permute-start.6) | collective-permute-done | bytes 32800 | tf_op jit(solution)/shard_map/ppermute | solution.py:13
  73.9 1.2 %multiply_reduce_fusion = (f32[128,512]{1,0:T(8,128)S(1)}, f32[128,512]{1,0:T(8,128)S(1)}) fusion(f32[16,512]{1,0:T(8,128)S(1)} %get-tuple-element.21, f32[16,512]{1,0:T(8,128)S(1)} %bitcast.66, f32[128]{0:T(128)S(1)} %iota_negate_fusion, f32[16,512]{1,0:T(8,128)S(1)} %get-tuple-element.22, f32[16,512]{1,0:T(8,128)S(1)} %get-tuple-element.20), kind=kLoop, calls=%fused_computation.6 | loop fusion | flops 6160384 | bytes 655872 | tf_op jit(solution)/shard_map/reduce_sum | solution.py:80
  75.2 0.8 multiply_convert_fusion
  76.2 0.3 multiply_reduce_fusion.5
  76.4 0.6 broadcast_in_dim.12
  77.0 4.5 %all-to-all-start = ((f32[8,1,128]{2,1,0:T(1,128)}), f32[8,1,128]{2,1,0:T(1,128)S(1)}, u32[]{:S(2)}, u32[]{:S(2)}) async-start(f32[8,1,128]{2,1,0:T(1,128)} %broadcast_in_dim.12), calls=%async_computation | async-start | bytes 8192 | tf_op jit(solution)/shard_map/all_to_all | solution.py:115
  81.6 5.1 %all-to-all-done = f32[8,1,128]{2,1,0:T(1,128)S(1)} async-done(((f32[8,1,128]{2,1,0:T(1,128)}), f32[8,1,128]{2,1,0:T(1,128)S(1)}, u32[]{:S(2)}, u32[]{:S(2)}) %all-to-all-start) | async-done | bytes 4128 | tf_op jit(solution)/shard_map/all_to_all | solution.py:115
  86.7 0.8 divide_convert_fusion
  (41 shorter events, 1.3 us)
Async XLA Ops:
  0.6 61.7 %copy-start = (bf16[128,512]{1,0:T(8,128)(2,1)S(1)}, bf16[128,512]{1,0:T(8,128)(2,1)}, u32[]{:S(2)}) copy-start(bf16[128,512]{1,0:T(8,128)(2,1)} %param.12) | copy-start | bytes 393220
  0.6 18.7 %copy-start.4 = (bf16[128,512]{1,0:T(8,128)(2,1)S(1)}, bf16[128,512]{1,0:T(8,128)(2,1)}, u32[]{:S(2)}) copy-start(bf16[128,512]{1,0:T(8,128)(2,1)} %param.13) | copy-start | bytes 393220
  0.7 15.9 %copy-start.1 = (f32[512,16]{0,1:T(8,128)S(1)}, f32[512,16]{0,1:T(8,128)}, u32[]{:S(2)}) copy-start(f32[512,16]{0,1:T(8,128)} %param.10) | copy-start | bytes 98308
  0.7 16.1 %copy-start.5 = (f32[512,16]{0,1:T(8,128)S(1)}, f32[512,16]{0,1:T(8,128)}, u32[]{:S(2)}) copy-start(f32[512,16]{0,1:T(8,128)} %param.9) | copy-start | bytes 98308
  0.7 15.6 %collective-permute-start = (bf16[128,512]{1,0:T(8,128)(2,1)}, bf16[128,512]{1,0:T(8,128)(2,1)S(1)}, u32[]{:S(2)}, u32[]{:S(2)}) collective-permute-start(bf16[128,512]{1,0:T(8,128)(2,1)} %param.8), channel_id=1, source_target_pairs={{0,8},{8,16},{16,24},{24,32},{32,40},{40,48},{48,56},{56,64},{64,7... | collective-permute-start | bytes 393224 | tf_op jit(solution)/shard_map/ppermute | solution.py:13
  5.6 56.4 %collective-permute-start.7 = (bf16[2,128,512]{2,1,0:T(8,128)(2,1)S(1)}, bf16[2,128,512]{2,1,0:T(8,128)(2,1)S(1)}, u32[]{:S(2)}, u32[]{:S(2)}) collective-permute-start(bf16[2,128,512]{2,1,0:T(8,128)(2,1)S(1)} %pad_maximum_fusion), channel_id=1, source_target_pairs={{0,8},{8,16},{16,24},{24,32},{32,40},{40,48},{48,56},{56,64},{64,7... | collective-permute-start | bytes 786440 | tf_op jit(solution)/shard_map/ppermute | solution.py:13
  16.8 8.4 %collective-permute-start.1 = (f32[16,512]{1,0:T(8,128)S(1)}, f32[16,512]{1,0:T(8,128)S(1)}, u32[]{:S(2)}, u32[]{:S(2)}) collective-permute-start(f32[16,512]{1,0:T(8,128)S(1)} %get-tuple-element.23), channel_id=1, source_target_pairs={{0,8},{8,16},{16,24},{24,32},{32,40},{40,48},{48,56},{56,64},{64,7... | collective-permute-start | bytes 98312 | tf_op jit(solution)/shard_map/ppermute | solution.py:13
  25.2 9.1 %collective-permute-start.2 = (f32[16,512]{1,0:T(8,128)S(1)}, f32[16,512]{1,0:T(8,128)S(1)}, u32[]{:S(2)}, u32[]{:S(2)}) collective-permute-start(f32[16,512]{1,0:T(8,128)S(1)} %fusion.39), channel_id=1, source_target_pairs={{0,16},{8,24},{16,32},{24,40},{32,48},{40,56},{48,64},{56,72},{64,... | collective-permute-start | bytes 98312 | tf_op jit(solution)/shard_map/ppermute | solution.py:13
  34.3 10.8 %collective-permute-start.3 = (f32[16,512]{1,0:T(8,128)S(1)}, f32[16,512]{1,0:T(8,128)S(1)}, u32[]{:S(2)}, u32[]{:S(2)}) collective-permute-start(f32[16,512]{1,0:T(8,128)S(1)} %get-tuple-element.18), channel_id=1, source_target_pairs={{0,32},{8,40},{16,48},{24,56},{32,64},{40,72},{48,80},{56,88},{64,... | collective-permute-start | bytes 98312 | tf_op jit(solution)/shard_map/ppermute | solution.py:13
  45.1 15.6 %collective-permute-start.4 = (f32[16,512]{1,0:T(8,128)S(1)}, f32[16,512]{1,0:T(8,128)S(1)}, u32[]{:S(2)}, u32[]{:S(2)}) collective-permute-start(f32[16,512]{1,0:T(8,128)S(1)} %fusion.40), channel_id=1, source_target_pairs={{0,64},{8,72},{16,80},{24,88},{32,96},{40,104},{48,112},{56,120},{... | collective-permute-start | bytes 98312 | tf_op jit(solution)/shard_map/ppermute | solution.py:13
  56.1 19.0 %copy-start.2 = (bf16[128,512]{1,0:T(8,128)(2,1)S(1)}, bf16[128,512]{1,0:T(8,128)(2,1)}, u32[]{:S(2)}) copy-start(bf16[128,512]{1,0:T(8,128)(2,1)} %param.8) | copy-start | bytes 393220
  56.1 19.0 %copy-start.3 = (bf16[128,512]{1,0:T(8,128)(2,1)S(1)}, bf16[128,512]{1,0:T(8,128)(2,1)}, u32[]{:S(2)}) copy-start(bf16[128,512]{1,0:T(8,128)(2,1)} %param.14) | copy-start | bytes 393220
  56.1 19.0 %copy-start.6 = (f32[512]{0:T(512)S(1)}, f32[512]{0:T(512)}, u32[]{:S(2)}) copy-start(f32[512]{0:T(512)} %param.11) | copy-start | bytes 6148
  60.7 5.8 %collective-permute-start.5 = (f32[16,512]{1,0:T(8,128)S(1)}, f32[16,512]{1,0:T(8,128)S(1)}, u32[]{:S(2)}, u32[]{:S(2)}) collective-permute-start(f32[16,512]{1,0:T(8,128)S(1)} %fusion.42), channel_id=1, source_target_pairs={{0,128},{8,136},{16,144},{24,152},{32,160},{40,168},{48,176},{56,1... | collective-permute-start | bytes 98312 | tf_op jit(solution)/shard_map/ppermute | solution.py:13
  62.6 24.1 %copy-start.7 = (f32[512]{0:T(512)S(1)}, f32[512]{0:T(512)}, u32[]{:S(2)}) copy-start(f32[512]{0:T(512)} %param.15) | copy-start | bytes 6148
  66.6 7.3 %collective-permute-start.6 = (f32[16,512]{1,0:T(8,128)S(1)}, f32[16,512]{1,0:T(8,128)S(1)}, u32[]{:S(2)}, u32[]{:S(2)}) collective-permute-start(f32[16,512]{1,0:T(8,128)S(1)} %get-tuple-element.16), channel_id=1, source_target_pairs={{0,256},{8,264},{16,272},{24,280},{32,288},{40,296},{48,304},{56,3... | collective-permute-start | bytes 98312 | tf_op jit(solution)/shard_map/ppermute | solution.py:13
  77.0 9.7 %all-to-all-start = ((f32[8,1,128]{2,1,0:T(1,128)}), f32[8,1,128]{2,1,0:T(1,128)S(1)}, u32[]{:S(2)}, u32[]{:S(2)}) async-start(f32[8,1,128]{2,1,0:T(1,128)} %broadcast_in_dim.12), calls=%async_computation | async-start | bytes 8192 | tf_op jit(solution)/shard_map/all_to_all | solution.py:115

commit v6 on v5

--- a/solution.py
+++ b/solution.py
@@ -55,14 +55,18 @@
     previous_signal = shifted(conv_input, "ctx", 1).astype(jnp.float32)
     previous_state, _, previous_local = block_terms(previous_signal, rates, weight, steps)
     own_state, fall, local_part = block_terms(signal, rates, weight, steps)
-    lookback = shifted(jnp.stack([key_rows, value_rows]), "ctx", 1)
-    previous_keys = lookback[0]
+    keys_values = jnp.stack([key_rows, value_rows])
 
     before_previous = jnp.zeros_like(previous_state)
     span = 1
     while span < ctx_count:
         sent = previous_state + before_previous
         got = shifted(sent, "ctx", span)
+        if span == 1:
+            got, keys_values = lax.optimization_barrier((got, keys_values))
+            lookback = shifted(keys_values, "ctx", 1)
+        if span == 4:
+            got, lookback = lax.optimization_barrier((got, lookback))
         if span == TIE_SPAN:
             got, local_part = lax.optimization_barrier((got, local_part))
         if span == 2 * TIE_SPAN:
@@ -70,6 +74,7 @@
         before_previous = before_previous + jnp.exp(-rates * float(row_count * span)) * got
         span *= 2
     before = jnp.exp(-rates * float(row_count)) * (previous_state + before_previous)
+    previous_keys = lookback[0]
 
     carried = jnp.exp(rates * last) * before
     convolved = local_part + jnp.sum(fall * carried[None], axis=1)

time: 88 us -> 87.7 us (level)
  waiting for transfers between devices: 31.3 us -> 36.2 us
  starting transfers between devices: 35.7 us -> 31.1 us
  other arithmetic: 6.44 us -> 5.48 us
    ppermute x8, waiting for transfers between devices: 26.2 us -> 31.1 us  [shifted(): return lax.ppermute(block, axis, route)]
    ppermute x8, starting transfers between devices: 31.2 us -> 26.4 us  [shifted(): return lax.ppermute(block, axis, route)]
    another operation x1, other arithmetic: 1 us -> 0.03 us  [per_device(): keys_values = jnp.stack([key_rows, value_rows])]
  transfers between devices with their start and end apart: 9 -> 9, of which waited for: 8 -> 8; matrix products, arithmetic and copies ran while one was open for 18% -> 16% of each run, Pallas kernels for 0% -> 0%
where the time goes in v6:
time: 87.7 us; the launch traced here: 86.8 us
  waiting for transfers between devices  36.2 us (41%)
  starting transfers between devices  31.1 us (35%)
  matrix products  11.6 us (13%)
  other arithmetic  5.48 us (6%)
  local copies, waits for them, and re-layouts  1.43 us (2%)
  between operations  0.99 us (1%)
    ppermute x8, waiting for transfers between devices, shifted(): return lax.ppermute(block, axis, route)  31.1 us
    ppermute x8, starting transfers between devices, shifted(): return lax.ppermute(block, axis, route)  26.4 us
    dot_general x2, matrix products, block_terms(): jnp.einsum('ts,src->trc', lower, lifted_lo, preferred_element_type=jnp.fl...  5.68 us
    dot_general x2, matrix products, block_terms(): jnp.einsum('ts,src->trc', lower, lifted_hi, preferred_element_type=jnp.fl...  5.46 us
    all_to_all x1, waiting for transfers between devices, per_device(): energy = jnp.sum(lax.all_to_all(spread, 'ch', 0, 0, tiled=True), axis=0)  5.08 us
    all_to_all x1, starting transfers between devices, per_device(): energy = jnp.sum(lax.all_to_all(spread, 'ch', 0, 0, tiled=True), axis=0)  4.6 us
  transfers between devices with their start and end apart: 9, of which 8 were waited for; matrix products, arithmetic and copies ran while one was open for 16% of the time, Pallas kernels for 0%

profile of v6, /device:TPU:6, one launch (start us, length us, event | category | flops | bytes accessed | tf_op | source)
XLA Modules:
  0.0 86.8 jit_solution(7254862774026398810)
XLA Ops:
  0.7 4.0 %collective-permute-start = (bf16[128,512]{1,0:T(8,128)(2,1)}, bf16[128,512]{1,0:T(8,128)(2,1)S(1)}, u32[]{:S(2)}, u32[]{:S(2)}) collective-permute-start(bf16[128,512]{1,0:T(8,128)(2,1)} %param.8), channel_id=1, source_target_pairs={{0,8},{8,16},{16,24},{24,32},{32,40},{40,48},{48,56},{56,64},{64,7... | collective-permute-start | bytes 393224 | tf_op jit(solution)/shard_map/ppermute | solution.py:13
  4.7 0.9 %convert_element_type.68 = f32[128,512]{1,0:T(8,128)S(1)} convert(bf16[128,512]{1,0:T(8,128)(2,1)} %param.8) | non-fusion elementwise | flops 65536 | bytes 393216 | tf_op jit(solution)/shard_map/convert_element_type | solution.py:49
  5.6 0.8 multiply_exponential_fusion.1
  6.4 3.5 %fusion.7 = f32[128,16,512]{2,0,1:T(8,128)} fusion(f32[128,512]{1,0:T(8,128)S(1)} %convert_element_type.68, f32[16,512]{1,0:T(8,128)} %bitcast.59), kind=kOutput, calls=%fused_computation.16 | convolution fusion | flops 272646144 | bytes 4489216 | tf_op jit(solution)/shard_map/ts,src->trc/dot_general | solution.py:33
  10.2 6.0 %collective-permute-done = bf16[128,512]{1,0:T(8,128)(2,1)S(1)} collective-permute-done((bf16[128,512]{1,0:T(8,128)(2,1)}, bf16[128,512]{1,0:T(8,128)(2,1)S(1)}, u32[]{:S(2)}, u32[]{:S(2)}) %collective-permute-start) | collective-permute-done | bytes 131104 | tf_op jit(solution)/shard_map/ppermute | solution.py:13
  16.2 0.3 multiply_reduce_fusion.4
  16.7 1.9 %collective-permute-start.1 = (f32[16,512]{1,0:T(8,128)S(1)}, f32[16,512]{1,0:T(8,128)S(1)}, u32[]{:S(2)}, u32[]{:S(2)}) collective-permute-start(f32[16,512]{1,0:T(8,128)S(1)} %get-tuple-element.31), channel_id=1, source_target_pairs={{0,8},{8,16},{16,24},{24,32},{32,40},{40,48},{48,56},{56,64},{64,7... | collective-permute-start | bytes 98312 | tf_op jit(solution)/shard_map/ppermute | solution.py:13
  18.8 0.1 copy.49
  18.9 5.7 %collective-permute-done.1 = f32[16,512]{1,0:T(8,128)S(1)} collective-permute-done((f32[16,512]{1,0:T(8,128)S(1)}, f32[16,512]{1,0:T(8,128)S(1)}, u32[]{:S(2)}, u32[]{:S(2)}) %collective-permute-start.1) | collective-permute-done | bytes 32800 | tf_op jit(solution)/shard_map/ppermute | solution.py:13
  24.6 1.9 %collective-permute-start.2 = (f32[16,512]{1,0:T(8,128)S(1)}, f32[16,512]{1,0:T(8,128)S(1)}, u32[]{:S(2)}, u32[]{:S(2)}) collective-permute-start(f32[16,512]{1,0:T(8,128)S(1)} %fusion.39), channel_id=1, source_target_pairs={{0,16},{8,24},{16,32},{24,40},{32,48},{40,56},{48,64},{56,72},{64,... | collective-permute-start | bytes 98312 | tf_op jit(solution)/shard_map/ppermute | solution.py:13
  26.6 4.3 %multiply_reduce_fusion.3 = f32[128,512]{1,0:T(8,128)S(1)} fusion(f32[128,16,512]{2,0,1:T(8,128)} %fusion.7, f32[128,512]{1,0:T(8,128)S(1)} %convert_element_type.68, f32[16,512]{1,0:T(8,128)S(1)} %bitcast.61, f32[128]{0:T(128)S(1)} %iota_negate_fusion, f32[16,512]{1,0:T(8,128)S(1)} %get-tuple-element.30), kind=kOutput, calls=%fused_computation.9 | convolution fusion | flops 278872064 | bytes 4784640 | tf_op jit(solution)/shard_map/ts,src->trc/dot_general | solution.py:35
  30.9 1.9 %collective-permute-start.4 = (bf16[2,128,512]{2,1,0:T(8,128)(2,1)S(1)}, bf16[2,128,512]{2,1,0:T(8,128)(2,1)S(1)}, u32[]{:S(2)}, u32[]{:S(2)}) collective-permute-start(bf16[2,128,512]{2,1,0:T(8,128)(2,1)S(1)} %pad_maximum_fusion), channel_id=1, source_target_pairs={{0,8},{8,16},{16,24},{24,32},{32,40},{40,48},{48,56},{56,64},{64,7... | collective-permute-start | bytes 786440 | tf_op jit(solution)/shard_map/ppermute | solution.py:13
  32.9 0.6 collective-permute-done.2
  33.5 6.8 %collective-permute-start.3 = (f32[16,512]{1,0:T(8,128)S(1)}, f32[16,512]{1,0:T(8,128)S(1)}, u32[]{:S(2)}, u32[]{:S(2)}) collective-permute-start(f32[16,512]{1,0:T(8,128)S(1)} %get-tuple-element.26), channel_id=1, source_target_pairs={{0,32},{8,40},{16,48},{24,56},{32,64},{40,72},{48,80},{56,88},{64,... | collective-permute-start | bytes 98312 | tf_op jit(solution)/shard_map/ppermute | solution.py:13
  40.3 1.3 %fusion.4 = f32[128,16,512]{2,0,1:T(8,128)S(1)} fusion(f32[128,512]{1,0:T(8,128)S(1)} %convert_element_type.67, f32[16,512]{1,0:T(8,128)S(1)} %bitcast.62), kind=kOutput, calls=%fused_computation.15 | convolution fusion | flops 273694720 | bytes 4489216 | tf_op jit(solution)/shard_map/ts,src->trc/dot_general | solution.py:35
  41.6 2.8 %collective-permute-done.3 = f32[16,512]{1,0:T(8,128)S(1)} collective-permute-done((f32[16,512]{1,0:T(8,128)S(1)}, f32[16,512]{1,0:T(8,128)S(1)}, u32[]{:S(2)}, u32[]{:S(2)}) %collective-permute-start.3) | collective-permute-done | bytes 32800 | tf_op jit(solution)/shard_map/ppermute | solution.py:13
  44.4 7.4 %collective-permute-start.5 = (f32[16,512]{1,0:T(8,128)S(1)}, f32[16,512]{1,0:T(8,128)S(1)}, u32[]{:S(2)}, u32[]{:S(2)}) collective-permute-start(f32[16,512]{1,0:T(8,128)S(1)} %fusion.40), channel_id=1, source_target_pairs={{0,64},{8,72},{16,80},{24,88},{32,96},{40,104},{48,112},{56,120},{... | collective-permute-start | bytes 98312 | tf_op jit(solution)/shard_map/ppermute | solution.py:13
  51.8 2.0 %multiply_reduce_fusion.2 = f32[128,512]{1,0:T(8,128)S(1)} fusion(f32[128,16,512]{2,0,1:T(8,128)S(1)} %fusion.4, f32[128,512]{1,0:T(8,128)S(1)} %convert_element_type.67, f32[16,512]{1,0:T(8,128)S(1)} %bitcast.63, f32[128]{0:T(128)S(1)} %iota_negate_fusion, f32[16,512]{1,0:T(8,128)S(1)} %get-tuple-element.30), kind=kOutput, calls=%fused_computation.8 | convolution fusion | flops 277823488 | bytes 4784640 | tf_op jit(solution)/shard_map/ts,src->trc/dot_general | solution.py:33
  54.0 0.1 copy.48
  54.1 5.8 %collective-permute-done.5 = f32[16,512]{1,0:T(8,128)S(1)} collective-permute-done((f32[16,512]{1,0:T(8,128)S(1)}, f32[16,512]{1,0:T(8,128)S(1)}, u32[]{:S(2)}, u32[]{:S(2)}) %collective-permute-start.5) | collective-permute-done | bytes 32800 | tf_op jit(solution)/shard_map/ppermute | solution.py:13
  60.0 1.3 %collective-permute-start.6 = (f32[16,512]{1,0:T(8,128)S(1)}, f32[16,512]{1,0:T(8,128)S(1)}, u32[]{:S(2)}, u32[]{:S(2)}) collective-permute-start(f32[16,512]{1,0:T(8,128)S(1)} %fusion.42), channel_id=1, source_target_pairs={{0,128},{8,136},{16,144},{24,152},{32,160},{40,168},{48,176},{56,1... | collective-permute-start | bytes 98312 | tf_op jit(solution)/shard_map/ppermute | solution.py:13
  61.3 0.3 fusion.45
  61.5 4.2 %collective-permute-done.6 = f32[16,512]{1,0:T(8,128)S(1)} collective-permute-done((f32[16,512]{1,0:T(8,128)S(1)}, f32[16,512]{1,0:T(8,128)S(1)}, u32[]{:S(2)}, u32[]{:S(2)}) %collective-permute-start.6) | collective-permute-done | bytes 32800 | tf_op jit(solution)/shard_map/ppermute | solution.py:13
  65.8 1.3 %collective-permute-start.7 = (f32[16,512]{1,0:T(8,128)S(1)}, f32[16,512]{1,0:T(8,128)S(1)}, u32[]{:S(2)}, u32[]{:S(2)}) collective-permute-start(f32[16,512]{1,0:T(8,128)S(1)} %get-tuple-element.24), channel_id=1, source_target_pairs={{0,256},{8,264},{16,272},{24,280},{32,288},{40,296},{48,304},{56,3... | collective-permute-start | bytes 98312 | tf_op jit(solution)/shard_map/ppermute | solution.py:13
  67.2 5.9 %collective-permute-done.7 = f32[16,512]{1,0:T(8,128)S(1)} collective-permute-done((f32[16,512]{1,0:T(8,128)S(1)}, f32[16,512]{1,0:T(8,128)S(1)}, u32[]{:S(2)}, u32[]{:S(2)}) %collective-permute-start.7) | collective-permute-done | bytes 32800 | tf_op jit(solution)/shard_map/ppermute | solution.py:13
  73.1 1.2 %multiply_reduce_fusion = (f32[128,512]{1,0:T(8,128)S(1)}, f32[128,512]{1,0:T(8,128)S(1)}) fusion(f32[16,512]{1,0:T(8,128)S(1)} %get-tuple-element.29, f32[16,512]{1,0:T(8,128)S(1)} %bitcast.64, f32[128]{0:T(128)S(1)} %iota_negate_fusion, f32[16,512]{1,0:T(8,128)S(1)} %get-tuple-element.30, f32[16,512]{1,0:T(8,128)S(1)} %get-tuple-element.28), kind=kLoop, calls=%fused_computation.6 | loop fusion | flops 6160384 | bytes 655872 | tf_op jit(solution)/shard_map/reduce_sum | solution.py:85
  74.4 0.8 multiply_convert_fusion
  75.4 0.3 multiply_reduce_fusion.5
  75.6 0.6 broadcast_in_dim.12
  76.2 4.6 %all-to-all-start = ((f32[8,1,128]{2,1,0:T(1,128)}), f32[8,1,128]{2,1,0:T(1,128)S(1)}, u32[]{:S(2)}, u32[]{:S(2)}) async-start(f32[8,1,128]{2,1,0:T(1,128)} %broadcast_in_dim.12), calls=%async_computation | async-start | bytes 8192 | tf_op jit(solution)/shard_map/all_to_all | solution.py:120
  81.0 5.1 %all-to-all-done = f32[8,1,128]{2,1,0:T(1,128)S(1)} async-done(((f32[8,1,128]{2,1,0:T(1,128)}), f32[8,1,128]{2,1,0:T(1,128)S(1)}, u32[]{:S(2)}, u32[]{:S(2)}) %all-to-all-start) | async-done | bytes 4128 | tf_op jit(solution)/shard_map/all_to_all | solution.py:120
  86.1 0.8 divide_convert_fusion
  (41 shorter events, 1.2 us)
Async XLA Ops:
  0.6 60.6 %copy-start = (bf16[128,512]{1,0:T(8,128)(2,1)S(1)}, bf16[128,512]{1,0:T(8,128)(2,1)}, u32[]{:S(2)}) copy-start(bf16[128,512]{1,0:T(8,128)(2,1)} %param.12) | copy-start | bytes 393220
  0.6 15.9 %copy-start.1 = (f32[512,16]{0,1:T(8,128)S(1)}, f32[512,16]{0,1:T(8,128)}, u32[]{:S(2)}) copy-start(f32[512,16]{0,1:T(8,128)} %param.10) | copy-start | bytes 98308
  0.7 9.5 %copy-start.3 = (bf16[128,512]{1,0:T(8,128)(2,1)S(1)}, bf16[128,512]{1,0:T(8,128)(2,1)}, u32[]{:S(2)}) copy-start(bf16[128,512]{1,0:T(8,128)(2,1)} %param.14) | copy-start | bytes 393220
  0.7 9.5 %copy-start.4 = (bf16[128,512]{1,0:T(8,128)(2,1)S(1)}, bf16[128,512]{1,0:T(8,128)(2,1)}, u32[]{:S(2)}) copy-start(bf16[128,512]{1,0:T(8,128)(2,1)} %param.13) | copy-start | bytes 393220
  0.7 16.0 %copy-start.5 = (f32[512,16]{0,1:T(8,128)S(1)}, f32[512,16]{0,1:T(8,128)}, u32[]{:S(2)}) copy-start(f32[512,16]{0,1:T(8,128)} %param.9) | copy-start | bytes 98308
  0.7 15.5 %collective-permute-start = (bf16[128,512]{1,0:T(8,128)(2,1)}, bf16[128,512]{1,0:T(8,128)(2,1)S(1)}, u32[]{:S(2)}, u32[]{:S(2)}) collective-permute-start(bf16[128,512]{1,0:T(8,128)(2,1)} %param.8), channel_id=1, source_target_pairs={{0,8},{8,16},{16,24},{24,32},{32,40},{40,48},{48,56},{56,64},{64,7... | collective-permute-start | bytes 393224 | tf_op jit(solution)/shard_map/ppermute | solution.py:13
  16.7 7.9 %collective-permute-start.1 = (f32[16,512]{1,0:T(8,128)S(1)}, f32[16,512]{1,0:T(8,128)S(1)}, u32[]{:S(2)}, u32[]{:S(2)}) collective-permute-start(f32[16,512]{1,0:T(8,128)S(1)} %get-tuple-element.31), channel_id=1, source_target_pairs={{0,8},{8,16},{16,24},{24,32},{32,40},{40,48},{48,56},{56,64},{64,7... | collective-permute-start | bytes 98312 | tf_op jit(solution)/shard_map/ppermute | solution.py:13
  24.6 8.8 %collective-permute-start.2 = (f32[16,512]{1,0:T(8,128)S(1)}, f32[16,512]{1,0:T(8,128)S(1)}, u32[]{:S(2)}, u32[]{:S(2)}) collective-permute-start(f32[16,512]{1,0:T(8,128)S(1)} %fusion.39), channel_id=1, source_target_pairs={{0,16},{8,24},{16,32},{24,40},{32,48},{40,56},{48,64},{56,72},{64,... | collective-permute-start | bytes 98312 | tf_op jit(solution)/shard_map/ppermute | solution.py:13
  30.9 13.5 %collective-permute-start.4 = (bf16[2,128,512]{2,1,0:T(8,128)(2,1)S(1)}, bf16[2,128,512]{2,1,0:T(8,128)(2,1)S(1)}, u32[]{:S(2)}, u32[]{:S(2)}) collective-permute-start(bf16[2,128,512]{2,1,0:T(8,128)(2,1)S(1)} %pad_maximum_fusion), channel_id=1, source_target_pairs={{0,8},{8,16},{16,24},{24,32},{32,40},{40,48},{48,56},{56,64},{64,7... | collective-permute-start | bytes 786440 | tf_op jit(solution)/shard_map/ppermute | solution.py:13
  33.5 10.9 %collective-permute-start.3 = (f32[16,512]{1,0:T(8,128)S(1)}, f32[16,512]{1,0:T(8,128)S(1)}, u32[]{:S(2)}, u32[]{:S(2)}) collective-permute-start(f32[16,512]{1,0:T(8,128)S(1)} %get-tuple-element.26), channel_id=1, source_target_pairs={{0,32},{8,40},{16,48},{24,56},{32,64},{40,72},{48,80},{56,88},{64,... | collective-permute-start | bytes 98312 | tf_op jit(solution)/shard_map/ppermute | solution.py:13
  44.4 15.5 %collective-permute-start.5 = (f32[16,512]{1,0:T(8,128)S(1)}, f32[16,512]{1,0:T(8,128)S(1)}, u32[]{:S(2)}, u32[]{:S(2)}) collective-permute-start(f32[16,512]{1,0:T(8,128)S(1)} %fusion.40), channel_id=1, source_target_pairs={{0,64},{8,72},{16,80},{24,88},{32,96},{40,104},{48,112},{56,120},{... | collective-permute-start | bytes 98312 | tf_op jit(solution)/shard_map/ppermute | solution.py:13
  53.8 20.6 %copy-start.2 = (bf16[128,512]{1,0:T(8,128)(2,1)S(1)}, bf16[128,512]{1,0:T(8,128)(2,1)}, u32[]{:S(2)}) copy-start(bf16[128,512]{1,0:T(8,128)(2,1)} %param.8) | copy-start | bytes 393220
  53.8 20.6 %copy-start.6 = (f32[512]{0:T(512)S(1)}, f32[512]{0:T(512)}, u32[]{:S(2)}) copy-start(f32[512]{0:T(512)} %param.11) | copy-start | bytes 6148
  60.0 5.8 %collective-permute-start.6 = (f32[16,512]{1,0:T(8,128)S(1)}, f32[16,512]{1,0:T(8,128)S(1)}, u32[]{:S(2)}, u32[]{:S(2)}) collective-permute-start(f32[16,512]{1,0:T(8,128)S(1)} %fusion.42), channel_id=1, source_target_pairs={{0,128},{8,136},{16,144},{24,152},{32,160},{40,168},{48,176},{56,1... | collective-permute-start | bytes 98312 | tf_op jit(solution)/shard_map/ppermute | solution.py:13
  61.5 24.5 %copy-start.7 = (f32[512]{0:T(512)S(1)}, f32[512]{0:T(512)}, u32[]{:S(2)}) copy-start(f32[512]{0:T(512)} %param.15) | copy-start | bytes 6148
  65.8 7.3 %collective-permute-start.7 = (f32[16,512]{1,0:T(8,128)S(1)}, f32[16,512]{1,0:T(8,128)S(1)}, u32[]{:S(2)}, u32[]{:S(2)}) collective-permute-start(f32[16,512]{1,0:T(8,128)S(1)} %get-tuple-element.24), channel_id=1, source_target_pairs={{0,256},{8,264},{16,272},{24,280},{32,288},{40,296},{48,304},{56,3... | collective-permute-start | bytes 98312 | tf_op jit(solution)/shard_map/ppermute | solution.py:13
  76.2 9.8 %all-to-all-start = ((f32[8,1,128]{2,1,0:T(1,128)}), f32[8,1,128]{2,1,0:T(1,128)S(1)}, u32[]{:S(2)}, u32[]{:S(2)}) async-start(f32[8,1,128]{2,1,0:T(1,128)} %broadcast_in_dim.12), calls=%async_computation | async-start | bytes 8192 | tf_op jit(solution)/shard_map/all_to_all | solution.py:120

commit v7 on v6

--- a/solution.py
+++ b/solution.py
@@ -4,7 +4,6 @@
 from jax.sharding import PartitionSpec as P
 
 HD = 128
-TIE_SPAN = 4
 
 
 def shifted(block, axis, distance):
@@ -34,9 +33,7 @@
         "ts,src->trc", lower, lifted_hi, preferred_element_type=jnp.float32
     ) + jnp.einsum("ts,src->trc", lower, lifted_lo, preferred_element_type=jnp.float32)
     fall = weight[None] * jnp.exp(-steps[:, None, None] * rates[None])
-    local_part = jnp.sum(fall * prefix, axis=1)
-
-    return own_state, fall, local_part
+    return own_state, fall, prefix
 
 
 def per_device(
@@ -53,8 +50,8 @@
     last = float(row_count - 1)
 
     previous_signal = shifted(conv_input, "ctx", 1).astype(jnp.float32)
-    previous_state, _, previous_local = block_terms(previous_signal, rates, weight, steps)
-    own_state, fall, local_part = block_terms(signal, rates, weight, steps)
+    previous_state, _, previous_prefix = block_terms(previous_signal, rates, weight, steps)
+    own_state, fall, own_prefix = block_terms(signal, rates, weight, steps)
     keys_values = jnp.stack([key_rows, value_rows])
 
     before_previous = jnp.zeros_like(previous_state)
@@ -67,10 +64,16 @@
             lookback = shifted(keys_values, "ctx", 1)
         if span == 4:
             got, lookback = lax.optimization_barrier((got, lookback))
-        if span == TIE_SPAN:
+        if span == ctx_count // 8:
+            got, previous_prefix = lax.optimization_barrier((got, previous_prefix))
+            previous_local = jnp.sum(fall * previous_prefix, axis=1)
+        if span == ctx_count // 4:
+            got, previous_local, own_prefix = lax.optimization_barrier(
+                (got, previous_local, own_prefix)
+            )
+            local_part = jnp.sum(fall * own_prefix, axis=1)
+        if span == ctx_count // 2:
             got, local_part = lax.optimization_barrier((got, local_part))
-        if span == 2 * TIE_SPAN:
-            got, previous_local = lax.optimization_barrier((got, previous_local))
         before_previous = before_previous + jnp.exp(-rates * float(row_count * span)) * got
         span *= 2
     before = jnp.exp(-rates * float(row_count)) * (previous_state + before_previous)

time: 87.7 us -> 87.9 us (level)
  other arithmetic: 5.48 us -> 9.49 us
  starting transfers between devices: 31.1 us -> 29.5 us
  matrix products: 11.6 us -> 10 us
    reduce_sum x0 -> x2, other arithmetic: none -> 4.01 us  [the longest x1 3.1 us: per_device(): previous_local = jnp.sum(fall * previous_prefix, axis=1)]
    ppermute x8, starting transfers between devices: 26.4 us -> 25.1 us  [shifted(): return lax.ppermute(block, axis, route)]
  transfers between devices with their start and end apart: 9 -> 9, of which waited for: 8 -> 8; matrix products, arithmetic and copies ran while one was open for 16% -> 19% of each run, Pallas kernels for 0% -> 0%
where the time goes in v7:
time: 87.9 us; the launch traced here: 87 us
  waiting for transfers between devices  35.4 us (40%)
  starting transfers between devices  29.5 us (34%)
  matrix products  10 us (11%)
  other arithmetic  9.49 us (11%)
  local copies, waits for them, and re-layouts  1.44 us (2%)
  between operations  1.02 us (1%)
    ppermute x8, waiting for transfers between devices, shifted(): return lax.ppermute(block, axis, route)  30.3 us
    ppermute x8, starting transfers between devices, shifted(): return lax.ppermute(block, axis, route)  25.1 us
    all_to_all x1, waiting for transfers between devices, per_device(): energy = jnp.sum(lax.all_to_all(spread, 'ch', 0, 0, tiled=True), axis=0)  5.08 us
    dot_general x2, matrix products, block_terms(): jnp.einsum('ts,src->trc', lower, lifted_lo, preferred_element_type=jnp.fl...  4.81 us
    dot_general x2, matrix products, block_terms(): jnp.einsum('ts,src->trc', lower, lifted_hi, preferred_element_type=jnp.fl...  4.73 us
    all_to_all x1, starting transfers between devices, per_device(): energy = jnp.sum(lax.all_to_all(spread, 'ch', 0, 0, tiled=True), axis=0)  4.48 us
    reduce_sum x1, other arithmetic, per_device(): previous_local = jnp.sum(fall * previous_prefix, axis=1)  3.1 us
  transfers between devices with their start and end apart: 9, of which 8 were waited for; matrix products, arithmetic and copies ran while one was open for 19% of the time, Pallas kernels for 0%

profile of v7, /device:TPU:6, one launch (start us, length us, event | category | flops | bytes accessed | tf_op | source)
XLA Modules:
  0.0 87.0 jit_solution(15820454778494819317)
XLA Ops:
  0.7 4.0 %collective-permute-start = (bf16[128,512]{1,0:T(8,128)(2,1)}, bf16[128,512]{1,0:T(8,128)(2,1)S(1)}, u32[]{:S(2)}, u32[]{:S(2)}) collective-permute-start(bf16[128,512]{1,0:T(8,128)(2,1)} %param.8), channel_id=1, source_target_pairs={{0,8},{8,16},{16,24},{24,32},{32,40},{40,48},{48,56},{56,64},{64,7... | collective-permute-start | bytes 393224 | tf_op jit(solution)/shard_map/ppermute | solution.py:12
  4.6 0.9 %convert_element_type.70 = f32[128,512]{1,0:T(8,128)S(1)} convert(bf16[128,512]{1,0:T(8,128)(2,1)} %param.8) | non-fusion elementwise | flops 65536 | bytes 393216 | tf_op jit(solution)/shard_map/convert_element_type | solution.py:46
  5.6 0.8 multiply_exponential_fusion.1
  6.4 1.6 %fusion.7 = f32[128,16,512]{2,0,1:T(8,128)S(1)} fusion(f32[128,512]{1,0:T(8,128)S(1)} %convert_element_type.70, f32[16,512]{1,0:T(8,128)} %bitcast.59), kind=kOutput, calls=%fused_computation.18 | convolution fusion | flops 272646144 | bytes 4489216 | tf_op jit(solution)/shard_map/ts,src->trc/dot_general | solution.py:32
  8.0 3.5 %convolution_add_fusion = f32[128,16,512]{2,0,1:T(8,128)} fusion(f32[128,16,512]{2,0,1:T(8,128)S(1)} %fusion.7, f32[128,512]{1,0:T(8,128)S(1)} %convert_element_type.70, f32[16,512]{1,0:T(8,128)S(1)} %bitcast.60), kind=kOutput, calls=%fused_computation.15 | convolution fusion | flops 274743296 | bytes 8683520 | tf_op jit(solution)/shard_map/ts,src->trc/dot_general | solution.py:34
  11.7 4.4 %collective-permute-done = bf16[128,512]{1,0:T(8,128)(2,1)S(1)} collective-permute-done((bf16[128,512]{1,0:T(8,128)(2,1)}, bf16[128,512]{1,0:T(8,128)(2,1)S(1)}, u32[]{:S(2)}, u32[]{:S(2)}) %collective-permute-start) | collective-permute-done | bytes 131104 | tf_op jit(solution)/shard_map/ppermute | solution.py:12
  16.2 0.3 multiply_reduce_fusion.4
  16.7 1.9 %collective-permute-start.1 = (f32[16,512]{1,0:T(8,128)S(1)}, f32[16,512]{1,0:T(8,128)S(1)}, u32[]{:S(2)}, u32[]{:S(2)}) collective-permute-start(f32[16,512]{1,0:T(8,128)S(1)} %get-tuple-element.37), channel_id=1, source_target_pairs={{0,8},{8,16},{16,24},{24,32},{32,40},{40,48},{48,56},{56,64},{64,7... | collective-permute-start | bytes 98312 | tf_op jit(solution)/shard_map/ppermute | solution.py:12
  18.9 5.7 %collective-permute-done.1 = f32[16,512]{1,0:T(8,128)S(1)} collective-permute-done((f32[16,512]{1,0:T(8,128)S(1)}, f32[16,512]{1,0:T(8,128)S(1)}, u32[]{:S(2)}, u32[]{:S(2)}) %collective-permute-start.1) | collective-permute-done | bytes 32800 | tf_op jit(solution)/shard_map/ppermute | solution.py:12
  24.6 1.9 %collective-permute-start.2 = (f32[16,512]{1,0:T(8,128)S(1)}, f32[16,512]{1,0:T(8,128)S(1)}, u32[]{:S(2)}, u32[]{:S(2)}) collective-permute-start(f32[16,512]{1,0:T(8,128)S(1)} %fusion.39), channel_id=1, source_target_pairs={{0,16},{8,24},{16,32},{24,40},{32,48},{40,56},{48,64},{56,72},{64,... | collective-permute-start | bytes 98312 | tf_op jit(solution)/shard_map/ppermute | solution.py:12
  26.5 1.3 %fusion.5 = f32[128,16,512]{2,0,1:T(8,128)S(1)} fusion(f32[128,512]{1,0:T(8,128)S(1)} %convert_element_type.67, f32[16,512]{1,0:T(8,128)S(1)} %bitcast.62), kind=kOutput, calls=%fused_computation.17 | convolution fusion | flops 273694720 | bytes 4489216 | tf_op jit(solution)/shard_map/ts,src->trc/dot_general | solution.py:34
  27.9 1.9 %collective-permute-start.4 = (bf16[2,128,512]{2,1,0:T(8,128)(2,1)S(1)}, bf16[2,128,512]{2,1,0:T(8,128)(2,1)S(1)}, u32[]{:S(2)}, u32[]{:S(2)}) collective-permute-start(bf16[2,128,512]{2,1,0:T(8,128)(2,1)S(1)} %pad_maximum_fusion), channel_id=1, source_target_pairs={{0,8},{8,16},{16,24},{24,32},{32,40},{40,48},{48,56},{56,64},{64,7... | collective-permute-start | bytes 786440 | tf_op jit(solution)/shard_map/ppermute | solution.py:12
  29.8 3.7 %collective-permute-done.2 = f32[16,512]{1,0:T(8,128)S(1)} collective-permute-done((f32[16,512]{1,0:T(8,128)S(1)}, f32[16,512]{1,0:T(8,128)S(1)}, u32[]{:S(2)}, u32[]{:S(2)}) %collective-permute-start.2) | collective-permute-done | bytes 32800 | tf_op jit(solution)/shard_map/ppermute | solution.py:12
  33.5 5.3 %collective-permute-start.3 = (f32[16,512]{1,0:T(8,128)S(1)}, f32[16,512]{1,0:T(8,128)S(1)}, u32[]{:S(2)}, u32[]{:S(2)}) collective-permute-start(f32[16,512]{1,0:T(8,128)S(1)} %get-tuple-element.32), channel_id=1, source_target_pairs={{0,32},{8,40},{16,48},{24,56},{32,64},{40,72},{48,80},{56,88},{64,... | collective-permute-start | bytes 98312 | tf_op jit(solution)/shard_map/ppermute | solution.py:12
  38.8 3.2 %convolution_add_fusion.1 = f32[128,16,512]{2,0,1:T(8,128)} fusion(f32[128,16,512]{2,0,1:T(8,128)S(1)} %fusion.5, f32[128,512]{1,0:T(8,128)S(1)} %convert_element_type.67, f32[16,512]{1,0:T(8,128)S(1)} %bitcast.63), kind=kOutput, calls=%fused_computation.16 | convolution fusion | flops 273694720 | bytes 8683520 | tf_op jit(solution)/shard_map/ts,src->trc/dot_general | solution.py:32
  42.0 2.7 %collective-permute-done.3 = f32[16,512]{1,0:T(8,128)S(1)} collective-permute-done((f32[16,512]{1,0:T(8,128)S(1)}, f32[16,512]{1,0:T(8,128)S(1)}, u32[]{:S(2)}, u32[]{:S(2)}) %collective-permute-start.3) | collective-permute-done | bytes 32800 | tf_op jit(solution)/shard_map/ppermute | solution.py:12
  44.7 7.5 %collective-permute-start.5 = (f32[16,512]{1,0:T(8,128)S(1)}, f32[16,512]{1,0:T(8,128)S(1)}, u32[]{:S(2)}, u32[]{:S(2)}) collective-permute-start(f32[16,512]{1,0:T(8,128)S(1)} %fusion.40), channel_id=1, source_target_pairs={{0,64},{8,72},{16,80},{24,88},{32,96},{40,104},{48,112},{56,120},{... | collective-permute-start | bytes 98312 | tf_op jit(solution)/shard_map/ppermute | solution.py:12
  52.6 0.3 fusion.45
  52.9 7.3 %collective-permute-done.5 = f32[16,512]{1,0:T(8,128)S(1)} collective-permute-done((f32[16,512]{1,0:T(8,128)S(1)}, f32[16,512]{1,0:T(8,128)S(1)}, u32[]{:S(2)}, u32[]{:S(2)}) %collective-permute-start.5) | collective-permute-done | bytes 32800 | tf_op jit(solution)/shard_map/ppermute | solution.py:12
  60.2 1.3 %collective-permute-start.6 = (f32[16,512]{1,0:T(8,128)S(1)}, f32[16,512]{1,0:T(8,128)S(1)}, u32[]{:S(2)}, u32[]{:S(2)}) collective-permute-start(f32[16,512]{1,0:T(8,128)S(1)} %fusion.42), channel_id=1, source_target_pairs={{0,128},{8,136},{16,144},{24,152},{32,160},{40,168},{48,176},{56,1... | collective-permute-start | bytes 98312 | tf_op jit(solution)/shard_map/ppermute | solution.py:12
  61.5 3.1 %multiply_reduce_fusion.3 = f32[128,512]{1,0:T(8,128)S(1)} fusion(f32[128,16,512]{2,0,1:T(8,128)} %convolution_add_fusion.1, f32[128]{0:T(128)S(1)} %iota_negate_fusion, f32[16,512]{1,0:T(8,128)S(1)} %get-tuple-element.36, f32[16,512]{1,0:T(8,128)S(1)} %bitcast.64), kind=kLoop, calls=%fused_computation.9 | loop fusion | flops 4128768 | bytes 4522496 | tf_op jit(solution)/shard_map/reduce_sum | solution.py:69
  64.6 1.4 %collective-permute-done.6 = f32[16,512]{1,0:T(8,128)S(1)} collective-permute-done((f32[16,512]{1,0:T(8,128)S(1)}, f32[16,512]{1,0:T(8,128)S(1)}, u32[]{:S(2)}, u32[]{:S(2)}) %collective-permute-start.6) | collective-permute-done | bytes 32800 | tf_op jit(solution)/shard_map/ppermute | solution.py:12
  66.1 1.3 %collective-permute-start.7 = (f32[16,512]{1,0:T(8,128)S(1)}, f32[16,512]{1,0:T(8,128)S(1)}, u32[]{:S(2)}, u32[]{:S(2)}) collective-permute-start(f32[16,512]{1,0:T(8,128)S(1)} %get-tuple-element.30), channel_id=1, source_target_pairs={{0,256},{8,264},{16,272},{24,280},{32,288},{40,296},{48,304},{56,3... | collective-permute-start | bytes 98312 | tf_op jit(solution)/shard_map/ppermute | solution.py:12
  67.4 0.9 %multiply_reduce_fusion.2 = f32[128,512]{1,0:T(8,128)S(1)} fusion(f32[128,16,512]{2,0,1:T(8,128)S(1)} %copy-done.1, f32[128]{0:T(128)S(1)} %iota_negate_fusion, f32[16,512]{1,0:T(8,128)S(1)} %get-tuple-element.36, f32[16,512]{1,0:T(8,128)S(1)} %bitcast.65), kind=kLoop, calls=%fused_computation.8 | loop fusion | flops 4128768 | bytes 4522496 | tf_op jit(solution)/shard_map/reduce_sum | solution.py:74
  68.3 5.1 %collective-permute-done.7 = f32[16,512]{1,0:T(8,128)S(1)} collective-permute-done((f32[16,512]{1,0:T(8,128)S(1)}, f32[16,512]{1,0:T(8,128)S(1)}, u32[]{:S(2)}, u32[]{:S(2)}) %collective-permute-start.7) | collective-permute-done | bytes 32800 | tf_op jit(solution)/shard_map/ppermute | solution.py:12
  73.4 1.2 %multiply_reduce_fusion = (f32[128,512]{1,0:T(8,128)S(1)}, f32[128,512]{1,0:T(8,128)S(1)}) fusion(f32[16,512]{1,0:T(8,128)S(1)} %get-tuple-element.35, f32[128]{0:T(128)S(1)} %iota_negate_fusion, f32[16,512]{1,0:T(8,128)S(1)} %get-tuple-element.36, f32[16,512]{1,0:T(8,128)S(1)} %bitcast.66, f32[16,512]{1,0:T(8,128)S(1)} %get-tuple-element.34), kind=kLoop, calls=%fused_computation.6 | loop fusion | flops 6160384 | bytes 655872 | tf_op jit(solution)/shard_map/reduce_sum | solution.py:88
  74.6 0.8 multiply_convert_fusion
  75.6 0.3 multiply_reduce_fusion.5
  75.9 0.6 broadcast_in_dim.12
  76.5 4.5 %all-to-all-start = ((f32[8,1,128]{2,1,0:T(1,128)}), f32[8,1,128]{2,1,0:T(1,128)S(1)}, u32[]{:S(2)}, u32[]{:S(2)}) async-start(f32[8,1,128]{2,1,0:T(1,128)} %broadcast_in_dim.12), calls=%async_computation | async-start | bytes 8192 | tf_op jit(solution)/shard_map/all_to_all | solution.py:123
  81.1 5.1 %all-to-all-done = f32[8,1,128]{2,1,0:T(1,128)S(1)} async-done(((f32[8,1,128]{2,1,0:T(1,128)}), f32[8,1,128]{2,1,0:T(1,128)S(1)}, u32[]{:S(2)}, u32[]{:S(2)}) %all-to-all-start) | async-done | bytes 4128 | tf_op jit(solution)/shard_map/all_to_all | solution.py:123
  86.2 0.8 divide_convert_fusion
  (45 shorter events, 1.5 us)
Async XLA Ops:
  0.6 51.9 %copy-start = (bf16[128,512]{1,0:T(8,128)(2,1)S(1)}, bf16[128,512]{1,0:T(8,128)(2,1)}, u32[]{:S(2)}) copy-start(bf16[128,512]{1,0:T(8,128)(2,1)} %param.12) | copy-start | bytes 393220
  0.6 7.4 %copy-start.2 = (f32[512,16]{0,1:T(8,128)S(1)}, f32[512,16]{0,1:T(8,128)}, u32[]{:S(2)}) copy-start(f32[512,16]{0,1:T(8,128)} %param.10) | copy-start | bytes 98308
  0.7 15.5 %collective-permute-start = (bf16[128,512]{1,0:T(8,128)(2,1)}, bf16[128,512]{1,0:T(8,128)(2,1)S(1)}, u32[]{:S(2)}, u32[]{:S(2)}) collective-permute-start(bf16[128,512]{1,0:T(8,128)(2,1)} %param.8), channel_id=1, source_target_pairs={{0,8},{8,16},{16,24},{24,32},{32,40},{40,48},{48,56},{56,64},{64,7... | collective-permute-start | bytes 393224 | tf_op jit(solution)/shard_map/ppermute | solution.py:12
  8.0 3.7 %copy-start.4 = (bf16[128,512]{1,0:T(8,128)(2,1)S(1)}, bf16[128,512]{1,0:T(8,128)(2,1)}, u32[]{:S(2)}) copy-start(bf16[128,512]{1,0:T(8,128)(2,1)} %param.14) | copy-start | bytes 393220
  8.0 3.7 %copy-start.5 = (bf16[128,512]{1,0:T(8,128)(2,1)S(1)}, bf16[128,512]{1,0:T(8,128)(2,1)}, u32[]{:S(2)}) copy-start(bf16[128,512]{1,0:T(8,128)(2,1)} %param.13) | copy-start | bytes 393220
  8.0 8.6 %copy-start.6 = (f32[512,16]{0,1:T(8,128)S(1)}, f32[512,16]{0,1:T(8,128)}, u32[]{:S(2)}) copy-start(f32[512,16]{0,1:T(8,128)} %param.9) | copy-start | bytes 98308
  16.7 7.9 %collective-permute-start.1 = (f32[16,512]{1,0:T(8,128)S(1)}, f32[16,512]{1,0:T(8,128)S(1)}, u32[]{:S(2)}, u32[]{:S(2)}) collective-permute-start(f32[16,512]{1,0:T(8,128)S(1)} %get-tuple-element.37), channel_id=1, source_target_pairs={{0,8},{8,16},{16,24},{24,32},{32,40},{40,48},{48,56},{56,64},{64,7... | collective-permute-start | bytes 98312 | tf_op jit(solution)/shard_map/ppermute | solution.py:12
  24.6 8.9 %collective-permute-start.2 = (f32[16,512]{1,0:T(8,128)S(1)}, f32[16,512]{1,0:T(8,128)S(1)}, u32[]{:S(2)}, u32[]{:S(2)}) collective-permute-start(f32[16,512]{1,0:T(8,128)S(1)} %fusion.39), channel_id=1, source_target_pairs={{0,16},{8,24},{16,32},{24,40},{32,48},{40,56},{48,64},{56,72},{64,... | collective-permute-start | bytes 98312 | tf_op jit(solution)/shard_map/ppermute | solution.py:12
  27.9 16.8 %collective-permute-start.4 = (bf16[2,128,512]{2,1,0:T(8,128)(2,1)S(1)}, bf16[2,128,512]{2,1,0:T(8,128)(2,1)S(1)}, u32[]{:S(2)}, u32[]{:S(2)}) collective-permute-start(bf16[2,128,512]{2,1,0:T(8,128)(2,1)S(1)} %pad_maximum_fusion), channel_id=1, source_target_pairs={{0,8},{8,16},{16,24},{24,32},{32,40},{40,48},{48,56},{56,64},{64,7... | collective-permute-start | bytes 786440 | tf_op jit(solution)/shard_map/ppermute | solution.py:12
  33.5 11.2 %collective-permute-start.3 = (f32[16,512]{1,0:T(8,128)S(1)}, f32[16,512]{1,0:T(8,128)S(1)}, u32[]{:S(2)}, u32[]{:S(2)}) collective-permute-start(f32[16,512]{1,0:T(8,128)S(1)} %get-tuple-element.32), channel_id=1, source_target_pairs={{0,32},{8,40},{16,48},{24,56},{32,64},{40,72},{48,80},{56,88},{64,... | collective-permute-start | bytes 98312 | tf_op jit(solution)/shard_map/ppermute | solution.py:12
  44.7 15.4 %collective-permute-start.5 = (f32[16,512]{1,0:T(8,128)S(1)}, f32[16,512]{1,0:T(8,128)S(1)}, u32[]{:S(2)}, u32[]{:S(2)}) collective-permute-start(f32[16,512]{1,0:T(8,128)S(1)} %fusion.40), channel_id=1, source_target_pairs={{0,64},{8,72},{16,80},{24,88},{32,96},{40,104},{48,112},{56,120},{... | collective-permute-start | bytes 98312 | tf_op jit(solution)/shard_map/ppermute | solution.py:12
  52.5 14.8 %copy-start.1 = (f32[128,16,512]{2,0,1:T(8,128)S(1)}, f32[128,16,512]{2,0,1:T(8,128)}, u32[]{:S(2)}) copy-start(f32[128,16,512]{2,0,1:T(8,128)} %convolution_add_fusion) | copy-start | bytes 12582916
  60.2 5.8 %collective-permute-start.6 = (f32[16,512]{1,0:T(8,128)S(1)}, f32[16,512]{1,0:T(8,128)S(1)}, u32[]{:S(2)}, u32[]{:S(2)}) collective-permute-start(f32[16,512]{1,0:T(8,128)S(1)} %fusion.42), channel_id=1, source_target_pairs={{0,128},{8,136},{16,144},{24,152},{32,160},{40,168},{48,176},{56,1... | collective-permute-start | bytes 98312 | tf_op jit(solution)/shard_map/ppermute | solution.py:12
  64.6 10.0 %copy-start.3 = (bf16[128,512]{1,0:T(8,128)(2,1)S(1)}, bf16[128,512]{1,0:T(8,128)(2,1)}, u32[]{:S(2)}) copy-start(bf16[128,512]{1,0:T(8,128)(2,1)} %param.8) | copy-start | bytes 393220
  64.6 10.0 %copy-start.7 = (f32[512]{0:T(512)S(1)}, f32[512]{0:T(512)}, u32[]{:S(2)}) copy-start(f32[512]{0:T(512)} %param.11) | copy-start | bytes 6148
  66.1 7.3 %collective-permute-start.7 = (f32[16,512]{1,0:T(8,128)S(1)}, f32[16,512]{1,0:T(8,128)S(1)}, u32[]{:S(2)}, u32[]{:S(2)}) collective-permute-start(f32[16,512]{1,0:T(8,128)S(1)} %get-tuple-element.30), channel_id=1, source_target_pairs={{0,256},{8,264},{16,272},{24,280},{32,288},{40,296},{48,304},{56,3... | collective-permute-start | bytes 98312 | tf_op jit(solution)/shard_map/ppermute | solution.py:12
  68.3 17.9 %copy-start.8 = (f32[512]{0:T(512)S(1)}, f32[512]{0:T(512)}, u32[]{:S(2)}) copy-start(f32[512]{0:T(512)} %param.15) | copy-start | bytes 6148
  76.5 9.7 %all-to-all-start = ((f32[8,1,128]{2,1,0:T(1,128)}), f32[8,1,128]{2,1,0:T(1,128)S(1)}, u32[]{:S(2)}, u32[]{:S(2)}) async-start(f32[8,1,128]{2,1,0:T(1,128)} %broadcast_in_dim.12), calls=%async_computation | async-start | bytes 8192 | tf_op jit(solution)/shard_map/all_to_all | solution.py:123

commit v8 on v7

--- a/solution.py
+++ b/solution.py
@@ -55,27 +55,36 @@
     keys_values = jnp.stack([key_rows, value_rows])
 
     before_previous = jnp.zeros_like(previous_state)
+    previous_local = local_part = None
     span = 1
     while span < ctx_count:
         sent = previous_state + before_previous
-        got = shifted(sent, "ctx", span)
+        reach = 4 if span * 4 == ctx_count else 2
+        got = jnp.zeros_like(sent)
+        for step in range(1, reach):
+            decay = jnp.exp(-rates * float(row_count * span * step))
+            got = got + decay * shifted(sent, "ctx", step * span)
         if span == 1:
             got, keys_values = lax.optimization_barrier((got, keys_values))
             lookback = shifted(keys_values, "ctx", 1)
-        if span == 4:
-            got, lookback = lax.optimization_barrier((got, lookback))
+        if span == ctx_count // 16:
+            got, lookback, previous_prefix = lax.optimization_barrier(
+                (got, lookback, previous_prefix)
+            )
+            previous_local = jnp.sum(fall * previous_prefix, axis=1)
         if span == ctx_count // 8:
-            got, previous_prefix = lax.optimization_barrier((got, previous_prefix))
-            previous_local = jnp.sum(fall * previous_prefix, axis=1)
-        if span == ctx_count // 4:
             got, previous_local, own_prefix = lax.optimization_barrier(
                 (got, previous_local, own_prefix)
             )
             local_part = jnp.sum(fall * own_prefix, axis=1)
-        if span == ctx_count // 2:
+        if span == ctx_count // 4:
             got, local_part = lax.optimization_barrier((got, local_part))
-        before_previous = before_previous + jnp.exp(-rates * float(row_count * span)) * got
-        span *= 2
+        before_previous = before_previous + got
+        span *= reach
+    if previous_local is None:
+        previous_local = jnp.sum(fall * previous_prefix, axis=1)
+    if local_part is None:
+        local_part = jnp.sum(fall * own_prefix, axis=1)
     before = jnp.exp(-rates * float(row_count)) * (previous_state + before_previous)
     previous_keys = lookback[0]
 

time: 87.9 us -> 86.2 us (0.981)
  waiting for transfers between devices: 35.4 us -> 32.6 us
  starting transfers between devices: 29.5 us -> 30.8 us
    ppermute x8 -> x9, waiting for transfers between devices: 30.3 us -> 27.5 us  [shifted(): return lax.ppermute(block, axis, route)]
    ppermute x8 -> x9, starting transfers between devices: 25.1 us -> 26.3 us  [shifted(): return lax.ppermute(block, axis, route)]
  transfers between devices with their start and end apart: 9 -> 10, of which waited for: 8 -> 9; matrix products, arithmetic and copies ran while one was open for 19% -> 19% of each run, Pallas kernels for 0% -> 0%
where the time goes in v8:
time: 86.2 us; the launch traced here: 85.6 us
  waiting for transfers between devices  32.6 us (38%)
  starting transfers between devices  30.8 us (36%)
  matrix products  10 us (12%)
  other arithmetic  9.66 us (11%)
  local copies, waits for them, and re-layouts  1.44 us (2%)
  between operations  1.06 us (1%)
    ppermute x9, waiting for transfers between devices, shifted(): return lax.ppermute(block, axis, route)  27.5 us
    ppermute x9, starting transfers between devices, shifted(): return lax.ppermute(block, axis, route)  26.3 us
    all_to_all x1, waiting for transfers between devices, per_device(): energy = jnp.sum(lax.all_to_all(spread, 'ch', 0, 0, tiled=True), axis=0)  5.08 us
    dot_general x2, matrix products, block_terms(): jnp.einsum('ts,src->trc', lower, lifted_lo, preferred_element_type=jnp.fl...  4.8 us
    dot_general x2, matrix products, block_terms(): jnp.einsum('ts,src->trc', lower, lifted_hi, preferred_element_type=jnp.fl...  4.73 us
    all_to_all x1, starting transfers between devices, per_device(): energy = jnp.sum(lax.all_to_all(spread, 'ch', 0, 0, tiled=True), axis=0)  4.46 us
    reduce_sum x1, other arithmetic, per_device(): previous_local = jnp.sum(fall * previous_prefix, axis=1)  3.25 us
  transfers between devices with their start and end apart: 10, of which 9 were waited for; matrix products, arithmetic and copies ran while one was open for 19% of the time, Pallas kernels for 0%

profile of v8, /device:TPU:6, one launch (start us, length us, event | category | flops | bytes accessed | tf_op | source)
XLA Modules:
  0.0 85.6 jit_solution(11021943150543581658)
XLA Ops:
  0.7 4.0 %collective-permute-start = (bf16[128,512]{1,0:T(8,128)(2,1)}, bf16[128,512]{1,0:T(8,128)(2,1)S(1)}, u32[]{:S(2)}, u32[]{:S(2)}) collective-permute-start(bf16[128,512]{1,0:T(8,128)(2,1)} %param.8), channel_id=1, source_target_pairs={{0,8},{8,16},{16,24},{24,32},{32,40},{40,48},{48,56},{56,64},{64,7... | collective-permute-start | bytes 393224 | tf_op jit(solution)/shard_map/ppermute | solution.py:12
  4.6 0.9 %convert_element_type.70 = f32[128,512]{1,0:T(8,128)S(1)} convert(bf16[128,512]{1,0:T(8,128)(2,1)} %param.8) | non-fusion elementwise | flops 65536 | bytes 393216 | tf_op jit(solution)/shard_map/convert_element_type | solution.py:46
  5.6 0.8 multiply_exponential_fusion.1
  6.4 1.6 %fusion.7 = f32[128,16,512]{2,0,1:T(8,128)S(1)} fusion(f32[128,512]{1,0:T(8,128)S(1)} %convert_element_type.70, f32[16,512]{1,0:T(8,128)} %bitcast.58), kind=kOutput, calls=%fused_computation.18 | convolution fusion | flops 272646144 | bytes 4489216 | tf_op jit(solution)/shard_map/ts,src->trc/dot_general | solution.py:32
  8.0 3.5 %convolution_add_fusion = f32[128,16,512]{2,0,1:T(8,128)} fusion(f32[128,16,512]{2,0,1:T(8,128)S(1)} %fusion.7, f32[128,512]{1,0:T(8,128)S(1)} %convert_element_type.70, f32[16,512]{1,0:T(8,128)S(1)} %bitcast.59), kind=kOutput, calls=%fused_computation.15 | convolution fusion | flops 274743296 | bytes 8683520 | tf_op jit(solution)/shard_map/ts,src->trc/dot_general | solution.py:34
  11.7 4.4 %collective-permute-done = bf16[128,512]{1,0:T(8,128)(2,1)S(1)} collective-permute-done((bf16[128,512]{1,0:T(8,128)(2,1)}, bf16[128,512]{1,0:T(8,128)(2,1)S(1)}, u32[]{:S(2)}, u32[]{:S(2)}) %collective-permute-start) | collective-permute-done | bytes 131104 | tf_op jit(solution)/shard_map/ppermute | solution.py:12
  16.2 0.3 multiply_reduce_fusion.4
  16.6 1.9 %collective-permute-start.1 = (f32[16,512]{1,0:T(8,128)S(1)}, f32[16,512]{1,0:T(8,128)S(1)}, u32[]{:S(2)}, u32[]{:S(2)}) collective-permute-start(f32[16,512]{1,0:T(8,128)S(1)} %exponential_multiply_fusion.3), channel_id=1, source_target_pairs={{0,8},{8,16},{16,24},{24,32},{32,40},{40,48},{48,56},{56,64},{64,7... | collective-permute-start | bytes 98312 | tf_op jit(solution)/shard_map/ppermute | solution.py:12
  18.8 5.7 %collective-permute-done.1 = f32[16,512]{1,0:T(8,128)S(1)} collective-permute-done((f32[16,512]{1,0:T(8,128)S(1)}, f32[16,512]{1,0:T(8,128)S(1)}, u32[]{:S(2)}, u32[]{:S(2)}) %collective-permute-start.1) | collective-permute-done | bytes 32800 | tf_op jit(solution)/shard_map/ppermute | solution.py:12
  24.6 1.9 %collective-permute-start.2 = (f32[16,512]{1,0:T(8,128)S(1)}, f32[16,512]{1,0:T(8,128)S(1)}, u32[]{:S(2)}, u32[]{:S(2)}) collective-permute-start(f32[16,512]{1,0:T(8,128)S(1)} %add.76), channel_id=1, source_target_pairs={{0,16},{8,24},{16,32},{24,40},{32,48},{40,56},{48,64},{56,72},{64,... | collective-permute-start | bytes 98312 | tf_op jit(solution)/shard_map/ppermute | solution.py:12
  26.5 1.3 %fusion.5 = f32[128,16,512]{2,0,1:T(8,128)S(1)} fusion(f32[128,512]{1,0:T(8,128)S(1)} %convert_element_type.67, f32[16,512]{1,0:T(8,128)S(1)} %bitcast.61), kind=kOutput, calls=%fused_computation.17 | convolution fusion | flops 273694720 | bytes 4489216 | tf_op jit(solution)/shard_map/ts,src->trc/dot_general | solution.py:34
  27.9 1.9 %collective-permute-start.4 = (bf16[2,128,512]{2,1,0:T(8,128)(2,1)S(1)}, bf16[2,128,512]{2,1,0:T(8,128)(2,1)S(1)}, u32[]{:S(2)}, u32[]{:S(2)}) collective-permute-start(bf16[2,128,512]{2,1,0:T(8,128)(2,1)S(1)} %pad_maximum_fusion), channel_id=1, source_target_pairs={{0,8},{8,16},{16,24},{24,32},{32,40},{40,48},{48,56},{56,64},{64,7... | collective-permute-start | bytes 786440 | tf_op jit(solution)/shard_map/ppermute | solution.py:12
  29.8 3.7 %collective-permute-done.2 = f32[16,512]{1,0:T(8,128)S(1)} collective-permute-done((f32[16,512]{1,0:T(8,128)S(1)}, f32[16,512]{1,0:T(8,128)S(1)}, u32[]{:S(2)}, u32[]{:S(2)}) %collective-permute-start.2) | collective-permute-done | bytes 32800 | tf_op jit(solution)/shard_map/ppermute | solution.py:12
  33.5 5.2 %collective-permute-start.3 = (f32[16,512]{1,0:T(8,128)S(1)}, f32[16,512]{1,0:T(8,128)S(1)}, u32[]{:S(2)}, u32[]{:S(2)}) collective-permute-start(f32[16,512]{1,0:T(8,128)S(1)} %fusion.41), channel_id=1, source_target_pairs={{0,32},{8,40},{16,48},{24,56},{32,64},{40,72},{48,80},{56,88},{64,... | collective-permute-start | bytes 98312 | tf_op jit(solution)/shard_map/ppermute | solution.py:12
  38.8 3.2 %convolution_add_fusion.1 = f32[128,16,512]{2,0,1:T(8,128)} fusion(f32[128,16,512]{2,0,1:T(8,128)S(1)} %fusion.5, f32[128,512]{1,0:T(8,128)S(1)} %convert_element_type.67, f32[16,512]{1,0:T(8,128)S(1)} %bitcast.62), kind=kOutput, calls=%fused_computation.16 | convolution fusion | flops 273694720 | bytes 8683520 | tf_op jit(solution)/shard_map/ts,src->trc/dot_general | solution.py:32
  41.9 2.8 %collective-permute-done.3 = f32[16,512]{1,0:T(8,128)S(1)} collective-permute-done((f32[16,512]{1,0:T(8,128)S(1)}, f32[16,512]{1,0:T(8,128)S(1)}, u32[]{:S(2)}, u32[]{:S(2)}) %collective-permute-start.3) | collective-permute-done | bytes 32800 | tf_op jit(solution)/shard_map/ppermute | solution.py:12
  44.8 7.5 %collective-permute-start.5 = (f32[16,512]{1,0:T(8,128)S(1)}, f32[16,512]{1,0:T(8,128)S(1)}, u32[]{:S(2)}, u32[]{:S(2)}) collective-permute-start(f32[16,512]{1,0:T(8,128)S(1)} %get-tuple-element.30), channel_id=1, source_target_pairs={{0,64},{8,72},{16,80},{24,88},{32,96},{40,104},{48,112},{56,120},{... | collective-permute-start | bytes 98312 | tf_op jit(solution)/shard_map/ppermute | solution.py:12
  52.6 3.3 %multiply_reduce_fusion.3 = f32[128,512]{1,0:T(8,128)S(1)} fusion(f32[128,16,512]{2,0,1:T(8,128)} %convolution_add_fusion.1, f32[128]{0:T(128)S(1)} %iota_negate_fusion, f32[16,512]{1,0:T(8,128)S(1)} %get-tuple-element.34, f32[16,512]{1,0:T(8,128)S(1)} %bitcast.63), kind=kLoop, calls=%fused_computation.9 | loop fusion | flops 4128768 | bytes 4522496 | tf_op jit(solution)/shard_map/reduce_sum | solution.py:74
  56.2 4.0 %collective-permute-done.5 = f32[16,512]{1,0:T(8,128)S(1)} collective-permute-done((f32[16,512]{1,0:T(8,128)S(1)}, f32[16,512]{1,0:T(8,128)S(1)}, u32[]{:S(2)}, u32[]{:S(2)}) %collective-permute-start.5) | collective-permute-done | bytes 32800 | tf_op jit(solution)/shard_map/ppermute | solution.py:12
  60.3 1.3 %collective-permute-start.6 = (f32[16,512]{1,0:T(8,128)S(1)}, f32[16,512]{1,0:T(8,128)S(1)}, u32[]{:S(2)}, u32[]{:S(2)}) collective-permute-start(f32[16,512]{1,0:T(8,128)S(1)} %get-tuple-element.28), channel_id=1, source_target_pairs={{0,128},{8,136},{16,144},{24,152},{32,160},{40,168},{48,176},{56,1... | collective-permute-start | bytes 98312 | tf_op jit(solution)/shard_map/ppermute | solution.py:12
  61.6 1.3 %collective-permute-start.7 = (f32[16,512]{1,0:T(8,128)S(1)}, f32[16,512]{1,0:T(8,128)S(1)}, u32[]{:S(2)}, u32[]{:S(2)}) collective-permute-start(f32[16,512]{1,0:T(8,128)S(1)} %get-tuple-element.28), channel_id=1, source_target_pairs={{0,256},{8,264},{16,272},{24,280},{32,288},{40,296},{48,304},{56,3... | collective-permute-start | bytes 98312 | tf_op jit(solution)/shard_map/ppermute | solution.py:12
  62.9 1.3 %collective-permute-start.8 = (f32[16,512]{1,0:T(8,128)S(1)}, f32[16,512]{1,0:T(8,128)S(1)}, u32[]{:S(2)}, u32[]{:S(2)}) collective-permute-start(f32[16,512]{1,0:T(8,128)S(1)} %get-tuple-element.28), channel_id=1, source_target_pairs={{0,384},{8,392},{16,400},{24,408},{32,416},{40,424},{48,432},{56,4... | collective-permute-start | bytes 98312 | tf_op jit(solution)/shard_map/ppermute | solution.py:12
  64.2 0.9 %multiply_reduce_fusion.2 = f32[128,512]{1,0:T(8,128)S(1)} fusion(f32[128,16,512]{2,0,1:T(8,128)S(1)} %copy-done.1, f32[128]{0:T(128)S(1)} %iota_negate_fusion, f32[16,512]{1,0:T(8,128)S(1)} %get-tuple-element.34, f32[16,512]{1,0:T(8,128)S(1)} %bitcast.64), kind=kLoop, calls=%fused_computation.8 | loop fusion | flops 4128768 | bytes 4522496 | tf_op jit(solution)/shard_map/reduce_sum | solution.py:79
  65.1 1.0 %collective-permute-done.6 = f32[16,512]{1,0:T(8,128)S(1)} collective-permute-done((f32[16,512]{1,0:T(8,128)S(1)}, f32[16,512]{1,0:T(8,128)S(1)}, u32[]{:S(2)}, u32[]{:S(2)}) %collective-permute-start.6) | collective-permute-done | bytes 32800 | tf_op jit(solution)/shard_map/ppermute | solution.py:12
  66.1 2.8 %collective-permute-done.7 = f32[16,512]{1,0:T(8,128)S(1)} collective-permute-done((f32[16,512]{1,0:T(8,128)S(1)}, f32[16,512]{1,0:T(8,128)S(1)}, u32[]{:S(2)}, u32[]{:S(2)}) %collective-permute-start.7) | collective-permute-done | bytes 32800 | tf_op jit(solution)/shard_map/ppermute | solution.py:12
  68.9 3.1 %collective-permute-done.8 = f32[16,512]{1,0:T(8,128)S(1)} collective-permute-done((f32[16,512]{1,0:T(8,128)S(1)}, f32[16,512]{1,0:T(8,128)S(1)}, u32[]{:S(2)}, u32[]{:S(2)}) %collective-permute-start.8) | collective-permute-done | bytes 32800 | tf_op jit(solution)/shard_map/ppermute | solution.py:12
  72.0 1.2 %multiply_reduce_fusion = (f32[128,512]{1,0:T(8,128)S(1)}, f32[128,512]{1,0:T(8,128)S(1)}) fusion(f32[16,512]{1,0:T(8,128)S(1)} %get-tuple-element.33, f32[128]{0:T(128)S(1)} %iota_negate_fusion, f32[16,512]{1,0:T(8,128)S(1)} %get-tuple-element.34, f32[16,512]{1,0:T(8,128)S(1)} %bitcast.65, f32[16,512]{1,0:T(8,128)S(1)} %get-tuple-element.32), kind=kLoop, calls=%fused_computation.6 | loop fusion | flops 6160384 | bytes 655872 | tf_op jit(solution)/shard_map/reduce_sum | solution.py:97
  73.3 0.8 multiply_convert_fusion
  74.5 0.6 broadcast_in_dim.12
  75.1 4.5 %all-to-all-start = ((f32[8,1,128]{2,1,0:T(1,128)}), f32[8,1,128]{2,1,0:T(1,128)S(1)}, u32[]{:S(2)}, u32[]{:S(2)}) async-start(f32[8,1,128]{2,1,0:T(1,128)} %broadcast_in_dim.12), calls=%async_computation | async-start | bytes 8192 | tf_op jit(solution)/shard_map/all_to_all | solution.py:132
  79.7 5.1 %all-to-all-done = f32[8,1,128]{2,1,0:T(1,128)S(1)} async-done(((f32[8,1,128]{2,1,0:T(1,128)}), f32[8,1,128]{2,1,0:T(1,128)S(1)}, u32[]{:S(2)}, u32[]{:S(2)}) %all-to-all-start) | async-done | bytes 4128 | tf_op jit(solution)/shard_map/all_to_all | solution.py:132
  84.8 0.8 divide_convert_fusion
  (50 shorter events, 2.0 us)
Async XLA Ops:
  0.6 55.2 %copy-start = (bf16[128,512]{1,0:T(8,128)(2,1)S(1)}, bf16[128,512]{1,0:T(8,128)(2,1)}, u32[]{:S(2)}) copy-start(bf16[128,512]{1,0:T(8,128)(2,1)} %param.12) | copy-start | bytes 393220
  0.6 7.4 %copy-start.2 = (f32[512,16]{0,1:T(8,128)S(1)}, f32[512,16]{0,1:T(8,128)}, u32[]{:S(2)}) copy-start(f32[512,16]{0,1:T(8,128)} %param.10) | copy-start | bytes 98308
  0.7 15.5 %collective-permute-start = (bf16[128,512]{1,0:T(8,128)(2,1)}, bf16[128,512]{1,0:T(8,128)(2,1)S(1)}, u32[]{:S(2)}, u32[]{:S(2)}) collective-permute-start(bf16[128,512]{1,0:T(8,128)(2,1)} %param.8), channel_id=1, source_target_pairs={{0,8},{8,16},{16,24},{24,32},{32,40},{40,48},{48,56},{56,64},{64,7... | collective-permute-start | bytes 393224 | tf_op jit(solution)/shard_map/ppermute | solution.py:12
  8.0 3.6 %copy-start.4 = (bf16[128,512]{1,0:T(8,128)(2,1)S(1)}, bf16[128,512]{1,0:T(8,128)(2,1)}, u32[]{:S(2)}) copy-start(bf16[128,512]{1,0:T(8,128)(2,1)} %param.14) | copy-start | bytes 393220
  8.0 3.6 %copy-start.5 = (bf16[128,512]{1,0:T(8,128)(2,1)S(1)}, bf16[128,512]{1,0:T(8,128)(2,1)}, u32[]{:S(2)}) copy-start(bf16[128,512]{1,0:T(8,128)(2,1)} %param.13) | copy-start | bytes 393220
  16.6 7.9 %collective-permute-start.1 = (f32[16,512]{1,0:T(8,128)S(1)}, f32[16,512]{1,0:T(8,128)S(1)}, u32[]{:S(2)}, u32[]{:S(2)}) collective-permute-start(f32[16,512]{1,0:T(8,128)S(1)} %exponential_multiply_fusion.3), channel_id=1, source_target_pairs={{0,8},{8,16},{16,24},{24,32},{32,40},{40,48},{48,56},{56,64},{64,7... | collective-permute-start | bytes 98312 | tf_op jit(solution)/shard_map/ppermute | solution.py:12
  24.6 8.9 %collective-permute-start.2 = (f32[16,512]{1,0:T(8,128)S(1)}, f32[16,512]{1,0:T(8,128)S(1)}, u32[]{:S(2)}, u32[]{:S(2)}) collective-permute-start(f32[16,512]{1,0:T(8,128)S(1)} %add.76), channel_id=1, source_target_pairs={{0,16},{8,24},{16,32},{24,40},{32,48},{40,56},{48,64},{56,72},{64,... | collective-permute-start | bytes 98312 | tf_op jit(solution)/shard_map/ppermute | solution.py:12
  27.9 16.9 %collective-permute-start.4 = (bf16[2,128,512]{2,1,0:T(8,128)(2,1)S(1)}, bf16[2,128,512]{2,1,0:T(8,128)(2,1)S(1)}, u32[]{:S(2)}, u32[]{:S(2)}) collective-permute-start(bf16[2,128,512]{2,1,0:T(8,128)(2,1)S(1)} %pad_maximum_fusion), channel_id=1, source_target_pairs={{0,8},{8,16},{16,24},{24,32},{32,40},{40,48},{48,56},{56,64},{64,7... | collective-permute-start | bytes 786440 | tf_op jit(solution)/shard_map/ppermute | solution.py:12
  33.5 11.2 %copy-start.6 = (f32[512,16]{0,1:T(8,128)S(1)}, f32[512,16]{0,1:T(8,128)}, u32[]{:S(2)}) copy-start(f32[512,16]{0,1:T(8,128)} %param.9) | copy-start | bytes 98308
  33.5 11.2 %collective-permute-start.3 = (f32[16,512]{1,0:T(8,128)S(1)}, f32[16,512]{1,0:T(8,128)S(1)}, u32[]{:S(2)}, u32[]{:S(2)}) collective-permute-start(f32[16,512]{1,0:T(8,128)S(1)} %fusion.41), channel_id=1, source_target_pairs={{0,32},{8,40},{16,48},{24,56},{32,64},{40,72},{48,80},{56,88},{64,... | collective-permute-start | bytes 98312 | tf_op jit(solution)/shard_map/ppermute | solution.py:12
  44.8 15.5 %collective-permute-start.5 = (f32[16,512]{1,0:T(8,128)S(1)}, f32[16,512]{1,0:T(8,128)S(1)}, u32[]{:S(2)}, u32[]{:S(2)}) collective-permute-start(f32[16,512]{1,0:T(8,128)S(1)} %get-tuple-element.30), channel_id=1, source_target_pairs={{0,64},{8,72},{16,80},{24,88},{32,96},{40,104},{48,112},{56,120},{... | collective-permute-start | bytes 98312 | tf_op jit(solution)/shard_map/ppermute | solution.py:12
  52.6 11.6 %copy-start.1 = (f32[128,16,512]{2,0,1:T(8,128)S(1)}, f32[128,16,512]{2,0,1:T(8,128)}, u32[]{:S(2)}) copy-start(f32[128,16,512]{2,0,1:T(8,128)} %convolution_add_fusion) | copy-start | bytes 12582916
  55.9 17.4 %copy-start.3 = (bf16[128,512]{1,0:T(8,128)(2,1)S(1)}, bf16[128,512]{1,0:T(8,128)(2,1)}, u32[]{:S(2)}) copy-start(bf16[128,512]{1,0:T(8,128)(2,1)} %param.8) | copy-start | bytes 393220
  55.9 17.4 %copy-start.7 = (f32[512]{0:T(512)S(1)}, f32[512]{0:T(512)}, u32[]{:S(2)}) copy-start(f32[512]{0:T(512)} %param.11) | copy-start | bytes 6148
  60.3 5.8 %collective-permute-start.6 = (f32[16,512]{1,0:T(8,128)S(1)}, f32[16,512]{1,0:T(8,128)S(1)}, u32[]{:S(2)}, u32[]{:S(2)}) collective-permute-start(f32[16,512]{1,0:T(8,128)S(1)} %get-tuple-element.28), channel_id=1, source_target_pairs={{0,128},{8,136},{16,144},{24,152},{32,160},{40,168},{48,176},{56,1... | collective-permute-start | bytes 98312 | tf_op jit(solution)/shard_map/ppermute | solution.py:12
  61.6 7.3 %collective-permute-start.7 = (f32[16,512]{1,0:T(8,128)S(1)}, f32[16,512]{1,0:T(8,128)S(1)}, u32[]{:S(2)}, u32[]{:S(2)}) collective-permute-start(f32[16,512]{1,0:T(8,128)S(1)} %get-tuple-element.28), channel_id=1, source_target_pairs={{0,256},{8,264},{16,272},{24,280},{32,288},{40,296},{48,304},{56,3... | collective-permute-start | bytes 98312 | tf_op jit(solution)/shard_map/ppermute | solution.py:12
  62.9 9.1 %collective-permute-start.8 = (f32[16,512]{1,0:T(8,128)S(1)}, f32[16,512]{1,0:T(8,128)S(1)}, u32[]{:S(2)}, u32[]{:S(2)}) collective-permute-start(f32[16,512]{1,0:T(8,128)S(1)} %get-tuple-element.28), channel_id=1, source_target_pairs={{0,384},{8,392},{16,400},{24,408},{32,416},{40,424},{48,432},{56,4... | collective-permute-start | bytes 98312 | tf_op jit(solution)/shard_map/ppermute | solution.py:12
  65.1 19.7 %copy-start.8 = (f32[512]{0:T(512)S(1)}, f32[512]{0:T(512)}, u32[]{:S(2)}) copy-start(f32[512]{0:T(512)} %param.15) | copy-start | bytes 6148
  75.1 9.7 %all-to-all-start = ((f32[8,1,128]{2,1,0:T(1,128)}), f32[8,1,128]{2,1,0:T(1,128)S(1)}, u32[]{:S(2)}, u32[]{:S(2)}) async-start(f32[8,1,128]{2,1,0:T(1,128)} %broadcast_in_dim.12), calls=%async_computation | async-start | bytes 8192 | tf_op jit(solution)/shard_map/all_to_all | solution.py:132

commit v9 on v8

--- a/solution.py
+++ b/solution.py
@@ -59,27 +59,28 @@
     span = 1
     while span < ctx_count:
         sent = previous_state + before_previous
-        reach = 4 if span * 4 == ctx_count else 2
-        got = jnp.zeros_like(sent)
-        for step in range(1, reach):
-            decay = jnp.exp(-rates * float(row_count * span * step))
-            got = got + decay * shifted(sent, "ctx", step * span)
+        reach = 4 if span >= 4 and span * 4 <= ctx_count else 2
+        parts = [shifted(sent, "ctx", step * span) for step in range(1, reach)]
+        got = parts[0]
         if span == 1:
             got, keys_values = lax.optimization_barrier((got, keys_values))
             lookback = shifted(keys_values, "ctx", 1)
-        if span == ctx_count // 16:
+        if span == ctx_count // 32:
             got, lookback, previous_prefix = lax.optimization_barrier(
                 (got, lookback, previous_prefix)
             )
             previous_local = jnp.sum(fall * previous_prefix, axis=1)
-        if span == ctx_count // 8:
+        if span == ctx_count // 16:
             got, previous_local, own_prefix = lax.optimization_barrier(
                 (got, previous_local, own_prefix)
             )
             local_part = jnp.sum(fall * own_prefix, axis=1)
         if span == ctx_count // 4:
             got, local_part = lax.optimization_barrier((got, local_part))
-        before_previous = before_previous + got
+        parts[0] = got
+        for step in range(1, reach):
+            decay = jnp.exp(-rates * float(row_count * span * step))
+            before_previous = before_previous + decay * parts[step - 1]
         span *= reach
     if previous_local is None:
         previous_local = jnp.sum(fall * previous_prefix, axis=1)

time: 86.2 us -> 87.8 us (1.019)
  starting transfers between devices: 30.8 us -> 33.4 us
  waiting for transfers between devices: 32.6 us -> 31.7 us
    ppermute x9 -> x10, starting transfers between devices: 26.3 us -> 28.9 us  [shifted(): return lax.ppermute(block, axis, route)]
    ppermute x9 -> x10, waiting for transfers between devices: 27.5 us -> 26.6 us  [shifted(): return lax.ppermute(block, axis, route)]
  transfers between devices with their start and end apart: 10 -> 11, of which waited for: 9 -> 10; matrix products, arithmetic and copies ran while one was open for 19% -> 19% of each run, Pallas kernels for 0% -> 0%
where the time goes in v9:
time: 87.8 us; the launch traced here: 87.3 us
  starting transfers between devices  33.4 us (38%)
  waiting for transfers between devices  31.7 us (36%)
  matrix products  10 us (11%)
  other arithmetic  9.67 us (11%)
  local copies, waits for them, and re-layouts  1.44 us (2%)
  between operations  1.03 us (1%)
    ppermute x10, starting transfers between devices, shifted(): return lax.ppermute(block, axis, route)  28.9 us
    ppermute x10, waiting for transfers between devices, shifted(): return lax.ppermute(block, axis, route)  26.6 us
    all_to_all x1, waiting for transfers between devices, per_device(): energy = jnp.sum(lax.all_to_all(spread, 'ch', 0, 0, tiled=True), axis=0)  5.08 us
    dot_general x2, matrix products, block_terms(): jnp.einsum('ts,src->trc', lower, lifted_lo, preferred_element_type=jnp.fl...  4.8 us
    dot_general x2, matrix products, block_terms(): jnp.einsum('ts,src->trc', lower, lifted_hi, preferred_element_type=jnp.fl...  4.73 us
    all_to_all x1, starting transfers between devices, per_device(): energy = jnp.sum(lax.all_to_all(spread, 'ch', 0, 0, tiled=True), axis=0)  4.5 us
    reduce_sum x1, other arithmetic, per_device(): previous_local = jnp.sum(fall * previous_prefix, axis=1)  3.26 us
  transfers between devices with their start and end apart: 11, of which 10 were waited for; matrix products, arithmetic and copies ran while one was open for 19% of the time, Pallas kernels for 0%

profile of v9, /device:TPU:6, one launch (start us, length us, event | category | flops | bytes accessed | tf_op | source)
XLA Modules:
  0.0 87.3 jit_solution(3936346573926425777)
XLA Ops:
  0.7 4.0 %collective-permute-start = (bf16[128,512]{1,0:T(8,128)(2,1)}, bf16[128,512]{1,0:T(8,128)(2,1)S(1)}, u32[]{:S(2)}, u32[]{:S(2)}) collective-permute-start(bf16[128,512]{1,0:T(8,128)(2,1)} %param.8), channel_id=1, source_target_pairs={{0,8},{8,16},{16,24},{24,32},{32,40},{40,48},{48,56},{56,64},{64,7... | collective-permute-start | bytes 393224 | tf_op jit(solution)/shard_map/ppermute | solution.py:12
  4.6 1.0 %convert_element_type.70 = f32[128,512]{1,0:T(8,128)S(1)} convert(bf16[128,512]{1,0:T(8,128)(2,1)} %param.8) | non-fusion elementwise | flops 65536 | bytes 393216 | tf_op jit(solution)/shard_map/convert_element_type | solution.py:46
  5.6 0.8 multiply_exponential_fusion.1
  6.5 1.6 %fusion.7 = f32[128,16,512]{2,0,1:T(8,128)S(1)} fusion(f32[128,512]{1,0:T(8,128)S(1)} %convert_element_type.70, f32[16,512]{1,0:T(8,128)} %bitcast.57), kind=kOutput, calls=%fused_computation.18 | convolution fusion | flops 272646144 | bytes 4489216 | tf_op jit(solution)/shard_map/ts,src->trc/dot_general | solution.py:32
  8.1 3.5 %convolution_add_fusion = f32[128,16,512]{2,0,1:T(8,128)} fusion(f32[128,16,512]{2,0,1:T(8,128)S(1)} %fusion.7, f32[128,512]{1,0:T(8,128)S(1)} %convert_element_type.70, f32[16,512]{1,0:T(8,128)S(1)} %bitcast.58), kind=kOutput, calls=%fused_computation.15 | convolution fusion | flops 274743296 | bytes 8683520 | tf_op jit(solution)/shard_map/ts,src->trc/dot_general | solution.py:34
  12.0 4.1 %collective-permute-done = bf16[128,512]{1,0:T(8,128)(2,1)S(1)} collective-permute-done((bf16[128,512]{1,0:T(8,128)(2,1)}, bf16[128,512]{1,0:T(8,128)(2,1)S(1)}, u32[]{:S(2)}, u32[]{:S(2)}) %collective-permute-start) | collective-permute-done | bytes 131104 | tf_op jit(solution)/shard_map/ppermute | solution.py:12
  16.7 1.9 %collective-permute-start.1 = (f32[16,512]{1,0:T(8,128)S(1)}, f32[16,512]{1,0:T(8,128)S(1)}, u32[]{:S(2)}, u32[]{:S(2)}) collective-permute-start(f32[16,512]{1,0:T(8,128)S(1)} %get-tuple-element.33), channel_id=1, source_target_pairs={{0,8},{8,16},{16,24},{24,32},{32,40},{40,48},{48,56},{56,64},{64,7... | collective-permute-start | bytes 98312 | tf_op jit(solution)/shard_map/ppermute | solution.py:12
  18.6 1.3 %fusion.5 = f32[128,16,512]{2,0,1:T(8,128)S(1)} fusion(f32[128,512]{1,0:T(8,128)S(1)} %convert_element_type.67, f32[16,512]{1,0:T(8,128)S(1)} %bitcast.60), kind=kOutput, calls=%fused_computation.17 | convolution fusion | flops 273694720 | bytes 4489216 | tf_op jit(solution)/shard_map/ts,src->trc/dot_general | solution.py:34
  19.9 4.6 %collective-permute-done.1 = f32[16,512]{1,0:T(8,128)S(1)} collective-permute-done((f32[16,512]{1,0:T(8,128)S(1)}, f32[16,512]{1,0:T(8,128)S(1)}, u32[]{:S(2)}, u32[]{:S(2)}) %collective-permute-start.1) | collective-permute-done | bytes 32800 | tf_op jit(solution)/shard_map/ppermute | solution.py:12
  24.6 1.9 %collective-permute-start.2 = (f32[16,512]{1,0:T(8,128)S(1)}, f32[16,512]{1,0:T(8,128)S(1)}, u32[]{:S(2)}, u32[]{:S(2)}) collective-permute-start(f32[16,512]{1,0:T(8,128)S(1)} %fusion.39), channel_id=1, source_target_pairs={{0,16},{8,24},{16,32},{24,40},{32,48},{40,56},{48,64},{56,72},{64,... | collective-permute-start | bytes 98312 | tf_op jit(solution)/shard_map/ppermute | solution.py:12
  26.5 2.1 %collective-permute-start.3 = (bf16[2,128,512]{2,1,0:T(8,128)(2,1)S(1)}, bf16[2,128,512]{2,1,0:T(8,128)(2,1)S(1)}, u32[]{:S(2)}, u32[]{:S(2)}) collective-permute-start(bf16[2,128,512]{2,1,0:T(8,128)(2,1)S(1)} %pad_maximum_fusion), channel_id=1, source_target_pairs={{0,8},{8,16},{16,24},{24,32},{32,40},{40,48},{48,56},{56,64},{64,7... | collective-permute-start | bytes 786440 | tf_op jit(solution)/shard_map/ppermute | solution.py:12
  28.6 3.2 %convolution_add_fusion.1 = f32[128,16,512]{2,0,1:T(8,128)} fusion(f32[128,16,512]{2,0,1:T(8,128)S(1)} %fusion.5, f32[128,512]{1,0:T(8,128)S(1)} %convert_element_type.67, f32[16,512]{1,0:T(8,128)S(1)} %bitcast.61), kind=kOutput, calls=%fused_computation.16 | convolution fusion | flops 273694720 | bytes 8683520 | tf_op jit(solution)/shard_map/ts,src->trc/dot_general | solution.py:32
  31.8 2.0 %collective-permute-done.2 = f32[16,512]{1,0:T(8,128)S(1)} collective-permute-done((f32[16,512]{1,0:T(8,128)S(1)}, f32[16,512]{1,0:T(8,128)S(1)}, u32[]{:S(2)}, u32[]{:S(2)}) %collective-permute-start.2) | collective-permute-done | bytes 32800 | tf_op jit(solution)/shard_map/ppermute | solution.py:12
  33.8 3.9 %collective-permute-done.3 = bf16[2,128,512]{2,1,0:T(8,128)(2,1)S(1)} collective-permute-done((bf16[2,128,512]{2,1,0:T(8,128)(2,1)S(1)}, bf16[2,128,512]{2,1,0:T(8,128)(2,1)S(1)}, u32[]{:S(2)}, u32[]{:S(2)}) %collective-permute-start.3) | collective-permute-done | bytes 262176 | tf_op jit(solution)/shard_map/ppermute | solution.py:12
  37.7 5.9 %collective-permute-start.4 = (f32[16,512]{1,0:T(8,128)S(1)}, f32[16,512]{1,0:T(8,128)S(1)}, u32[]{:S(2)}, u32[]{:S(2)}) collective-permute-start(f32[16,512]{1,0:T(8,128)S(1)} %fusion.40), channel_id=1, source_target_pairs={{0,32},{8,40},{16,48},{24,56},{32,64},{40,72},{48,80},{56,88},{64,... | collective-permute-start | bytes 98312 | tf_op jit(solution)/shard_map/ppermute | solution.py:12
  43.6 7.3 %collective-permute-start.5 = (f32[16,512]{1,0:T(8,128)S(1)}, f32[16,512]{1,0:T(8,128)S(1)}, u32[]{:S(2)}, u32[]{:S(2)}) collective-permute-start(f32[16,512]{1,0:T(8,128)S(1)} %fusion.40), channel_id=1, source_target_pairs={{0,64},{8,72},{16,80},{24,88},{32,96},{40,104},{48,112},{56,120},{... | collective-permute-start | bytes 98312 | tf_op jit(solution)/shard_map/ppermute | solution.py:12
  51.0 1.9 %collective-permute-start.6 = (f32[16,512]{1,0:T(8,128)S(1)}, f32[16,512]{1,0:T(8,128)S(1)}, u32[]{:S(2)}, u32[]{:S(2)}) collective-permute-start(f32[16,512]{1,0:T(8,128)S(1)} %fusion.40), channel_id=1, source_target_pairs={{0,96},{8,104},{16,112},{24,120},{32,128},{40,136},{48,144},{56,15... | collective-permute-start | bytes 98312 | tf_op jit(solution)/shard_map/ppermute | solution.py:12
  53.2 3.3 %multiply_reduce_fusion.3 = f32[128,512]{1,0:T(8,128)S(1)} fusion(f32[128,16,512]{2,0,1:T(8,128)} %convolution_add_fusion.1, f32[128]{0:T(128)S(1)} %iota_negate_fusion, f32[16,512]{1,0:T(8,128)S(1)} %get-tuple-element.32, f32[16,512]{1,0:T(8,128)S(1)} %bitcast.62), kind=kLoop, calls=%fused_computation.9 | loop fusion | flops 4128768 | bytes 4522496 | tf_op jit(solution)/shard_map/reduce_sum | solution.py:72
  56.9 2.3 %collective-permute-done.5 = f32[16,512]{1,0:T(8,128)S(1)} collective-permute-done((f32[16,512]{1,0:T(8,128)S(1)}, f32[16,512]{1,0:T(8,128)S(1)}, u32[]{:S(2)}, u32[]{:S(2)}) %collective-permute-start.5) | collective-permute-done | bytes 32800 | tf_op jit(solution)/shard_map/ppermute | solution.py:12
  59.1 2.8 %collective-permute-done.6 = f32[16,512]{1,0:T(8,128)S(1)} collective-permute-done((f32[16,512]{1,0:T(8,128)S(1)}, f32[16,512]{1,0:T(8,128)S(1)}, u32[]{:S(2)}, u32[]{:S(2)}) %collective-permute-start.6) | collective-permute-done | bytes 32800 | tf_op jit(solution)/shard_map/ppermute | solution.py:12
  62.0 1.3 %collective-permute-start.7 = (f32[16,512]{1,0:T(8,128)S(1)}, f32[16,512]{1,0:T(8,128)S(1)}, u32[]{:S(2)}, u32[]{:S(2)}) collective-permute-start(f32[16,512]{1,0:T(8,128)S(1)} %get-tuple-element.28), channel_id=1, source_target_pairs={{0,128},{8,136},{16,144},{24,152},{32,160},{40,168},{48,176},{56,1... | collective-permute-start | bytes 98312 | tf_op jit(solution)/shard_map/ppermute | solution.py:12
  63.3 1.3 %collective-permute-start.8 = (f32[16,512]{1,0:T(8,128)S(1)}, f32[16,512]{1,0:T(8,128)S(1)}, u32[]{:S(2)}, u32[]{:S(2)}) collective-permute-start(f32[16,512]{1,0:T(8,128)S(1)} %get-tuple-element.28), channel_id=1, source_target_pairs={{0,256},{8,264},{16,272},{24,280},{32,288},{40,296},{48,304},{56,3... | collective-permute-start | bytes 98312 | tf_op jit(solution)/shard_map/ppermute | solution.py:12
  64.6 1.3 %collective-permute-start.9 = (f32[16,512]{1,0:T(8,128)S(1)}, f32[16,512]{1,0:T(8,128)S(1)}, u32[]{:S(2)}, u32[]{:S(2)}) collective-permute-start(f32[16,512]{1,0:T(8,128)S(1)} %get-tuple-element.28), channel_id=1, source_target_pairs={{0,384},{8,392},{16,400},{24,408},{32,416},{40,424},{48,432},{56,4... | collective-permute-start | bytes 98312 | tf_op jit(solution)/shard_map/ppermute | solution.py:12
  65.9 0.9 %multiply_reduce_fusion.2 = f32[128,512]{1,0:T(8,128)S(1)} fusion(f32[128,16,512]{2,0,1:T(8,128)S(1)} %copy-done.1, f32[128]{0:T(128)S(1)} %iota_negate_fusion, f32[16,512]{1,0:T(8,128)S(1)} %get-tuple-element.32, f32[16,512]{1,0:T(8,128)S(1)} %bitcast.63), kind=kLoop, calls=%fused_computation.8 | loop fusion | flops 4128768 | bytes 4522496 | tf_op jit(solution)/shard_map/reduce_sum | solution.py:77
  66.8 1.0 %collective-permute-done.7 = f32[16,512]{1,0:T(8,128)S(1)} collective-permute-done((f32[16,512]{1,0:T(8,128)S(1)}, f32[16,512]{1,0:T(8,128)S(1)}, u32[]{:S(2)}, u32[]{:S(2)}) %collective-permute-start.7) | collective-permute-done | bytes 32800 | tf_op jit(solution)/shard_map/ppermute | solution.py:12
  67.8 2.8 %collective-permute-done.8 = f32[16,512]{1,0:T(8,128)S(1)} collective-permute-done((f32[16,512]{1,0:T(8,128)S(1)}, f32[16,512]{1,0:T(8,128)S(1)}, u32[]{:S(2)}, u32[]{:S(2)}) %collective-permute-start.8) | collective-permute-done | bytes 32800 | tf_op jit(solution)/shard_map/ppermute | solution.py:12
  70.6 3.1 %collective-permute-done.9 = f32[16,512]{1,0:T(8,128)S(1)} collective-permute-done((f32[16,512]{1,0:T(8,128)S(1)}, f32[16,512]{1,0:T(8,128)S(1)}, u32[]{:S(2)}, u32[]{:S(2)}) %collective-permute-start.9) | collective-permute-done | bytes 32800 | tf_op jit(solution)/shard_map/ppermute | solution.py:12
  73.7 1.2 %multiply_reduce_fusion = (f32[128,512]{1,0:T(8,128)S(1)}, f32[128,512]{1,0:T(8,128)S(1)}) fusion(f32[16,512]{1,0:T(8,128)S(1)} %get-tuple-element.31, f32[128]{0:T(128)S(1)} %iota_negate_fusion, f32[16,512]{1,0:T(8,128)S(1)} %get-tuple-element.32, f32[16,512]{1,0:T(8,128)S(1)} %bitcast.64, f32[16,512]{1,0:T(8,128)S(1)} %get-tuple-element.30), kind=kLoop, calls=%fused_computation.6 | loop fusion | flops 6160384 | bytes 655872 | tf_op jit(solution)/shard_map/reduce_sum | solution.py:98
  74.9 0.8 multiply_convert_fusion
  76.8 4.5 %all-to-all-start = ((f32[8,1,128]{2,1,0:T(1,128)}), f32[8,1,128]{2,1,0:T(1,128)S(1)}, u32[]{:S(2)}, u32[]{:S(2)}) async-start(f32[8,1,128]{2,1,0:T(1,128)} %broadcast_in_dim.12), calls=%async_computation | async-start | bytes 8192 | tf_op jit(solution)/shard_map/all_to_all | solution.py:133
  81.4 5.1 %all-to-all-done = f32[8,1,128]{2,1,0:T(1,128)S(1)} async-done(((f32[8,1,128]{2,1,0:T(1,128)}), f32[8,1,128]{2,1,0:T(1,128)S(1)}, u32[]{:S(2)}, u32[]{:S(2)}) %all-to-all-start) | async-done | bytes 4128 | tf_op jit(solution)/shard_map/all_to_all | solution.py:133
  86.5 0.8 divide_convert_fusion
  (47 shorter events, 2.9 us)
Async XLA Ops:
  0.6 55.8 %copy-start = (bf16[128,512]{1,0:T(8,128)(2,1)S(1)}, bf16[128,512]{1,0:T(8,128)(2,1)}, u32[]{:S(2)}) copy-start(bf16[128,512]{1,0:T(8,128)(2,1)} %param.12) | copy-start | bytes 393220
  0.6 7.4 %copy-start.2 = (f32[512,16]{0,1:T(8,128)S(1)}, f32[512,16]{0,1:T(8,128)}, u32[]{:S(2)}) copy-start(f32[512,16]{0,1:T(8,128)} %param.10) | copy-start | bytes 98308
  0.7 15.5 %collective-permute-start = (bf16[128,512]{1,0:T(8,128)(2,1)}, bf16[128,512]{1,0:T(8,128)(2,1)S(1)}, u32[]{:S(2)}, u32[]{:S(2)}) collective-permute-start(bf16[128,512]{1,0:T(8,128)(2,1)} %param.8), channel_id=1, source_target_pairs={{0,8},{8,16},{16,24},{24,32},{32,40},{40,48},{48,56},{56,64},{64,7... | collective-permute-start | bytes 393224 | tf_op jit(solution)/shard_map/ppermute | solution.py:12
  8.1 3.7 %copy-start.5 = (bf16[128,512]{1,0:T(8,128)(2,1)S(1)}, bf16[128,512]{1,0:T(8,128)(2,1)}, u32[]{:S(2)}) copy-start(bf16[128,512]{1,0:T(8,128)(2,1)} %param.13) | copy-start | bytes 393220
  8.1 3.9 %copy-start.4 = (bf16[128,512]{1,0:T(8,128)(2,1)S(1)}, bf16[128,512]{1,0:T(8,128)(2,1)}, u32[]{:S(2)}) copy-start(bf16[128,512]{1,0:T(8,128)(2,1)} %param.14) | copy-start | bytes 393220
  8.1 8.5 %copy-start.6 = (f32[512,16]{0,1:T(8,128)S(1)}, f32[512,16]{0,1:T(8,128)}, u32[]{:S(2)}) copy-start(f32[512,16]{0,1:T(8,128)} %param.9) | copy-start | bytes 98308
  16.7 7.9 %collective-permute-start.1 = (f32[16,512]{1,0:T(8,128)S(1)}, f32[16,512]{1,0:T(8,128)S(1)}, u32[]{:S(2)}, u32[]{:S(2)}) collective-permute-start(f32[16,512]{1,0:T(8,128)S(1)} %get-tuple-element.33), channel_id=1, source_target_pairs={{0,8},{8,16},{16,24},{24,32},{32,40},{40,48},{48,56},{56,64},{64,7... | collective-permute-start | bytes 98312 | tf_op jit(solution)/shard_map/ppermute | solution.py:12
  24.6 9.2 %collective-permute-start.2 = (f32[16,512]{1,0:T(8,128)S(1)}, f32[16,512]{1,0:T(8,128)S(1)}, u32[]{:S(2)}, u32[]{:S(2)}) collective-permute-start(f32[16,512]{1,0:T(8,128)S(1)} %fusion.39), channel_id=1, source_target_pairs={{0,16},{8,24},{16,32},{24,40},{32,48},{40,56},{48,64},{56,72},{64,... | collective-permute-start | bytes 98312 | tf_op jit(solution)/shard_map/ppermute | solution.py:12
  26.5 11.2 %collective-permute-start.3 = (bf16[2,128,512]{2,1,0:T(8,128)(2,1)S(1)}, bf16[2,128,512]{2,1,0:T(8,128)(2,1)S(1)}, u32[]{:S(2)}, u32[]{:S(2)}) collective-permute-start(bf16[2,128,512]{2,1,0:T(8,128)(2,1)S(1)} %pad_maximum_fusion), channel_id=1, source_target_pairs={{0,8},{8,16},{16,24},{24,32},{32,40},{40,48},{48,56},{56,64},{64,7... | collective-permute-start | bytes 786440 | tf_op jit(solution)/shard_map/ppermute | solution.py:12
  37.7 19.1 %collective-permute-start.4 = (f32[16,512]{1,0:T(8,128)S(1)}, f32[16,512]{1,0:T(8,128)S(1)}, u32[]{:S(2)}, u32[]{:S(2)}) collective-permute-start(f32[16,512]{1,0:T(8,128)S(1)} %fusion.40), channel_id=1, source_target_pairs={{0,32},{8,40},{16,48},{24,56},{32,64},{40,72},{48,80},{56,88},{64,... | collective-permute-start | bytes 98312 | tf_op jit(solution)/shard_map/ppermute | solution.py:12
  43.6 15.5 %collective-permute-start.5 = (f32[16,512]{1,0:T(8,128)S(1)}, f32[16,512]{1,0:T(8,128)S(1)}, u32[]{:S(2)}, u32[]{:S(2)}) collective-permute-start(f32[16,512]{1,0:T(8,128)S(1)} %fusion.40), channel_id=1, source_target_pairs={{0,64},{8,72},{16,80},{24,88},{32,96},{40,104},{48,112},{56,120},{... | collective-permute-start | bytes 98312 | tf_op jit(solution)/shard_map/ppermute | solution.py:12
  51.0 10.9 %collective-permute-start.6 = (f32[16,512]{1,0:T(8,128)S(1)}, f32[16,512]{1,0:T(8,128)S(1)}, u32[]{:S(2)}, u32[]{:S(2)}) collective-permute-start(f32[16,512]{1,0:T(8,128)S(1)} %fusion.40), channel_id=1, source_target_pairs={{0,96},{8,104},{16,112},{24,120},{32,128},{40,136},{48,144},{56,15... | collective-permute-start | bytes 98312 | tf_op jit(solution)/shard_map/ppermute | solution.py:12
  53.2 12.7 %copy-start.1 = (f32[128,16,512]{2,0,1:T(8,128)S(1)}, f32[128,16,512]{2,0,1:T(8,128)}, u32[]{:S(2)}) copy-start(f32[128,16,512]{2,0,1:T(8,128)} %convolution_add_fusion) | copy-start | bytes 12582916
  56.5 18.4 %copy-start.3 = (bf16[128,512]{1,0:T(8,128)(2,1)S(1)}, bf16[128,512]{1,0:T(8,128)(2,1)}, u32[]{:S(2)}) copy-start(bf16[128,512]{1,0:T(8,128)(2,1)} %param.8) | copy-start | bytes 393220
  56.5 18.4 %copy-start.7 = (f32[512]{0:T(512)S(1)}, f32[512]{0:T(512)}, u32[]{:S(2)}) copy-start(f32[512]{0:T(512)} %param.11) | copy-start | bytes 6148
  62.0 5.8 %collective-permute-start.7 = (f32[16,512]{1,0:T(8,128)S(1)}, f32[16,512]{1,0:T(8,128)S(1)}, u32[]{:S(2)}, u32[]{:S(2)}) collective-permute-start(f32[16,512]{1,0:T(8,128)S(1)} %get-tuple-element.28), channel_id=1, source_target_pairs={{0,128},{8,136},{16,144},{24,152},{32,160},{40,168},{48,176},{56,1... | collective-permute-start | bytes 98312 | tf_op jit(solution)/shard_map/ppermute | solution.py:12
  63.3 7.3 %collective-permute-start.8 = (f32[16,512]{1,0:T(8,128)S(1)}, f32[16,512]{1,0:T(8,128)S(1)}, u32[]{:S(2)}, u32[]{:S(2)}) collective-permute-start(f32[16,512]{1,0:T(8,128)S(1)} %get-tuple-element.28), channel_id=1, source_target_pairs={{0,256},{8,264},{16,272},{24,280},{32,288},{40,296},{48,304},{56,3... | collective-permute-start | bytes 98312 | tf_op jit(solution)/shard_map/ppermute | solution.py:12
  64.6 9.1 %collective-permute-start.9 = (f32[16,512]{1,0:T(8,128)S(1)}, f32[16,512]{1,0:T(8,128)S(1)}, u32[]{:S(2)}, u32[]{:S(2)}) collective-permute-start(f32[16,512]{1,0:T(8,128)S(1)} %get-tuple-element.28), channel_id=1, source_target_pairs={{0,384},{8,392},{16,400},{24,408},{32,416},{40,424},{48,432},{56,4... | collective-permute-start | bytes 98312 | tf_op jit(solution)/shard_map/ppermute | solution.py:12
  66.8 19.7 %copy-start.8 = (f32[512]{0:T(512)S(1)}, f32[512]{0:T(512)}, u32[]{:S(2)}) copy-start(f32[512]{0:T(512)} %param.15) | copy-start | bytes 6148
  76.8 9.7 %all-to-all-start = ((f32[8,1,128]{2,1,0:T(1,128)}), f32[8,1,128]{2,1,0:T(1,128)S(1)}, u32[]{:S(2)}, u32[]{:S(2)}) async-start(f32[8,1,128]{2,1,0:T(1,128)} %broadcast_in_dim.12), calls=%async_computation | async-start | bytes 8192 | tf_op jit(solution)/shard_map/all_to_all | solution.py:133

commit v10 on v8

--- a/solution.py
+++ b/solution.py
@@ -61,7 +61,7 @@
         sent = previous_state + before_previous
         reach = 4 if span * 4 == ctx_count else 2
         got = jnp.zeros_like(sent)
-        for step in range(1, reach):
+        for step in sorted(range(1, reach), key=lambda k: -min(k, reach - k)):
             decay = jnp.exp(-rates * float(row_count * span * step))
             got = got + decay * shifted(sent, "ctx", step * span)
         if span == 1:

time: 86.2 us -> 85.5 us (level)
  transfers between devices with their start and end apart: 10 -> 10, of which waited for: 9 -> 8; matrix products, arithmetic and copies ran while one was open for 19% -> 20% of each run, Pallas kernels for 0% -> 0%
where the time goes in v10:
time: 85.5 us; the launch traced here: 84.9 us
  waiting for transfers between devices  32 us (37%)
  starting transfers between devices  30.8 us (36%)
  matrix products  10 us (12%)
  other arithmetic  9.66 us (11%)
  local copies, waits for them, and re-layouts  1.44 us (2%)
  between operations  1.06 us (1%)
    ppermute x9, waiting for transfers between devices, shifted(): return lax.ppermute(block, axis, route)  26.9 us
    ppermute x9, starting transfers between devices, shifted(): return lax.ppermute(block, axis, route)  26.3 us
    all_to_all x1, waiting for transfers between devices, per_device(): energy = jnp.sum(lax.all_to_all(spread, 'ch', 0, 0, tiled=True), axis=0)  5.08 us
    dot_general x2, matrix products, block_terms(): jnp.einsum('ts,src->trc', lower, lifted_lo, preferred_element_type=jnp.fl...  4.8 us
    dot_general x2, matrix products, block_terms(): jnp.einsum('ts,src->trc', lower, lifted_hi, preferred_element_type=jnp.fl...  4.73 us
    all_to_all x1, starting transfers between devices, per_device(): energy = jnp.sum(lax.all_to_all(spread, 'ch', 0, 0, tiled=True), axis=0)  4.46 us
    reduce_sum x1, other arithmetic, per_device(): previous_local = jnp.sum(fall * previous_prefix, axis=1)  3.25 us
  transfers between devices with their start and end apart: 10, of which 8 were waited for; matrix products, arithmetic and copies ran while one was open for 20% of the time, Pallas kernels for 0%

profile of v10, /device:TPU:6, one launch (start us, length us, event | category | flops | bytes accessed | tf_op | source)
XLA Modules:
  0.0 84.9 jit_solution(7589411560665318414)
XLA Ops:
  0.7 4.0 %collective-permute-start = (bf16[128,512]{1,0:T(8,128)(2,1)}, bf16[128,512]{1,0:T(8,128)(2,1)S(1)}, u32[]{:S(2)}, u32[]{:S(2)}) collective-permute-start(bf16[128,512]{1,0:T(8,128)(2,1)} %param.8), channel_id=1, source_target_pairs={{0,8},{8,16},{16,24},{24,32},{32,40},{40,48},{48,56},{56,64},{64,7... | collective-permute-start | bytes 393224 | tf_op jit(solution)/shard_map/ppermute | solution.py:12
  4.6 0.9 %convert_element_type.70 = f32[128,512]{1,0:T(8,128)S(1)} convert(bf16[128,512]{1,0:T(8,128)(2,1)} %param.8) | non-fusion elementwise | flops 65536 | bytes 393216 | tf_op jit(solution)/shard_map/convert_element_type | solution.py:46
  5.6 0.8 multiply_exponential_fusion.1
  6.4 1.6 %fusion.7 = f32[128,16,512]{2,0,1:T(8,128)S(1)} fusion(f32[128,512]{1,0:T(8,128)S(1)} %convert_element_type.70, f32[16,512]{1,0:T(8,128)} %bitcast.58), kind=kOutput, calls=%fused_computation.18 | convolution fusion | flops 272646144 | bytes 4489216 | tf_op jit(solution)/shard_map/ts,src->trc/dot_general | solution.py:32
  8.0 3.5 %convolution_add_fusion = f32[128,16,512]{2,0,1:T(8,128)} fusion(f32[128,16,512]{2,0,1:T(8,128)S(1)} %fusion.7, f32[128,512]{1,0:T(8,128)S(1)} %convert_element_type.70, f32[16,512]{1,0:T(8,128)S(1)} %bitcast.59), kind=kOutput, calls=%fused_computation.15 | convolution fusion | flops 274743296 | bytes 8683520 | tf_op jit(solution)/shard_map/ts,src->trc/dot_general | solution.py:34
  11.7 4.4 %collective-permute-done = bf16[128,512]{1,0:T(8,128)(2,1)S(1)} collective-permute-done((bf16[128,512]{1,0:T(8,128)(2,1)}, bf16[128,512]{1,0:T(8,128)(2,1)S(1)}, u32[]{:S(2)}, u32[]{:S(2)}) %collective-permute-start) | collective-permute-done | bytes 131104 | tf_op jit(solution)/shard_map/ppermute | solution.py:12
  16.2 0.3 multiply_reduce_fusion.4
  16.6 1.9 %collective-permute-start.1 = (f32[16,512]{1,0:T(8,128)S(1)}, f32[16,512]{1,0:T(8,128)S(1)}, u32[]{:S(2)}, u32[]{:S(2)}) collective-permute-start(f32[16,512]{1,0:T(8,128)S(1)} %exponential_multiply_fusion.3), channel_id=1, source_target_pairs={{0,8},{8,16},{16,24},{24,32},{32,40},{40,48},{48,56},{56,64},{64,7... | collective-permute-start | bytes 98312 | tf_op jit(solution)/shard_map/ppermute | solution.py:12
  18.8 5.7 %collective-permute-done.1 = f32[16,512]{1,0:T(8,128)S(1)} collective-permute-done((f32[16,512]{1,0:T(8,128)S(1)}, f32[16,512]{1,0:T(8,128)S(1)}, u32[]{:S(2)}, u32[]{:S(2)}) %collective-permute-start.1) | collective-permute-done | bytes 32800 | tf_op jit(solution)/shard_map/ppermute | solution.py:12
  24.6 1.9 %collective-permute-start.2 = (f32[16,512]{1,0:T(8,128)S(1)}, f32[16,512]{1,0:T(8,128)S(1)}, u32[]{:S(2)}, u32[]{:S(2)}) collective-permute-start(f32[16,512]{1,0:T(8,128)S(1)} %add.76), channel_id=1, source_target_pairs={{0,16},{8,24},{16,32},{24,40},{32,48},{40,56},{48,64},{56,72},{64,... | collective-permute-start | bytes 98312 | tf_op jit(solution)/shard_map/ppermute | solution.py:12
  26.5 1.3 %fusion.5 = f32[128,16,512]{2,0,1:T(8,128)S(1)} fusion(f32[128,512]{1,0:T(8,128)S(1)} %convert_element_type.67, f32[16,512]{1,0:T(8,128)S(1)} %bitcast.61), kind=kOutput, calls=%fused_computation.17 | convolution fusion | flops 273694720 | bytes 4489216 | tf_op jit(solution)/shard_map/ts,src->trc/dot_general | solution.py:34
  27.9 1.9 %collective-permute-start.4 = (bf16[2,128,512]{2,1,0:T(8,128)(2,1)S(1)}, bf16[2,128,512]{2,1,0:T(8,128)(2,1)S(1)}, u32[]{:S(2)}, u32[]{:S(2)}) collective-permute-start(bf16[2,128,512]{2,1,0:T(8,128)(2,1)S(1)} %pad_maximum_fusion), channel_id=1, source_target_pairs={{0,8},{8,16},{16,24},{24,32},{32,40},{40,48},{48,56},{56,64},{64,7... | collective-permute-start | bytes 786440 | tf_op jit(solution)/shard_map/ppermute | solution.py:12
  29.8 3.7 %collective-permute-done.2 = f32[16,512]{1,0:T(8,128)S(1)} collective-permute-done((f32[16,512]{1,0:T(8,128)S(1)}, f32[16,512]{1,0:T(8,128)S(1)}, u32[]{:S(2)}, u32[]{:S(2)}) %collective-permute-start.2) | collective-permute-done | bytes 32800 | tf_op jit(solution)/shard_map/ppermute | solution.py:12
  33.5 5.2 %collective-permute-start.3 = (f32[16,512]{1,0:T(8,128)S(1)}, f32[16,512]{1,0:T(8,128)S(1)}, u32[]{:S(2)}, u32[]{:S(2)}) collective-permute-start(f32[16,512]{1,0:T(8,128)S(1)} %fusion.41), channel_id=1, source_target_pairs={{0,32},{8,40},{16,48},{24,56},{32,64},{40,72},{48,80},{56,88},{64,... | collective-permute-start | bytes 98312 | tf_op jit(solution)/shard_map/ppermute | solution.py:12
  38.8 3.2 %convolution_add_fusion.1 = f32[128,16,512]{2,0,1:T(8,128)} fusion(f32[128,16,512]{2,0,1:T(8,128)S(1)} %fusion.5, f32[128,512]{1,0:T(8,128)S(1)} %convert_element_type.67, f32[16,512]{1,0:T(8,128)S(1)} %bitcast.62), kind=kOutput, calls=%fused_computation.16 | convolution fusion | flops 273694720 | bytes 8683520 | tf_op jit(solution)/shard_map/ts,src->trc/dot_general | solution.py:32
  41.9 2.8 %collective-permute-done.3 = f32[16,512]{1,0:T(8,128)S(1)} collective-permute-done((f32[16,512]{1,0:T(8,128)S(1)}, f32[16,512]{1,0:T(8,128)S(1)}, u32[]{:S(2)}, u32[]{:S(2)}) %collective-permute-start.3) | collective-permute-done | bytes 32800 | tf_op jit(solution)/shard_map/ppermute | solution.py:12
  44.8 7.5 %collective-permute-start.5 = (f32[16,512]{1,0:T(8,128)S(1)}, f32[16,512]{1,0:T(8,128)S(1)}, u32[]{:S(2)}, u32[]{:S(2)}) collective-permute-start(f32[16,512]{1,0:T(8,128)S(1)} %get-tuple-element.30), channel_id=1, source_target_pairs={{0,64},{8,72},{16,80},{24,88},{32,96},{40,104},{48,112},{56,120},{... | collective-permute-start | bytes 98312 | tf_op jit(solution)/shard_map/ppermute | solution.py:12
  52.6 3.3 %multiply_reduce_fusion.3 = f32[128,512]{1,0:T(8,128)S(1)} fusion(f32[128,16,512]{2,0,1:T(8,128)} %convolution_add_fusion.1, f32[128]{0:T(128)S(1)} %iota_negate_fusion, f32[16,512]{1,0:T(8,128)S(1)} %get-tuple-element.34, f32[16,512]{1,0:T(8,128)S(1)} %bitcast.63), kind=kLoop, calls=%fused_computation.9 | loop fusion | flops 4128768 | bytes 4522496 | tf_op jit(solution)/shard_map/reduce_sum | solution.py:74
  56.2 4.0 %collective-permute-done.5 = f32[16,512]{1,0:T(8,128)S(1)} collective-permute-done((f32[16,512]{1,0:T(8,128)S(1)}, f32[16,512]{1,0:T(8,128)S(1)}, u32[]{:S(2)}, u32[]{:S(2)}) %collective-permute-start.5) | collective-permute-done | bytes 32800 | tf_op jit(solution)/shard_map/ppermute | solution.py:12
  60.2 1.3 %collective-permute-start.6 = (f32[16,512]{1,0:T(8,128)S(1)}, f32[16,512]{1,0:T(8,128)S(1)}, u32[]{:S(2)}, u32[]{:S(2)}) collective-permute-start(f32[16,512]{1,0:T(8,128)S(1)} %get-tuple-element.28), channel_id=1, source_target_pairs={{0,256},{8,264},{16,272},{24,280},{32,288},{40,296},{48,304},{56,3... | collective-permute-start | bytes 98312 | tf_op jit(solution)/shard_map/ppermute | solution.py:12
  61.5 1.3 %collective-permute-start.7 = (f32[16,512]{1,0:T(8,128)S(1)}, f32[16,512]{1,0:T(8,128)S(1)}, u32[]{:S(2)}, u32[]{:S(2)}) collective-permute-start(f32[16,512]{1,0:T(8,128)S(1)} %get-tuple-element.28), channel_id=1, source_target_pairs={{0,128},{8,136},{16,144},{24,152},{32,160},{40,168},{48,176},{56,1... | collective-permute-start | bytes 98312 | tf_op jit(solution)/shard_map/ppermute | solution.py:12
  62.8 1.3 %collective-permute-start.8 = (f32[16,512]{1,0:T(8,128)S(1)}, f32[16,512]{1,0:T(8,128)S(1)}, u32[]{:S(2)}, u32[]{:S(2)}) collective-permute-start(f32[16,512]{1,0:T(8,128)S(1)} %get-tuple-element.28), channel_id=1, source_target_pairs={{0,384},{8,392},{16,400},{24,408},{32,416},{40,424},{48,432},{56,4... | collective-permute-start | bytes 98312 | tf_op jit(solution)/shard_map/ppermute | solution.py:12
  64.2 0.9 %multiply_reduce_fusion.2 = f32[128,512]{1,0:T(8,128)S(1)} fusion(f32[128,16,512]{2,0,1:T(8,128)S(1)} %copy-done.1, f32[128]{0:T(128)S(1)} %iota_negate_fusion, f32[16,512]{1,0:T(8,128)S(1)} %get-tuple-element.34, f32[16,512]{1,0:T(8,128)S(1)} %bitcast.64), kind=kLoop, calls=%fused_computation.8 | loop fusion | flops 4128768 | bytes 4522496 | tf_op jit(solution)/shard_map/reduce_sum | solution.py:79
  65.1 2.5 %collective-permute-done.6 = f32[16,512]{1,0:T(8,128)S(1)} collective-permute-done((f32[16,512]{1,0:T(8,128)S(1)}, f32[16,512]{1,0:T(8,128)S(1)}, u32[]{:S(2)}, u32[]{:S(2)}) %collective-permute-start.6) | collective-permute-done | bytes 32800 | tf_op jit(solution)/shard_map/ppermute | solution.py:12
  67.6 3.8 %collective-permute-done.8 = f32[16,512]{1,0:T(8,128)S(1)} collective-permute-done((f32[16,512]{1,0:T(8,128)S(1)}, f32[16,512]{1,0:T(8,128)S(1)}, u32[]{:S(2)}, u32[]{:S(2)}) %collective-permute-start.8) | collective-permute-done | bytes 32800 | tf_op jit(solution)/shard_map/ppermute | solution.py:12
  71.4 1.2 %multiply_reduce_fusion = (f32[128,512]{1,0:T(8,128)S(1)}, f32[128,512]{1,0:T(8,128)S(1)}) fusion(f32[16,512]{1,0:T(8,128)S(1)} %get-tuple-element.33, f32[128]{0:T(128)S(1)} %iota_negate_fusion, f32[16,512]{1,0:T(8,128)S(1)} %get-tuple-element.34, f32[16,512]{1,0:T(8,128)S(1)} %bitcast.65, f32[16,512]{1,0:T(8,128)S(1)} %get-tuple-element.32), kind=kLoop, calls=%fused_computation.6 | loop fusion | flops 6160384 | bytes 655872 | tf_op jit(solution)/shard_map/reduce_sum | solution.py:97
  72.6 0.8 multiply_convert_fusion
  73.6 0.3 multiply_reduce_fusion.5
  73.9 0.6 broadcast_in_dim.12
  74.5 4.5 %all-to-all-start = ((f32[8,1,128]{2,1,0:T(1,128)}), f32[8,1,128]{2,1,0:T(1,128)S(1)}, u32[]{:S(2)}, u32[]{:S(2)}) async-start(f32[8,1,128]{2,1,0:T(1,128)} %broadcast_in_dim.12), calls=%async_computation | async-start | bytes 8192 | tf_op jit(solution)/shard_map/all_to_all | solution.py:132
  79.1 5.1 %all-to-all-done = f32[8,1,128]{2,1,0:T(1,128)S(1)} async-done(((f32[8,1,128]{2,1,0:T(1,128)}), f32[8,1,128]{2,1,0:T(1,128)S(1)}, u32[]{:S(2)}, u32[]{:S(2)}) %all-to-all-start) | async-done | bytes 4128 | tf_op jit(solution)/shard_map/all_to_all | solution.py:132
  84.2 0.8 divide_convert_fusion
  (50 shorter events, 1.7 us)
Async XLA Ops:
  0.6 55.2 %copy-start = (bf16[128,512]{1,0:T(8,128)(2,1)S(1)}, bf16[128,512]{1,0:T(8,128)(2,1)}, u32[]{:S(2)}) copy-start(bf16[128,512]{1,0:T(8,128)(2,1)} %param.12) | copy-start | bytes 393220
  0.6 7.4 %copy-start.2 = (f32[512,16]{0,1:T(8,128)S(1)}, f32[512,16]{0,1:T(8,128)}, u32[]{:S(2)}) copy-start(f32[512,16]{0,1:T(8,128)} %param.10) | copy-start | bytes 98308
  0.7 15.5 %collective-permute-start = (bf16[128,512]{1,0:T(8,128)(2,1)}, bf16[128,512]{1,0:T(8,128)(2,1)S(1)}, u32[]{:S(2)}, u32[]{:S(2)}) collective-permute-start(bf16[128,512]{1,0:T(8,128)(2,1)} %param.8), channel_id=1, source_target_pairs={{0,8},{8,16},{16,24},{24,32},{32,40},{40,48},{48,56},{56,64},{64,7... | collective-permute-start | bytes 393224 | tf_op jit(solution)/shard_map/ppermute | solution.py:12
  8.0 3.6 %copy-start.4 = (bf16[128,512]{1,0:T(8,128)(2,1)S(1)}, bf16[128,512]{1,0:T(8,128)(2,1)}, u32[]{:S(2)}) copy-start(bf16[128,512]{1,0:T(8,128)(2,1)} %param.14) | copy-start | bytes 393220
  8.0 3.6 %copy-start.5 = (bf16[128,512]{1,0:T(8,128)(2,1)S(1)}, bf16[128,512]{1,0:T(8,128)(2,1)}, u32[]{:S(2)}) copy-start(bf16[128,512]{1,0:T(8,128)(2,1)} %param.13) | copy-start | bytes 393220
  16.6 7.9 %collective-permute-start.1 = (f32[16,512]{1,0:T(8,128)S(1)}, f32[16,512]{1,0:T(8,128)S(1)}, u32[]{:S(2)}, u32[]{:S(2)}) collective-permute-start(f32[16,512]{1,0:T(8,128)S(1)} %exponential_multiply_fusion.3), channel_id=1, source_target_pairs={{0,8},{8,16},{16,24},{24,32},{32,40},{40,48},{48,56},{56,64},{64,7... | collective-permute-start | bytes 98312 | tf_op jit(solution)/shard_map/ppermute | solution.py:12
  24.6 8.9 %collective-permute-start.2 = (f32[16,512]{1,0:T(8,128)S(1)}, f32[16,512]{1,0:T(8,128)S(1)}, u32[]{:S(2)}, u32[]{:S(2)}) collective-permute-start(f32[16,512]{1,0:T(8,128)S(1)} %add.76), channel_id=1, source_target_pairs={{0,16},{8,24},{16,32},{24,40},{32,48},{40,56},{48,64},{56,72},{64,... | collective-permute-start | bytes 98312 | tf_op jit(solution)/shard_map/ppermute | solution.py:12
  27.9 16.9 %collective-permute-start.4 = (bf16[2,128,512]{2,1,0:T(8,128)(2,1)S(1)}, bf16[2,128,512]{2,1,0:T(8,128)(2,1)S(1)}, u32[]{:S(2)}, u32[]{:S(2)}) collective-permute-start(bf16[2,128,512]{2,1,0:T(8,128)(2,1)S(1)} %pad_maximum_fusion), channel_id=1, source_target_pairs={{0,8},{8,16},{16,24},{24,32},{32,40},{40,48},{48,56},{56,64},{64,7... | collective-permute-start | bytes 786440 | tf_op jit(solution)/shard_map/ppermute | solution.py:12
  33.5 11.2 %copy-start.6 = (f32[512,16]{0,1:T(8,128)S(1)}, f32[512,16]{0,1:T(8,128)}, u32[]{:S(2)}) copy-start(f32[512,16]{0,1:T(8,128)} %param.9) | copy-start | bytes 98308
  33.5 11.2 %collective-permute-start.3 = (f32[16,512]{1,0:T(8,128)S(1)}, f32[16,512]{1,0:T(8,128)S(1)}, u32[]{:S(2)}, u32[]{:S(2)}) collective-permute-start(f32[16,512]{1,0:T(8,128)S(1)} %fusion.41), channel_id=1, source_target_pairs={{0,32},{8,40},{16,48},{24,56},{32,64},{40,72},{48,80},{56,88},{64,... | collective-permute-start | bytes 98312 | tf_op jit(solution)/shard_map/ppermute | solution.py:12
  44.8 15.4 %collective-permute-start.5 = (f32[16,512]{1,0:T(8,128)S(1)}, f32[16,512]{1,0:T(8,128)S(1)}, u32[]{:S(2)}, u32[]{:S(2)}) collective-permute-start(f32[16,512]{1,0:T(8,128)S(1)} %get-tuple-element.30), channel_id=1, source_target_pairs={{0,64},{8,72},{16,80},{24,88},{32,96},{40,104},{48,112},{56,120},{... | collective-permute-start | bytes 98312 | tf_op jit(solution)/shard_map/ppermute | solution.py:12
  52.6 11.6 %copy-start.1 = (f32[128,16,512]{2,0,1:T(8,128)S(1)}, f32[128,16,512]{2,0,1:T(8,128)}, u32[]{:S(2)}) copy-start(f32[128,16,512]{2,0,1:T(8,128)} %convolution_add_fusion) | copy-start | bytes 12582916
  55.9 16.7 %copy-start.3 = (bf16[128,512]{1,0:T(8,128)(2,1)S(1)}, bf16[128,512]{1,0:T(8,128)(2,1)}, u32[]{:S(2)}) copy-start(bf16[128,512]{1,0:T(8,128)(2,1)} %param.8) | copy-start | bytes 393220
  55.9 16.7 %copy-start.7 = (f32[512]{0:T(512)S(1)}, f32[512]{0:T(512)}, u32[]{:S(2)}) copy-start(f32[512]{0:T(512)} %param.11) | copy-start | bytes 6148
  60.2 7.3 %collective-permute-start.6 = (f32[16,512]{1,0:T(8,128)S(1)}, f32[16,512]{1,0:T(8,128)S(1)}, u32[]{:S(2)}, u32[]{:S(2)}) collective-permute-start(f32[16,512]{1,0:T(8,128)S(1)} %get-tuple-element.28), channel_id=1, source_target_pairs={{0,256},{8,264},{16,272},{24,280},{32,288},{40,296},{48,304},{56,3... | collective-permute-start | bytes 98312 | tf_op jit(solution)/shard_map/ppermute | solution.py:12
  61.5 6.0 %collective-permute-start.7 = (f32[16,512]{1,0:T(8,128)S(1)}, f32[16,512]{1,0:T(8,128)S(1)}, u32[]{:S(2)}, u32[]{:S(2)}) collective-permute-start(f32[16,512]{1,0:T(8,128)S(1)} %get-tuple-element.28), channel_id=1, source_target_pairs={{0,128},{8,136},{16,144},{24,152},{32,160},{40,168},{48,176},{56,1... | collective-permute-start | bytes 98312 | tf_op jit(solution)/shard_map/ppermute | solution.py:12
  62.8 8.5 %collective-permute-start.8 = (f32[16,512]{1,0:T(8,128)S(1)}, f32[16,512]{1,0:T(8,128)S(1)}, u32[]{:S(2)}, u32[]{:S(2)}) collective-permute-start(f32[16,512]{1,0:T(8,128)S(1)} %get-tuple-element.28), channel_id=1, source_target_pairs={{0,384},{8,392},{16,400},{24,408},{32,416},{40,424},{48,432},{56,4... | collective-permute-start | bytes 98312 | tf_op jit(solution)/shard_map/ppermute | solution.py:12
  65.1 19.1 %copy-start.8 = (f32[512]{0:T(512)S(1)}, f32[512]{0:T(512)}, u32[]{:S(2)}) copy-start(f32[512]{0:T(512)} %param.15) | copy-start | bytes 6148
  74.5 9.7 %all-to-all-start = ((f32[8,1,128]{2,1,0:T(1,128)}), f32[8,1,128]{2,1,0:T(1,128)S(1)}, u32[]{:S(2)}, u32[]{:S(2)}) async-start(f32[8,1,128]{2,1,0:T(1,128)} %broadcast_in_dim.12), calls=%async_computation | async-start | bytes 8192 | tf_op jit(solution)/shard_map/all_to_all | solution.py:132

commit v11 on v10

--- a/solution.py
+++ b/solution.py
@@ -64,7 +64,7 @@
         for step in sorted(range(1, reach), key=lambda k: -min(k, reach - k)):
             decay = jnp.exp(-rates * float(row_count * span * step))
             got = got + decay * shifted(sent, "ctx", step * span)
-        if span == 1:
+        if span == 2:
             got, keys_values = lax.optimization_barrier((got, keys_values))
             lookback = shifted(keys_values, "ctx", 1)
         if span == ctx_count // 16:

time: 85.5 us -> 87.9 us (1.028)
  waiting for transfers between devices: 32 us -> 34.6 us
    ppermute x9, waiting for transfers between devices: 26.9 us -> 29.6 us  [shifted(): return lax.ppermute(block, axis, route)]
  transfers between devices with their start and end apart: 10 -> 10, of which waited for: 8 -> 9; matrix products, arithmetic and copies ran while one was open for 20% -> 19% of each run, Pallas kernels for 0% -> 0%
where the time goes in v11:
time: 87.9 us; the launch traced here: 87.3 us
  waiting for transfers between devices  34.6 us (39%)
  starting transfers between devices  30.5 us (35%)
  matrix products  10 us (11%)
  other arithmetic  9.66 us (11%)
  local copies, waits for them, and re-layouts  1.44 us (2%)
  between operations  1.04 us (1%)
    ppermute x9, waiting for transfers between devices, shifted(): return lax.ppermute(block, axis, route)  29.6 us
    ppermute x9, starting transfers between devices, shifted(): return lax.ppermute(block, axis, route)  26 us
    all_to_all x1, waiting for transfers between devices, per_device(): energy = jnp.sum(lax.all_to_all(spread, 'ch', 0, 0, tiled=True), axis=0)  5.08 us
    dot_general x2, matrix products, block_terms(): jnp.einsum('ts,src->trc', lower, lifted_lo, preferred_element_type=jnp.fl...  4.8 us
    dot_general x2, matrix products, block_terms(): jnp.einsum('ts,src->trc', lower, lifted_hi, preferred_element_type=jnp.fl...  4.73 us
    all_to_all x1, starting transfers between devices, per_device(): energy = jnp.sum(lax.all_to_all(spread, 'ch', 0, 0, tiled=True), axis=0)  4.47 us
    reduce_sum x1, other arithmetic, per_device(): previous_local = jnp.sum(fall * previous_prefix, axis=1)  3.25 us
  transfers between devices with their start and end apart: 10, of which 9 were waited for; matrix products, arithmetic and copies ran while one was open for 19% of the time, Pallas kernels for 0%

profile of v11, /device:TPU:6, one launch (start us, length us, event | category | flops | bytes accessed | tf_op | source)
XLA Modules:
  0.0 87.3 jit_solution(9111059089833347395)
XLA Ops:
  0.7 4.0 %collective-permute-start = (bf16[128,512]{1,0:T(8,128)(2,1)}, bf16[128,512]{1,0:T(8,128)(2,1)S(1)}, u32[]{:S(2)}, u32[]{:S(2)}) collective-permute-start(bf16[128,512]{1,0:T(8,128)(2,1)} %param.8), channel_id=1, source_target_pairs={{0,8},{8,16},{16,24},{24,32},{32,40},{40,48},{48,56},{56,64},{64,7... | collective-permute-start | bytes 393224 | tf_op jit(solution)/shard_map/ppermute | solution.py:12
  4.6 0.9 %convert_element_type.70 = f32[128,512]{1,0:T(8,128)S(1)} convert(bf16[128,512]{1,0:T(8,128)(2,1)} %param.8) | non-fusion elementwise | flops 65536 | bytes 393216 | tf_op jit(solution)/shard_map/convert_element_type | solution.py:46
  5.6 0.8 multiply_exponential_fusion.1
  6.4 1.6 %fusion.7 = f32[128,16,512]{2,0,1:T(8,128)S(1)} fusion(f32[128,512]{1,0:T(8,128)S(1)} %convert_element_type.70, f32[16,512]{1,0:T(8,128)} %bitcast.59), kind=kOutput, calls=%fused_computation.18 | convolution fusion | flops 272646144 | bytes 4489216 | tf_op jit(solution)/shard_map/ts,src->trc/dot_general | solution.py:32
  8.0 3.5 %convolution_add_fusion = f32[128,16,512]{2,0,1:T(8,128)} fusion(f32[128,16,512]{2,0,1:T(8,128)S(1)} %fusion.7, f32[128,512]{1,0:T(8,128)S(1)} %convert_element_type.70, f32[16,512]{1,0:T(8,128)S(1)} %bitcast.60), kind=kOutput, calls=%fused_computation.15 | convolution fusion | flops 274743296 | bytes 8683520 | tf_op jit(solution)/shard_map/ts,src->trc/dot_general | solution.py:34
  11.7 4.4 %collective-permute-done = bf16[128,512]{1,0:T(8,128)(2,1)S(1)} collective-permute-done((bf16[128,512]{1,0:T(8,128)(2,1)}, bf16[128,512]{1,0:T(8,128)(2,1)S(1)}, u32[]{:S(2)}, u32[]{:S(2)}) %collective-permute-start) | collective-permute-done | bytes 131104 | tf_op jit(solution)/shard_map/ppermute | solution.py:12
  16.2 0.3 multiply_reduce_fusion.4
  16.6 1.9 %collective-permute-start.1 = (f32[16,512]{1,0:T(8,128)S(1)}, f32[16,512]{1,0:T(8,128)S(1)}, u32[]{:S(2)}, u32[]{:S(2)}) collective-permute-start(f32[16,512]{1,0:T(8,128)S(1)} %exponential_multiply_fusion.4), channel_id=1, source_target_pairs={{0,8},{8,16},{16,24},{24,32},{32,40},{40,48},{48,56},{56,64},{64,7... | collective-permute-start | bytes 98312 | tf_op jit(solution)/shard_map/ppermute | solution.py:12
  18.8 5.7 %collective-permute-done.1 = f32[16,512]{1,0:T(8,128)S(1)} collective-permute-done((f32[16,512]{1,0:T(8,128)S(1)}, f32[16,512]{1,0:T(8,128)S(1)}, u32[]{:S(2)}, u32[]{:S(2)}) %collective-permute-start.1) | collective-permute-done | bytes 32800 | tf_op jit(solution)/shard_map/ppermute | solution.py:12
  24.6 1.9 %collective-permute-start.2 = (f32[16,512]{1,0:T(8,128)S(1)}, f32[16,512]{1,0:T(8,128)S(1)}, u32[]{:S(2)}, u32[]{:S(2)}) collective-permute-start(f32[16,512]{1,0:T(8,128)S(1)} %fusion.40), channel_id=1, source_target_pairs={{0,16},{8,24},{16,32},{24,40},{32,48},{40,56},{48,64},{56,72},{64,... | collective-permute-start | bytes 98312 | tf_op jit(solution)/shard_map/ppermute | solution.py:12
  26.5 1.3 %fusion.5 = f32[128,16,512]{2,0,1:T(8,128)S(1)} fusion(f32[128,512]{1,0:T(8,128)S(1)} %convert_element_type.67, f32[16,512]{1,0:T(8,128)S(1)} %bitcast.62), kind=kOutput, calls=%fused_computation.17 | convolution fusion | flops 273694720 | bytes 4489216 | tf_op jit(solution)/shard_map/ts,src->trc/dot_general | solution.py:34
  27.8 5.5 %collective-permute-done.2 = f32[16,512]{1,0:T(8,128)S(1)} collective-permute-done((f32[16,512]{1,0:T(8,128)S(1)}, f32[16,512]{1,0:T(8,128)S(1)}, u32[]{:S(2)}, u32[]{:S(2)}) %collective-permute-start.2) | collective-permute-done | bytes 32800 | tf_op jit(solution)/shard_map/ppermute | solution.py:12
  33.4 2.9 %collective-permute-start.3 = (f32[16,512]{1,0:T(8,128)S(1)}, f32[16,512]{1,0:T(8,128)S(1)}, u32[]{:S(2)}, u32[]{:S(2)}) collective-permute-start(f32[16,512]{1,0:T(8,128)S(1)} %fusion.43), channel_id=1, source_target_pairs={{0,32},{8,40},{16,48},{24,56},{32,64},{40,72},{48,80},{56,88},{64,... | collective-permute-start | bytes 98312 | tf_op jit(solution)/shard_map/ppermute | solution.py:12
  36.3 2.7 %collective-permute-start.4 = (bf16[2,128,512]{2,1,0:T(8,128)(2,1)S(1)}, bf16[2,128,512]{2,1,0:T(8,128)(2,1)S(1)}, u32[]{:S(2)}, u32[]{:S(2)}) collective-permute-start(bf16[2,128,512]{2,1,0:T(8,128)(2,1)S(1)} %pad_maximum_fusion), channel_id=1, source_target_pairs={{0,8},{8,16},{16,24},{24,32},{32,40},{40,48},{48,56},{56,64},{64,7... | collective-permute-start | bytes 786440 | tf_op jit(solution)/shard_map/ppermute | solution.py:12
  39.0 3.2 %convolution_add_fusion.1 = f32[128,16,512]{2,0,1:T(8,128)} fusion(f32[128,16,512]{2,0,1:T(8,128)S(1)} %fusion.5, f32[128,512]{1,0:T(8,128)S(1)} %convert_element_type.67, f32[16,512]{1,0:T(8,128)S(1)} %bitcast.63), kind=kOutput, calls=%fused_computation.16 | convolution fusion | flops 273694720 | bytes 8683520 | tf_op jit(solution)/shard_map/ts,src->trc/dot_general | solution.py:32
  42.2 2.3 %collective-permute-done.3 = f32[16,512]{1,0:T(8,128)S(1)} collective-permute-done((f32[16,512]{1,0:T(8,128)S(1)}, f32[16,512]{1,0:T(8,128)S(1)}, u32[]{:S(2)}, u32[]{:S(2)}) %collective-permute-start.3) | collective-permute-done | bytes 32800 | tf_op jit(solution)/shard_map/ppermute | solution.py:12
  44.4 2.6 %collective-permute-done.4 = bf16[2,128,512]{2,1,0:T(8,128)(2,1)S(1)} collective-permute-done((bf16[2,128,512]{2,1,0:T(8,128)(2,1)S(1)}, bf16[2,128,512]{2,1,0:T(8,128)(2,1)S(1)}, u32[]{:S(2)}, u32[]{:S(2)}) %collective-permute-start.4) | collective-permute-done | bytes 262176 | tf_op jit(solution)/shard_map/ppermute | solution.py:12
  47.1 8.8 %collective-permute-start.5 = (f32[16,512]{1,0:T(8,128)S(1)}, f32[16,512]{1,0:T(8,128)S(1)}, u32[]{:S(2)}, u32[]{:S(2)}) collective-permute-start(f32[16,512]{1,0:T(8,128)S(1)} %get-tuple-element.30), channel_id=1, source_target_pairs={{0,64},{8,72},{16,80},{24,88},{32,96},{40,104},{48,112},{56,120},{... | collective-permute-start | bytes 98312 | tf_op jit(solution)/shard_map/ppermute | solution.py:12
  56.2 3.3 %multiply_reduce_fusion.3 = f32[128,512]{1,0:T(8,128)S(1)} fusion(f32[128,16,512]{2,0,1:T(8,128)} %convolution_add_fusion.1, f32[128]{0:T(128)S(1)} %iota_negate_fusion, f32[16,512]{1,0:T(8,128)S(1)} %get-tuple-element.34, f32[16,512]{1,0:T(8,128)S(1)} %bitcast.64), kind=kLoop, calls=%fused_computation.9 | loop fusion | flops 4128768 | bytes 4522496 | tf_op jit(solution)/shard_map/reduce_sum | solution.py:74
  59.8 2.7 %collective-permute-done.5 = f32[16,512]{1,0:T(8,128)S(1)} collective-permute-done((f32[16,512]{1,0:T(8,128)S(1)}, f32[16,512]{1,0:T(8,128)S(1)}, u32[]{:S(2)}, u32[]{:S(2)}) %collective-permute-start.5) | collective-permute-done | bytes 32800 | tf_op jit(solution)/shard_map/ppermute | solution.py:12
  62.6 1.3 %collective-permute-start.6 = (f32[16,512]{1,0:T(8,128)S(1)}, f32[16,512]{1,0:T(8,128)S(1)}, u32[]{:S(2)}, u32[]{:S(2)}) collective-permute-start(f32[16,512]{1,0:T(8,128)S(1)} %get-tuple-element.28), channel_id=1, source_target_pairs={{0,256},{8,264},{16,272},{24,280},{32,288},{40,296},{48,304},{56,3... | collective-permute-start | bytes 98312 | tf_op jit(solution)/shard_map/ppermute | solution.py:12
  63.9 1.3 %collective-permute-start.7 = (f32[16,512]{1,0:T(8,128)S(1)}, f32[16,512]{1,0:T(8,128)S(1)}, u32[]{:S(2)}, u32[]{:S(2)}) collective-permute-start(f32[16,512]{1,0:T(8,128)S(1)} %get-tuple-element.28), channel_id=1, source_target_pairs={{0,128},{8,136},{16,144},{24,152},{32,160},{40,168},{48,176},{56,1... | collective-permute-start | bytes 98312 | tf_op jit(solution)/shard_map/ppermute | solution.py:12
  65.2 1.3 %collective-permute-start.8 = (f32[16,512]{1,0:T(8,128)S(1)}, f32[16,512]{1,0:T(8,128)S(1)}, u32[]{:S(2)}, u32[]{:S(2)}) collective-permute-start(f32[16,512]{1,0:T(8,128)S(1)} %get-tuple-element.28), channel_id=1, source_target_pairs={{0,384},{8,392},{16,400},{24,408},{32,416},{40,424},{48,432},{56,4... | collective-permute-start | bytes 98312 | tf_op jit(solution)/shard_map/ppermute | solution.py:12
  66.5 0.9 %multiply_reduce_fusion.2 = f32[128,512]{1,0:T(8,128)S(1)} fusion(f32[128,16,512]{2,0,1:T(8,128)S(1)} %copy-done.1, f32[128]{0:T(128)S(1)} %iota_negate_fusion, f32[16,512]{1,0:T(8,128)S(1)} %get-tuple-element.34, f32[16,512]{1,0:T(8,128)S(1)} %bitcast.65), kind=kLoop, calls=%fused_computation.8 | loop fusion | flops 4128768 | bytes 4522496 | tf_op jit(solution)/shard_map/reduce_sum | solution.py:79
  67.4 2.5 %collective-permute-done.6 = f32[16,512]{1,0:T(8,128)S(1)} collective-permute-done((f32[16,512]{1,0:T(8,128)S(1)}, f32[16,512]{1,0:T(8,128)S(1)}, u32[]{:S(2)}, u32[]{:S(2)}) %collective-permute-start.6) | collective-permute-done | bytes 32800 | tf_op jit(solution)/shard_map/ppermute | solution.py:12
  69.9 3.8 %collective-permute-done.8 = f32[16,512]{1,0:T(8,128)S(1)} collective-permute-done((f32[16,512]{1,0:T(8,128)S(1)}, f32[16,512]{1,0:T(8,128)S(1)}, u32[]{:S(2)}, u32[]{:S(2)}) %collective-permute-start.8) | collective-permute-done | bytes 32800 | tf_op jit(solution)/shard_map/ppermute | solution.py:12
  73.7 1.2 %multiply_reduce_fusion = (f32[128,512]{1,0:T(8,128)S(1)}, f32[128,512]{1,0:T(8,128)S(1)}) fusion(f32[16,512]{1,0:T(8,128)S(1)} %get-tuple-element.33, f32[128]{0:T(128)S(1)} %iota_negate_fusion, f32[16,512]{1,0:T(8,128)S(1)} %get-tuple-element.34, f32[16,512]{1,0:T(8,128)S(1)} %bitcast.66, f32[16,512]{1,0:T(8,128)S(1)} %get-tuple-element.32), kind=kLoop, calls=%fused_computation.6 | loop fusion | flops 6160384 | bytes 655872 | tf_op jit(solution)/shard_map/reduce_sum | solution.py:97
  74.9 0.8 multiply_convert_fusion
  76.2 0.6 broadcast_in_dim.12
  76.8 4.5 %all-to-all-start = ((f32[8,1,128]{2,1,0:T(1,128)}), f32[8,1,128]{2,1,0:T(1,128)S(1)}, u32[]{:S(2)}, u32[]{:S(2)}) async-start(f32[8,1,128]{2,1,0:T(1,128)} %broadcast_in_dim.12), calls=%async_computation | async-start | bytes 8192 | tf_op jit(solution)/shard_map/all_to_all | solution.py:132
  81.4 5.1 %all-to-all-done = f32[8,1,128]{2,1,0:T(1,128)S(1)} async-done(((f32[8,1,128]{2,1,0:T(1,128)}), f32[8,1,128]{2,1,0:T(1,128)S(1)}, u32[]{:S(2)}, u32[]{:S(2)}) %all-to-all-start) | async-done | bytes 4128 | tf_op jit(solution)/shard_map/all_to_all | solution.py:132
  86.5 0.8 divide_convert_fusion
  (50 shorter events, 2.0 us)
Async XLA Ops:
  0.6 58.8 %copy-start = (bf16[128,512]{1,0:T(8,128)(2,1)S(1)}, bf16[128,512]{1,0:T(8,128)(2,1)}, u32[]{:S(2)}) copy-start(bf16[128,512]{1,0:T(8,128)(2,1)} %param.12) | copy-start | bytes 393220
  0.6 7.4 %copy-start.2 = (f32[512,16]{0,1:T(8,128)S(1)}, f32[512,16]{0,1:T(8,128)}, u32[]{:S(2)}) copy-start(f32[512,16]{0,1:T(8,128)} %param.10) | copy-start | bytes 98308
  0.7 15.5 %collective-permute-start = (bf16[128,512]{1,0:T(8,128)(2,1)}, bf16[128,512]{1,0:T(8,128)(2,1)S(1)}, u32[]{:S(2)}, u32[]{:S(2)}) collective-permute-start(bf16[128,512]{1,0:T(8,128)(2,1)} %param.8), channel_id=1, source_target_pairs={{0,8},{8,16},{16,24},{24,32},{32,40},{40,48},{48,56},{56,64},{64,7... | collective-permute-start | bytes 393224 | tf_op jit(solution)/shard_map/ppermute | solution.py:12
  8.0 3.6 %copy-start.4 = (bf16[128,512]{1,0:T(8,128)(2,1)S(1)}, bf16[128,512]{1,0:T(8,128)(2,1)}, u32[]{:S(2)}) copy-start(bf16[128,512]{1,0:T(8,128)(2,1)} %param.14) | copy-start | bytes 393220
  8.0 3.6 %copy-start.5 = (bf16[128,512]{1,0:T(8,128)(2,1)S(1)}, bf16[128,512]{1,0:T(8,128)(2,1)}, u32[]{:S(2)}) copy-start(bf16[128,512]{1,0:T(8,128)(2,1)} %param.13) | copy-start | bytes 393220
  16.6 7.9 %collective-permute-start.1 = (f32[16,512]{1,0:T(8,128)S(1)}, f32[16,512]{1,0:T(8,128)S(1)}, u32[]{:S(2)}, u32[]{:S(2)}) collective-permute-start(f32[16,512]{1,0:T(8,128)S(1)} %exponential_multiply_fusion.4), channel_id=1, source_target_pairs={{0,8},{8,16},{16,24},{24,32},{32,40},{40,48},{48,56},{56,64},{64,7... | collective-permute-start | bytes 98312 | tf_op jit(solution)/shard_map/ppermute | solution.py:12
  24.6 8.8 %collective-permute-start.2 = (f32[16,512]{1,0:T(8,128)S(1)}, f32[16,512]{1,0:T(8,128)S(1)}, u32[]{:S(2)}, u32[]{:S(2)}) collective-permute-start(f32[16,512]{1,0:T(8,128)S(1)} %fusion.40), channel_id=1, source_target_pairs={{0,16},{8,24},{16,32},{24,40},{32,48},{40,56},{48,64},{56,72},{64,... | collective-permute-start | bytes 98312 | tf_op jit(solution)/shard_map/ppermute | solution.py:12
  33.4 13.6 %copy-start.6 = (f32[512,16]{0,1:T(8,128)S(1)}, f32[512,16]{0,1:T(8,128)}, u32[]{:S(2)}) copy-start(f32[512,16]{0,1:T(8,128)} %param.9) | copy-start | bytes 98308
  33.4 11.0 %collective-permute-start.3 = (f32[16,512]{1,0:T(8,128)S(1)}, f32[16,512]{1,0:T(8,128)S(1)}, u32[]{:S(2)}, u32[]{:S(2)}) collective-permute-start(f32[16,512]{1,0:T(8,128)S(1)} %fusion.43), channel_id=1, source_target_pairs={{0,32},{8,40},{16,48},{24,56},{32,64},{40,72},{48,80},{56,88},{64,... | collective-permute-start | bytes 98312 | tf_op jit(solution)/shard_map/ppermute | solution.py:12
  36.3 10.7 %collective-permute-start.4 = (bf16[2,128,512]{2,1,0:T(8,128)(2,1)S(1)}, bf16[2,128,512]{2,1,0:T(8,128)(2,1)S(1)}, u32[]{:S(2)}, u32[]{:S(2)}) collective-permute-start(bf16[2,128,512]{2,1,0:T(8,128)(2,1)S(1)} %pad_maximum_fusion), channel_id=1, source_target_pairs={{0,8},{8,16},{16,24},{24,32},{32,40},{40,48},{48,56},{56,64},{64,7... | collective-permute-start | bytes 786440 | tf_op jit(solution)/shard_map/ppermute | solution.py:12
  47.1 15.5 %collective-permute-start.5 = (f32[16,512]{1,0:T(8,128)S(1)}, f32[16,512]{1,0:T(8,128)S(1)}, u32[]{:S(2)}, u32[]{:S(2)}) collective-permute-start(f32[16,512]{1,0:T(8,128)S(1)} %get-tuple-element.30), channel_id=1, source_target_pairs={{0,64},{8,72},{16,80},{24,88},{32,96},{40,104},{48,112},{56,120},{... | collective-permute-start | bytes 98312 | tf_op jit(solution)/shard_map/ppermute | solution.py:12
  56.2 10.3 %copy-start.1 = (f32[128,16,512]{2,0,1:T(8,128)S(1)}, f32[128,16,512]{2,0,1:T(8,128)}, u32[]{:S(2)}) copy-start(f32[128,16,512]{2,0,1:T(8,128)} %convolution_add_fusion) | copy-start | bytes 12582916
  59.4 15.5 %copy-start.3 = (bf16[128,512]{1,0:T(8,128)(2,1)S(1)}, bf16[128,512]{1,0:T(8,128)(2,1)}, u32[]{:S(2)}) copy-start(bf16[128,512]{1,0:T(8,128)(2,1)} %param.8) | copy-start | bytes 393220
  59.4 15.5 %copy-start.7 = (f32[512]{0:T(512)S(1)}, f32[512]{0:T(512)}, u32[]{:S(2)}) copy-start(f32[512]{0:T(512)} %param.11) | copy-start | bytes 6148
  62.6 7.3 %collective-permute-start.6 = (f32[16,512]{1,0:T(8,128)S(1)}, f32[16,512]{1,0:T(8,128)S(1)}, u32[]{:S(2)}, u32[]{:S(2)}) collective-permute-start(f32[16,512]{1,0:T(8,128)S(1)} %get-tuple-element.28), channel_id=1, source_target_pairs={{0,256},{8,264},{16,272},{24,280},{32,288},{40,296},{48,304},{56,3... | collective-permute-start | bytes 98312 | tf_op jit(solution)/shard_map/ppermute | solution.py:12
  63.9 6.0 %collective-permute-start.7 = (f32[16,512]{1,0:T(8,128)S(1)}, f32[16,512]{1,0:T(8,128)S(1)}, u32[]{:S(2)}, u32[]{:S(2)}) collective-permute-start(f32[16,512]{1,0:T(8,128)S(1)} %get-tuple-element.28), channel_id=1, source_target_pairs={{0,128},{8,136},{16,144},{24,152},{32,160},{40,168},{48,176},{56,1... | collective-permute-start | bytes 98312 | tf_op jit(solution)/shard_map/ppermute | solution.py:12
  65.2 8.5 %collective-permute-start.8 = (f32[16,512]{1,0:T(8,128)S(1)}, f32[16,512]{1,0:T(8,128)S(1)}, u32[]{:S(2)}, u32[]{:S(2)}) collective-permute-start(f32[16,512]{1,0:T(8,128)S(1)} %get-tuple-element.28), channel_id=1, source_target_pairs={{0,384},{8,392},{16,400},{24,408},{32,416},{40,424},{48,432},{56,4... | collective-permute-start | bytes 98312 | tf_op jit(solution)/shard_map/ppermute | solution.py:12
  67.4 19.1 %copy-start.8 = (f32[512]{0:T(512)S(1)}, f32[512]{0:T(512)}, u32[]{:S(2)}) copy-start(f32[512]{0:T(512)} %param.15) | copy-start | bytes 6148
  76.8 9.7 %all-to-all-start = ((f32[8,1,128]{2,1,0:T(1,128)}), f32[8,1,128]{2,1,0:T(1,128)S(1)}, u32[]{:S(2)}, u32[]{:S(2)}) async-start(f32[8,1,128]{2,1,0:T(1,128)} %broadcast_in_dim.12), calls=%async_computation | async-start | bytes 8192 | tf_op jit(solution)/shard_map/all_to_all | solution.py:132
